TPU v7x, 256 devices: a whole 4x4x8 slice. The times are simulated.
256 devices in a mesh: pipe: 4 (over x), expert: 16 (over z, core), dp: 4 (over y).
Axes of the slice: x: 4, y: 4, z: 8, core: 2. Of those that a mesh axis runs over, the one named last changes fastest.
Arguments:
- inputs: bfloat16 [4, 8192, 4096], P('pipe', ('expert', 'dp')), may hold values from -6 to 6
- routes: int32 [4, 8192, 1], P('pipe', ('expert', 'dp')), may hold values from 0 to 15; in each aligned block of 128 rows (0 to 127, 128 to 255, ..., all dimensions but the last counted through in order) at most 10 rows name the same one
- router_scores: float32 [4, 8192, 8], P('pipe', ('expert', 'dp')), may hold values from -2 to 2
- cotangent: bfloat16 [4, 8192, 4096], P('pipe', ('expert', 'dp')), may hold values from -6 to 6
- w_gate: bfloat16 [4, 16, 768, 4096], P('pipe', 'expert', 'dp'), may hold values from -0.09375 to 0.09375
- w_up: bfloat16 [4, 16, 768, 4096], P('pipe', 'expert', 'dp'), may hold values from -0.09375 to 0.09375
- w_down: bfloat16 [4, 16, 768, 4096], P('pipe', 'expert', 'dp'), may hold values from -0.21875 to 0.21875
Outputs:
- score_grad: float32 [4, 8192, 8], P('pipe', ('expert', 'dp'))
- grad_prev: bfloat16 [4, 8192, 4096], P('pipe', ('expert', 'dp'))
- grad_gate: bfloat16 [4, 16, 768, 4096], P('pipe', 'expert', 'dp')
- grad_up: bfloat16 [4, 16, 768, 4096], P('pipe', 'expert', 'dp')
- grad_down: bfloat16 [4, 16, 768, 4096], P('pipe', 'expert', 'dp')
Inputs may be any that keep to these rules, and one draw needn't show every extreme that they name: `routes`: among the 128 tokens of one device in one section (one block) no expert is named more than 10 times, and in every draw some block names some expert exactly 10 times. Every expert is named by some token.
All inputs are finite; a program needn't handle non-finite values.
Results may differ from a plain program's by a relative error of at most 0.02.
Values may be sent and summed in bfloat16 or wider, within the bound.
No kernel may reach another device: no remote copies, remote signals or barrier semaphores. Data moves between devices by JAX's collectives and lax.ppermute only.
A program may use at most 128 MiB of HBM per device.

v0:
```python
import jax
import jax.numpy as jnp
from jax import lax
from jax.sharding import PartitionSpec as P


def from_behind(shard, axis, by):
    length = lax.axis_size(axis)
    pairs = [(i, i + by) for i in range(length) if 0 <= i + by < length]
    return lax.ppermute(shard, axis, pairs)


def route_tables(route_col, score_rows, experts, capacity):
    expert_ids = jnp.arange(experts, dtype=jnp.int32)
    onehot = (route_col[:, None] == expert_ids).astype(jnp.int32)
    earlier = jnp.cumsum(onehot, axis=0) - onehot
    slot = jnp.sum(onehot * earlier, axis=1)
    position = route_col * capacity + slot
    raised = jnp.exp(score_rows)
    weights = raised / jnp.sum(raised, axis=1, keepdims=True)
    gate = lax.optimization_barrier(weights[:, 0].astype(jnp.bfloat16)).astype(jnp.float32)
    table = position[:, None] == jnp.arange(experts * capacity, dtype=jnp.int32)
    return (weights, gate, table)


def per_device(inputs, routes, router_scores, cotangent, w_gate, w_up, w_down):
    tokens_in = inputs[0]
    upstream = cotangent[0]
    route_col = routes[0][:, 0]
    score_rows = router_scores[0]
    gate_mat = w_gate[0, 0]
    up_mat = w_up[0, 0]
    down_mat = w_down[0, 0]
    experts = lax.axis_size("expert")
    groups = lax.axis_size("dp")
    token_count, model_width = tokens_in.shape
    capacity = max(2, token_count * 5 // (4 * experts))
    weights, gate, table = route_tables(route_col, score_rows, experts, capacity)
    table_half = table.astype(jnp.bfloat16)
    token_contract = (((0,), (0,)), ((), ()))
    feature_contract = (((1,), (1,)), ((), ()))
    local_x = lax.dot_general(
        table_half, tokens_in, token_contract, preferred_element_type=jnp.float32
    )
    local_x = local_x.astype(jnp.bfloat16).reshape(experts, capacity, model_width)
    local_upstream = lax.dot_general(
        table_half, upstream, token_contract, preferred_element_type=jnp.float32
    )
    local_upstream = local_upstream.astype(jnp.bfloat16).reshape(experts, capacity, model_width)
    local_gate = jnp.sum(jnp.where(table, gate[:, None], jnp.float32(0.0)), axis=0)
    local_gate = local_gate.astype(jnp.bfloat16).reshape(experts, capacity)
    copies_x = jnp.broadcast_to(local_x[:, None], (experts, groups, capacity, model_width)).reshape(
        experts * groups, capacity, model_width
    )
    copies_upstream = jnp.broadcast_to(
        local_upstream[:, None], (experts, groups, capacity, model_width)
    ).reshape(experts * groups, capacity, model_width)
    copies_gate = jnp.broadcast_to(local_gate[:, None], (experts, groups, capacity)).reshape(
        experts * groups, capacity
    )
    rows_x, rows_upstream, rows_gate = (
        lax.all_to_all(copies_x, ("expert", "dp"), split_axis=0, concat_axis=0, tiled=True),
        lax.all_to_all(copies_upstream, ("expert", "dp"), split_axis=0, concat_axis=0, tiled=True),
        lax.all_to_all(copies_gate, ("expert", "dp"), split_axis=0, concat_axis=0, tiled=True),
    )
    rows_x = rows_x.reshape(-1, model_width)
    grid_upstream = rows_upstream.reshape(experts, groups, capacity, model_width)
    rows_grad = (
        rows_gate.reshape(-1).astype(jnp.float32)[:, None]
        * grid_upstream.reshape(-1, model_width).astype(jnp.float32)
    ).astype(jnp.bfloat16)
    gate_pre = lax.dot_general(
        rows_x, gate_mat, feature_contract, preferred_element_type=jnp.float32
    )
    up_pre = lax.dot_general(rows_x, up_mat, feature_contract, preferred_element_type=jnp.float32)
    gate_sig = jax.nn.sigmoid(gate_pre)
    activated = (gate_pre * gate_sig * up_pre).astype(jnp.bfloat16)
    partial_out = jnp.dot(activated, down_mat, preferred_element_type=jnp.float32)
    summed_out = lax.psum_scatter(
        partial_out.reshape(experts, groups, capacity, model_width).astype(jnp.bfloat16),
        "dp",
        scatter_dimension=1,
        tiled=True,
    )
    flat_out = lax.all_to_all(
        summed_out.reshape(experts, capacity, model_width),
        "expert",
        split_axis=0,
        concat_axis=0,
        tiled=True,
    ).reshape(-1, model_width)
    scores_grad = lax.dot_general(
        upstream, flat_out, feature_contract, preferred_element_type=jnp.float32
    )
    gate_grad = jnp.sum(jnp.where(table, scores_grad, jnp.float32(0.0)), axis=1)
    is_first = (jnp.arange(score_rows.shape[1]) == 0).astype(jnp.float32)
    score_grad = gate_grad[:, None] * weights[:, 0:1] * (is_first - weights)
    hidden_grad = lax.dot_general(
        rows_grad, down_mat, feature_contract, preferred_element_type=jnp.float32
    )
    pre_gate = (hidden_grad * up_pre * gate_sig * (1.0 + gate_pre * (1.0 - gate_sig))).astype(
        jnp.bfloat16
    )
    pre_up = (hidden_grad * gate_pre * gate_sig).astype(jnp.bfloat16)
    grad_down = lax.dot_general(
        activated, rows_grad, token_contract, preferred_element_type=jnp.float32
    ).astype(jnp.bfloat16)
    grad_gate = lax.dot_general(
        pre_gate, rows_x, token_contract, preferred_element_type=jnp.float32
    ).astype(jnp.bfloat16)
    grad_up = lax.dot_general(
        pre_up, rows_x, token_contract, preferred_element_type=jnp.float32
    ).astype(jnp.bfloat16)
    partial_in = jnp.dot(pre_gate, gate_mat, preferred_element_type=jnp.float32)
    partial_in = partial_in + jnp.dot(pre_up, up_mat, preferred_element_type=jnp.float32)
    outgoing = partial_in.astype(jnp.bfloat16).reshape(experts * groups, capacity, model_width)
    arrived = lax.all_to_all(outgoing, ("expert", "dp"), split_axis=0, concat_axis=0, tiled=True)
    flat_in = jnp.sum(
        arrived.reshape(experts, groups, capacity, model_width).astype(jnp.float32), axis=1
    )
    flat_in = flat_in.astype(jnp.bfloat16).reshape(-1, model_width)
    input_grad = jnp.dot(table_half, flat_in, preferred_element_type=jnp.float32).astype(
        jnp.bfloat16
    )
    handed = from_behind(input_grad, "pipe", -1)
    return (
        score_grad[None],
        handed[None],
        grad_gate[None, None],
        grad_up[None, None],
        grad_down[None, None],
    )


def solution(mesh):
    in_specs = (
        P("pipe", ("expert", "dp"), None),
        P("pipe", ("expert", "dp"), None),
        P("pipe", ("expert", "dp"), None),
        P("pipe", ("expert", "dp"), None),
        P("pipe", "expert", "dp", None),
        P("pipe", "expert", "dp", None),
        P("pipe", "expert", "dp", None),
    )
    out_specs = (
        P("pipe", ("expert", "dp"), None),
        P("pipe", ("expert", "dp"), None),
        P("pipe", "expert", "dp", None),
        P("pipe", "expert", "dp", None),
        P("pipe", "expert", "dp", None),
    )
    return jax.shard_map(
        per_device, mesh=mesh, in_specs=in_specs, out_specs=out_specs, check_vma=False
    )
```

profile of v0, /device:TPU:1, one launch (start us, length us, event | category | flops | bytes accessed | tf_op | source)
XLA Modules:
  0.0 732.6 jit_solution(1868994716766504811)
XLA Ops:
  12.0 13.2 %all-to-all-start.2 = ((bf16[64,1,10]{2,1,0:T(2,128)(2,1)}), bf16[64,1,10]{2,1,0:T(2,128)(2,1)S(1)}, u32[]{:S(2)}, u32[]{:S(2)}) async-start(bf16[64,1,10]{2,1,0:T(2,128)(2,1)} %copy.22), calls=%async_computation.3 | async-start | bytes 65536 | tf_op jit(solution)/shard_map/all_to_all | solution.py:64
  28.5 5.8 all-to-all-done.2
  34.3 5.9 broadcast_in_dim.57
  40.1 6.1 all-to-all-start
  49.5 179.7 %all-to-all-done = bf16[64,10,4096]{2,1,0:T(8,128)(2,1)} async-done(((bf16[64,10,4096]{2,1,0:T(8,128)(2,1)}), bf16[64,10,4096]{2,1,0:T(8,128)(2,1)}, u32[]{:S(2)}, u32[]{:S(2)}) %all-to-all-start) | async-done | bytes 5242912 | tf_op jit(solution)/shard_map/all_to_all | solution.py:62
  229.2 6.0 broadcast_in_dim.63
  235.2 9.5 %all-to-all-start.3 = ((bf16[64,10,4096]{2,1,0:T(8,128)(2,1)}), bf16[64,10,4096]{2,1,0:T(8,128)(2,1)}, u32[]{:S(2)}, u32[]{:S(2)}) async-start(bf16[64,10,4096]{2,1,0:T(8,128)(2,1)} %bitcast.73), calls=%async_computation.4 | async-start | bytes 16777216 | tf_op jit(solution)/shard_map/all_to_all | solution.py:63
  245.0 8.8 %reshape.104 = bf16[640,4096]{1,0:T(8,128)(2,1)} reshape(bf16[64,10,4096]{2,1,0:T(8,128)(2,1)} %all-to-all-done) | data formatting | bytes 10485760 | tf_op jit(solution)/shard_map/reshape | solution.py:66
  253.8 5.3 fusion.10
  261.8 165.9 %all-to-all-done.3 = bf16[64,10,4096]{2,1,0:T(8,128)(2,1)} async-done(((bf16[64,10,4096]{2,1,0:T(8,128)(2,1)}), bf16[64,10,4096]{2,1,0:T(8,128)(2,1)}, u32[]{:S(2)}, u32[]{:S(2)}) %all-to-all-start.3) | async-done | bytes 5242912 | tf_op jit(solution)/shard_map/all_to_all | solution.py:63
  427.6 10.0 %multiply_convert_fusion = bf16[64,10,4096]{2,1,0:T(8,128)(2,1)} fusion(f32[64,10]{1,0:T(8,128)S(1)} %bitcast.76, bf16[64,10,4096]{2,1,0:T(8,128)(2,1)} %all-to-all-done.3), kind=kLoop, calls=%fused_computation | loop fusion | flops 7864320 | bytes 10488320 | tf_op jit(solution)/shard_map/convert_element_type | solution.py:71
  437.6 8.7 %convert_element_type.113 = bf16[640,4096]{1,0:T(8,128)(2,1)} reshape(bf16[64,10,4096]{2,1,0:T(8,128)(2,1)} %multiply_convert_fusion) | data formatting | bytes 10485760 | tf_op jit(solution)/shard_map/convert_element_type | solution.py:71
  446.3 4.6 multiply_convert_fusion.7
  462.0 8.4 %reshape.108 = bf16[64,10,4096]{2,1,0:T(8,128)(2,1)} reshape(bf16[640,4096]{1,0:T(8,128)(2,1)} %add_convert_fusion) | data formatting | bytes 10485760 | tf_op jit(solution)/shard_map/reshape | solution.py:116
  470.5 9.5 %all-to-all-start.4 = ((bf16[64,10,4096]{2,1,0:T(8,128)(2,1)}), bf16[64,10,4096]{2,1,0:T(8,128)(2,1)}, u32[]{:S(2)}, u32[]{:S(2)}) async-start(bf16[64,10,4096]{2,1,0:T(8,128)(2,1)} %reshape.108), calls=%async_computation.5 | async-start | bytes 16777216 | tf_op jit(solution)/shard_map/all_to_all | solution.py:117
  480.0 80.6 %reduce-scatter.2.cloned.1.call-done = bf16[16,1,10,4096]{3,0,2,1:T(8,128)(2,1)} async-done(((bf16[16,4,10,4096]{3,0,2,1:T(8,128)(2,1)}), bf16[16,1,10,4096]{3,0,2,1:T(8,128)(2,1)}) %reduce-scatter.2.cloned.1.call-update) | async-done | bytes 1310736 | tf_op jit(solution)/shard_map/reduce_scatter | solution.py:79
  564.0 98.9 %all-to-all-done.4 = bf16[64,10,4096]{2,1,0:T(8,128)(2,1)} async-done(((bf16[64,10,4096]{2,1,0:T(8,128)(2,1)}), bf16[64,10,4096]{2,1,0:T(8,128)(2,1)}, u32[]{:S(2)}, u32[]{:S(2)}) %all-to-all-start.4) | async-done | bytes 5242912 | tf_op jit(solution)/shard_map/all_to_all | solution.py:117
  662.9 7.3 all-to-all-start.1
  670.4 7.0 bitcast_reduce_fusion
  682.2 5.0 fusion.5
  687.3 9.7 %reshape.113 = f32[640,4096]{1,0:T(8,128)} reshape(bf16[64,10,4096]{2,1,0:T(8,128)(2,1)} %all-to-all-done.3) | data formatting | bytes 15728640 | tf_op jit(solution)/shard_map/convert_element_type | solution.py:70
  697.0 5.0 fusion.4
  702.0 6.6 fusion.3
  708.6 10.6 %all-to-all-done.1 = bf16[16,10,4096]{2,1,0:T(8,128)(2,1)} async-done(((bf16[16,10,4096]{2,1,0:T(8,128)(2,1)}), bf16[16,10,4096]{2,1,0:T(8,128)(2,1)}, u32[]{:S(2)}, u32[]{:S(2)}) %all-to-all-start.1) | async-done | bytes 1310752 | tf_op jit(solution)/shard_map/all_to_all | solution.py:85
  (56 shorter events, 40.4 us)
Async XLA Ops:
  7.2 439.1 %copy-start = (bf16[1,1,192,4096]{3,2,1,0:T(8,128)(2,1)S(1)}, bf16[1,1,192,4096]{3,2,1,0:T(8,128)(2,1)}, u32[]{:S(2)}) copy-start(bf16[1,1,192,4096]{3,2,1,0:T(8,128)(2,1)} %param.13) | copy-start | bytes 4718596
  12.0 22.2 %all-to-all-start.2 = ((bf16[64,1,10]{2,1,0:T(2,128)(2,1)}), bf16[64,1,10]{2,1,0:T(2,128)(2,1)S(1)}, u32[]{:S(2)}, u32[]{:S(2)}) async-start(bf16[64,1,10]{2,1,0:T(2,128)(2,1)} %copy.22), calls=%async_computation.3 | async-start | bytes 65536 | tf_op jit(solution)/shard_map/all_to_all | solution.py:64
  40.1 189.1 %all-to-all-start = ((bf16[64,10,4096]{2,1,0:T(8,128)(2,1)}), bf16[64,10,4096]{2,1,0:T(8,128)(2,1)}, u32[]{:S(2)}, u32[]{:S(2)}) async-start(bf16[64,10,4096]{2,1,0:T(8,128)(2,1)} %bitcast.74), calls=%async_computation | async-start | bytes 16777216 | tf_op jit(solution)/shard_map/all_to_all | solution.py:62
  235.2 192.4 %all-to-all-start.3 = ((bf16[64,10,4096]{2,1,0:T(8,128)(2,1)}), bf16[64,10,4096]{2,1,0:T(8,128)(2,1)}, u32[]{:S(2)}, u32[]{:S(2)}) async-start(bf16[64,10,4096]{2,1,0:T(8,128)(2,1)} %bitcast.73), calls=%async_computation.4 | async-start | bytes 16777216 | tf_op jit(solution)/shard_map/all_to_all | solution.py:63
  244.7 315.8 %reduce-scatter.2.cloned.1.call-start = ((), (), s32[]{:S(2)}) async-start(), calls=%async_computation.6 | async-start | bytes 6553600 | tf_op jit(solution)/shard_map/reduce_scatter | solution.py:79
  245.0 8.8 %copy-start.5 = (bf16[1,1,192,4096]{3,2,1,0:T(8,128)(2,1)S(1)}, bf16[1,1,192,4096]{3,2,1,0:T(8,128)(2,1)}, u32[]{:S(2)}) copy-start(bf16[1,1,192,4096]{3,2,1,0:T(8,128)(2,1)} %param.12) | copy-start | bytes 4718596
  253.8 5.3 copy-start.2
  253.8 5.3 copy-start.3
  437.6 8.7 %copy-start.8 = (f32[640,192]{0,1:T(8,128)S(1)}, f32[640,192]{0,1:T(8,128)}, u32[]{:S(2)}) copy-start(f32[640,192]{0,1:T(8,128)} %fusion.10) | copy-start | bytes 1474564
  455.2 1.4 copy-start.4
  456.6 1.6 copy-start.6
  470.5 192.4 %all-to-all-start.4 = ((bf16[64,10,4096]{2,1,0:T(8,128)(2,1)}), bf16[64,10,4096]{2,1,0:T(8,128)(2,1)}, u32[]{:S(2)}, u32[]{:S(2)}) async-start(bf16[64,10,4096]{2,1,0:T(8,128)(2,1)} %reshape.108), calls=%async_computation.5 | async-start | bytes 16777216 | tf_op jit(solution)/shard_map/all_to_all | solution.py:117
  662.9 56.4 %all-to-all-start.1 = ((bf16[16,10,4096]{2,1,0:T(8,128)(2,1)}), bf16[16,10,4096]{2,1,0:T(8,128)(2,1)}, u32[]{:S(2)}, u32[]{:S(2)}) async-start(bf16[16,10,4096]{2,1,0:T(8,128)(2,1)} %copy.21), calls=%async_computation.2 | async-start | bytes 4194304 | tf_op jit(solution)/shard_map/all_to_all | solution.py:85
  680.7 27.9 %collective-permute-start = (bf16[128,4096]{1,0:T(8,128)(2,1)}, bf16[128,4096]{1,0:T(8,128)(2,1)}, u32[]{:S(2)}, u32[]{:S(2)}) collective-permute-start(bf16[128,4096]{1,0:T(8,128)(2,1)} %convolution_convert_fusion.5), channel_id=1, source_target_pairs={{64,0},{128,64},{192,128},{65,1},{129,65},{193,129},{66,2},{130,66... | collective-permute-start | bytes 3145736 | tf_op jit(solution)/shard_map/ppermute | solution.py:10
  708.6 14.2 %copy-start.7 = (f32[1,128,8]{1,2,0:T(8,128)S(1)}, f32[1,128,8]{1,2,0:T(8,128)}, u32[]{:S(2)}) copy-start(f32[1,128,8]{1,2,0:T(8,128)} %param.9) | copy-start | bytes 12292
  708.6 17.1 %copy-start.1 = (bf16[1,1,192,4096]{3,2,1,0:T(8,128)(2,1)S(1)}, bf16[1,1,192,4096]{3,2,1,0:T(8,128)(2,1)}, u32[]{:S(2)}) copy-start(bf16[1,1,192,4096]{3,2,1,0:T(8,128)(2,1)} %param.13) | copy-start | bytes 4718596
Sparse Core Ops, SparseCore 0:
  455.3 105.2 reduce-scatter.1
where the time goes:
time: 734 us; the launch traced here: 733 us
  waiting for transfers between devices  541 us (74%)
  local copies, waits for them, and re-layouts  62.5 us (9%)
  starting transfers between devices  47.4 us (6%)
  matrix products  45.2 us (6%)
  other arithmetic  21.8 us (3%)
  between operations  14.2 us (2%)
    all_to_all x1, waiting for transfers between devices, per_device(): lax.all_to_all(copies_x, ('expert', 'dp'), split_axis=0, concat_axis=0, t...  180 us
    all_to_all x1, waiting for transfers between devices, per_device(): lax.all_to_all(copies_upstream, ('expert', 'dp'), split_axis=0, concat_ax...  166 us
    all_to_all x1, waiting for transfers between devices, per_device(): lax.all_to_all(outgoing, ('expert', 'dp'), split_axis=0, concat_axis=0, t...  98.9 us
    reduce_scatter x1, waiting for transfers between devices, per_device(): lax.psum_scatter(partial_out.reshape(experts, groups, capacity, model_wid...  80.6 us
  transfers between devices with their start and end apart: 7, of which 6 were waited for; matrix products, arithmetic and copies ran while one was open for 11% of the time, Pallas kernels for 0%

commit v1 on v0

--- a/solution.py
+++ b/solution.py
@@ -43,32 +43,21 @@
         table_half, tokens_in, token_contract, preferred_element_type=jnp.float32
     )
     local_x = local_x.astype(jnp.bfloat16).reshape(experts, capacity, model_width)
-    local_upstream = lax.dot_general(
+    local_up = lax.dot_general(
         table_half, upstream, token_contract, preferred_element_type=jnp.float32
     )
-    local_upstream = local_upstream.astype(jnp.bfloat16).reshape(experts, capacity, model_width)
+    local_up = local_up.astype(jnp.bfloat16).reshape(experts, capacity, model_width)
     local_gate = jnp.sum(jnp.where(table, gate[:, None], jnp.float32(0.0)), axis=0)
     local_gate = local_gate.astype(jnp.bfloat16).reshape(experts, capacity)
-    copies_x = jnp.broadcast_to(local_x[:, None], (experts, groups, capacity, model_width)).reshape(
-        experts * groups, capacity, model_width
+    x_e = lax.all_to_all(local_x, "expert", 0, 0, tiled=True)
+    up_e = lax.all_to_all(local_up, "expert", 0, 0, tiled=True)
+    gate_e = lax.all_to_all(local_gate, "expert", 0, 0, tiled=True)
+    rows_x = lax.all_gather(x_e, "dp", axis=0, tiled=True).reshape(-1, model_width)
+    rows_up = lax.all_gather(up_e, "dp", axis=0, tiled=True).reshape(-1, model_width)
+    rows_gate = lax.all_gather(gate_e, "dp", axis=0, tiled=True).reshape(-1)
+    rows_grad = (rows_gate.astype(jnp.float32)[:, None] * rows_up.astype(jnp.float32)).astype(
+        jnp.bfloat16
     )
-    copies_upstream = jnp.broadcast_to(
-        local_upstream[:, None], (experts, groups, capacity, model_width)
-    ).reshape(experts * groups, capacity, model_width)
-    copies_gate = jnp.broadcast_to(local_gate[:, None], (experts, groups, capacity)).reshape(
-        experts * groups, capacity
-    )
-    rows_x, rows_upstream, rows_gate = (
-        lax.all_to_all(copies_x, ("expert", "dp"), split_axis=0, concat_axis=0, tiled=True),
-        lax.all_to_all(copies_upstream, ("expert", "dp"), split_axis=0, concat_axis=0, tiled=True),
-        lax.all_to_all(copies_gate, ("expert", "dp"), split_axis=0, concat_axis=0, tiled=True),
-    )
-    rows_x = rows_x.reshape(-1, model_width)
-    grid_upstream = rows_upstream.reshape(experts, groups, capacity, model_width)
-    rows_grad = (
-        rows_gate.reshape(-1).astype(jnp.float32)[:, None]
-        * grid_upstream.reshape(-1, model_width).astype(jnp.float32)
-    ).astype(jnp.bfloat16)
     gate_pre = lax.dot_general(
         rows_x, gate_mat, feature_contract, preferred_element_type=jnp.float32
     )
@@ -76,23 +65,12 @@
     gate_sig = jax.nn.sigmoid(gate_pre)
     activated = (gate_pre * gate_sig * up_pre).astype(jnp.bfloat16)
     partial_out = jnp.dot(activated, down_mat, preferred_element_type=jnp.float32)
-    summed_out = lax.psum_scatter(
-        partial_out.reshape(experts, groups, capacity, model_width).astype(jnp.bfloat16),
-        "dp",
-        scatter_dimension=1,
-        tiled=True,
-    )
-    flat_out = lax.all_to_all(
-        summed_out.reshape(experts, capacity, model_width),
-        "expert",
-        split_axis=0,
-        concat_axis=0,
-        tiled=True,
-    ).reshape(-1, model_width)
-    scores_grad = lax.dot_general(
-        upstream, flat_out, feature_contract, preferred_element_type=jnp.float32
-    )
-    gate_grad = jnp.sum(jnp.where(table, scores_grad, jnp.float32(0.0)), axis=1)
+    row_score = jnp.sum(partial_out * rows_up.astype(jnp.float32), axis=1)
+    row_score = lax.psum_scatter(
+        row_score.reshape(groups, experts, capacity), "dp", scatter_dimension=0, tiled=True
+    ).reshape(experts, capacity)
+    slot_score = lax.all_to_all(row_score, "expert", 0, 0, tiled=True).reshape(-1)
+    gate_grad = jnp.sum(jnp.where(table, slot_score[None, :], jnp.float32(0.0)), axis=1)
     is_first = (jnp.arange(score_rows.shape[1]) == 0).astype(jnp.float32)
     score_grad = gate_grad[:, None] * weights[:, 0:1] * (is_first - weights)
     hidden_grad = lax.dot_general(
@@ -113,12 +91,10 @@
     ).astype(jnp.bfloat16)
     partial_in = jnp.dot(pre_gate, gate_mat, preferred_element_type=jnp.float32)
     partial_in = partial_in + jnp.dot(pre_up, up_mat, preferred_element_type=jnp.float32)
-    outgoing = partial_in.astype(jnp.bfloat16).reshape(experts * groups, capacity, model_width)
-    arrived = lax.all_to_all(outgoing, ("expert", "dp"), split_axis=0, concat_axis=0, tiled=True)
-    flat_in = jnp.sum(
-        arrived.reshape(experts, groups, capacity, model_width).astype(jnp.float32), axis=1
-    )
-    flat_in = flat_in.astype(jnp.bfloat16).reshape(-1, model_width)
+    outgoing = partial_in.astype(jnp.bfloat16).reshape(groups, experts, capacity, model_width)
+    summed = lax.psum_scatter(outgoing, "dp", scatter_dimension=0, tiled=True)
+    summed = summed.reshape(experts, capacity, model_width)
+    flat_in = lax.all_to_all(summed, "expert", 0, 0, tiled=True).reshape(-1, model_width)
     input_grad = jnp.dot(table_half, flat_in, preferred_element_type=jnp.float32).astype(
         jnp.bfloat16
     )

time: 734 us -> 498 us (0.68)
  waiting for transfers between devices: 541 us -> 200 us
  blocking collectives: 0 us -> 134 us
  starting transfers between devices: 47.4 us -> 19.8 us
  local copies, waits for them, and re-layouts: 62.5 us -> 76.7 us
  other arithmetic: 21.8 us -> 8.57 us
    all_to_all x5 -> x2, waiting for transfers between devices: 461 us -> 55.1 us  [the longest x1 48.4 us: per_device(): lax.all_to_all(summed, 'expert', 0, 0, tiled=True).reshape(-1, model_width)]
    all_to_all x0 -> x3, blocking collectives: none -> 125 us  [the longest x1 61 us: per_device(): up_e = lax.all_to_all(local_up, 'expert', 0, 0, tiled=True)]
    all_gather x0 -> x2, waiting for transfers between devices: none -> 35 us  [the longest x1 35 us: per_device(): lax.all_gather(x_e, 'dp', axis=0, tiled=True).reshape(-1, model_width)]
    all_to_all x5 -> x2, starting transfers between devices: 45.6 us -> 17.6 us  [the longest x1 9.91 us: per_device(): lax.all_to_all(row_score, 'expert', 0, 0, tiled=True).reshape(-1)]
    reduce_scatter x1 -> x2, waiting for transfers between devices: 80.6 us -> 102 us  [the longest x1 80.8 us: per_device(): summed = lax.psum_scatter(outgoing, 'dp', scatter_dimension=0, tiled=True)]
    convert_element_type x4 -> x6, local copies, waits for them, and re-layouts: 18.7 us -> 39.8 us  [the longest x2 24.5 us: per_device(): row_score = jnp.sum(partial_out * rows_up.astype(jnp.float32), axis=1)]
    broadcast_in_dim x5 -> x1, local copies, waits for them, and re-layouts: 15 us -> 0.08 us  [per_device(): jnp.where(table, slot_score[None, :], jnp.float32(0.0))]
    all_gather x0 -> x1, blocking collectives: none -> 9.03 us  [per_device(): rows_gate = lax.all_gather(gate_e, 'dp', axis=0, tiled=True).reshape(-1)]
  transfers between devices with their start and end apart: 7 -> 7, of which waited for: 6 -> 6; matrix products, arithmetic and copies ran while one was open for 11% -> 9% of each run, Pallas kernels for 0% -> 0%
where the time goes in v1:
time: 498 us; the launch traced here: 497 us
  waiting for transfers between devices  200 us (40%)
  blocking collectives  134 us (27%)
  local copies, waits for them, and re-layouts  76.7 us (15%)
  matrix products  43 us (9%)
  starting transfers between devices  19.8 us (4%)
  between operations  14.1 us (3%)
  other arithmetic  8.57 us (2%)
    reduce_scatter x1, waiting for transfers between devices, per_device(): summed = lax.psum_scatter(outgoing, 'dp', scatter_dimension=0, tiled=True)  80.8 us
    all_to_all x1, blocking collectives, per_device(): up_e = lax.all_to_all(local_up, 'expert', 0, 0, tiled=True)  61 us
    all_to_all x1, blocking collectives, per_device(): x_e = lax.all_to_all(local_x, 'expert', 0, 0, tiled=True)  53.9 us
    all_to_all x1, waiting for transfers between devices, per_device(): lax.all_to_all(summed, 'expert', 0, 0, tiled=True).reshape(-1, model_width)  48.4 us
    all_gather x1, waiting for transfers between devices, per_device(): lax.all_gather(x_e, 'dp', axis=0, tiled=True).reshape(-1, model_width)  35 us
    convert_element_type x2, local copies, waits for them, and re-layouts, per_device(): row_score = jnp.sum(partial_out * rows_up.astype(jnp.float32), axis=1)  24.5 us
    reduce_scatter x1, waiting for transfers between devices, per_device(): lax.psum_scatter(row_score.reshape(groups, experts, capacity), 'dp', scat...  21.3 us
    convert_element_type x2, local copies, waits for them, and re-layouts, per_device(): (rows_gate.astype(jnp.float32)[:, None] * rows_up.astype(jnp.float32)).as...  15.1 us
  transfers between devices with their start and end apart: 7, of which 6 were waited for; matrix products, arithmetic and copies ran while one was open for 9% of the time, Pallas kernels for 0%

profile of v1, /device:TPU:1, one launch (start us, length us, event | category | flops | bytes accessed | tf_op | source)
XLA Modules:
  0.0 496.6 jit_solution(5466417958805610884)
XLA Ops:
  13.1 61.0 %all_to_all.33 = bf16[16,10,4096]{2,1,0:T(8,128)(2,1)S(1)} all-to-all(bf16[16,10,4096]{2,1,0:T(8,128)(2,1)} %reshape.106), channel_id=1, replica_groups=mesh['pipe'=4,'expert'=16,'dp'=4] {'expert'}, dimensions={0} | all-to-all | bytes 2621440 | tf_op jit(solution)/shard_map/all_to_all | solution.py:53
  79.2 53.9 %all_to_all.34 = bf16[16,10,4096]{2,1,0:T(8,128)(2,1)S(1)} all-to-all(bf16[16,10,4096]{2,1,0:T(8,128)(2,1)} %reshape.104), channel_id=1, replica_groups=mesh['pipe'=4,'expert'=16,'dp'=4] {'expert'}, dimensions={0} | all-to-all | bytes 2621440 | tf_op jit(solution)/shard_map/all_to_all | solution.py:52
  135.2 12.2 %copy.39 = f32[64,10,4096]{2,1,0:T(8,128)} copy(bf16[64,10,4096]{2,0,1:T(8,128)(2,1)} %all-gather.6.cloned.1.call-done) | data formatting | bytes 15728640 | tf_op jit(solution)/shard_map/convert_element_type | solution.py:68
  147.4 12.4 %reshape.111 = f32[640,4096]{1,0:T(8,128)} reshape(f32[64,10,4096]{2,1,0:T(8,128)} %copy.39) | data formatting | bytes 20971520 | tf_op jit(solution)/shard_map/convert_element_type | solution.py:68
  159.7 35.0 %all-gather.4.cloned.1.call-done = bf16[64,10,4096]{2,0,1:T(8,128)(2,1)} async-done(((bf16[16,10,4096]{2,0,1:T(8,128)(2,1)}), bf16[64,10,4096]{2,0,1:T(8,128)(2,1)}) %all-gather.4.cloned.1.call-update) | async-done | bytes 5242896 | tf_op jit(solution)/shard_map/all_gather | solution.py:55
  194.7 8.9 %copy.37 = bf16[64,10,4096]{2,1,0:T(8,128)(2,1)} copy(bf16[64,10,4096]{2,0,1:T(8,128)(2,1)} %all-gather.4.cloned.1.call-done) | data formatting | bytes 10485760 | tf_op jit(solution)/shard_map/all_gather | solution.py:55
  203.7 8.7 %reshape.105 = bf16[640,4096]{1,0:T(8,128)(2,1)} reshape(bf16[64,10,4096]{2,1,0:T(8,128)(2,1)} %copy.37) | data formatting | bytes 10485760 | tf_op jit(solution)/shard_map/reshape | solution.py:55
  217.0 4.6 multiply_convert_fusion.9
  224.2 21.3 %reduce-scatter.3.cloned.1.call-done = f32[1,16,10]{2,1,0:T(8,128)} async-done(((f32[4,16,10]{2,1,0:T(8,128)}), f32[1,16,10]{2,1,0:T(8,128)}) %reduce-scatter.3.cloned.1.call-update) | async-done | bytes 656 | tf_op jit(solution)/shard_map/reduce_scatter | solution.py:69
  245.5 9.9 %all-to-all-start.2 = ((f32[16,1,10]{2,1,0:T(1,128)}), f32[16,1,10]{2,1,0:T(1,128)S(1)}, u32[]{:S(2)}, u32[]{:S(2)}) async-start(f32[16,1,10]{2,1,0:T(1,128)} %bitcast.68), calls=%async_computation.3 | async-start | bytes 16384 | tf_op jit(solution)/shard_map/all_to_all | solution.py:72
  255.7 6.7 %all-to-all-done.2 = f32[16,1,10]{2,1,0:T(1,128)S(1)} async-done(((f32[16,1,10]{2,1,0:T(1,128)}), f32[16,1,10]{2,1,0:T(1,128)S(1)}, u32[]{:S(2)}, u32[]{:S(2)}) %all-to-all-start.2) | async-done | bytes 672 | tf_op jit(solution)/shard_map/all_to_all | solution.py:72
  264.0 10.1 %all_to_all.35 = bf16[16,1,10]{2,1,0:T(2,128)(2,1)S(1)} all-to-all(bf16[16,1,10]{2,1,0:T(2,128)(2,1)S(1)} %convert_element_type.125), channel_id=1, replica_groups=mesh['pipe'=4,'expert'=16,'dp'=4] {'expert'}, dimensions={0} | all-to-all | bytes 640 | tf_op jit(solution)/shard_map/all_to_all | solution.py:54
  274.1 9.0 %all-gather = bf16[64,1,10]{2,0,1:T(8,128)(2,1)S(1)} all-gather(bf16[16,1,10]{2,0,1:T(8,128)(2,1)S(1)} %copy.42), channel_id=2, replica_groups=mesh['pipe'=4,'expert'=16,'dp'=4] {'dp'}, dimensions={0}, use_global_device_ids=true | all-gather | bytes 1600 | tf_op jit(solution)/shard_map/all_gather | solution.py:57
  287.7 6.4 %copy.44 = bf16[64,10,4096]{2,1,0:T(8,128)(2,1)} copy(bf16[64,10,4096]{2,0,1:T(8,128)(2,1)S(1)} %multiply_convert_fusion.1) | data formatting | bytes 10485760 | tf_op jit(solution)/shard_map/convert_element_type | solution.py:58
  294.1 8.7 %convert_element_type.110 = bf16[640,4096]{1,0:T(8,128)(2,1)} reshape(bf16[64,10,4096]{2,1,0:T(8,128)(2,1)} %copy.44) | data formatting | bytes 10485760 | tf_op jit(solution)/shard_map/convert_element_type | solution.py:58
  302.8 5.0 %multiply_convert_fusion.7 = (bf16[640,192]{0,1:T(8,128)(2,1)S(1)}, bf16[640,192]{0,1:T(8,128)(2,1)S(1)}) fusion(f32[640,192]{0,1:T(8,128)S(1)} %copy-done.8, f32[640,192]{0,1:T(8,128)S(1)} %get-tuple-element.10, bf16[640,4096]{1,0:T(8,128)(2,1)} %convert_element_type.110, bf16[1,1,192,4096]{3,2,1,0:T(8,128)(2,1)} %param.13), kind=kOutput, calls=%fused_computation.27 | convolution fusion | flops 1008230400 | bytes 8290304 | tf_op jit(solution)/shard_map/dot_general | solution.py:76
  313.5 8.2 %reshape.108 = bf16[4,16,10,4096]{3,2,1,0:T(8,128)(2,1)} reshape(bf16[640,4096]{1,0:T(8,128)(2,1)} %add_convert_fusion) | data formatting | bytes 10485760 | tf_op jit(solution)/shard_map/reshape | solution.py:94
  321.7 80.8 %reduce-scatter.5.cloned.1.call-done = bf16[1,16,10,4096]{3,2,1,0:T(8,128)(2,1)} async-done(((bf16[4,16,10,4096]{3,2,1,0:T(8,128)(2,1)}), bf16[1,16,10,4096]{3,2,1,0:T(8,128)(2,1)}) %reduce-scatter.5.cloned.1.call-update) | async-done | bytes 1310736 | tf_op jit(solution)/shard_map/reduce_scatter | solution.py:95
  402.5 7.6 %all-to-all-start.4 = ((bf16[16,10,4096]{2,1,0:T(8,128)(2,1)}), bf16[16,10,4096]{2,1,0:T(8,128)(2,1)}, u32[]{:S(2)}, u32[]{:S(2)}) async-start(bf16[16,10,4096]{2,1,0:T(8,128)(2,1)} %bitcast.66), calls=%async_computation.6 | async-start | bytes 4194304 | tf_op jit(solution)/shard_map/all_to_all | solution.py:97
  410.8 48.4 %all-to-all-done.4 = bf16[16,10,4096]{2,1,0:T(8,128)(2,1)} async-done(((bf16[16,10,4096]{2,1,0:T(8,128)(2,1)}), bf16[16,10,4096]{2,1,0:T(8,128)(2,1)}, u32[]{:S(2)}, u32[]{:S(2)}) %all-to-all-start.4) | async-done | bytes 1310752 | tf_op jit(solution)/shard_map/all_to_all | solution.py:97
  464.1 5.0 %fusion.4 = bf16[1,1,192,4096]{3,2,1,0:T(8,128)(2,1)} fusion(bf16[640,192]{0,1:T(8,128)(2,1)S(1)} %get-tuple-element.8, bf16[640,4096]{1,0:T(8,128)(2,1)} %reshape.105), kind=kOutput, calls=%fused_computation.13 | convolution fusion | flops 1007419392 | bytes 7061504 | tf_op jit(solution)/shard_map/dot_general | solution.py:86
  469.3 5.0 %fusion.5 = bf16[1,1,192,4096]{3,2,1,0:T(8,128)(2,1)} fusion(bf16[640,192]{0,1:T(8,128)(2,1)S(1)} %copy-done.2, bf16[640,4096]{1,0:T(8,128)(2,1)} %reshape.105), kind=kOutput, calls=%fused_computation.14 | convolution fusion | flops 1007419392 | bytes 7061504 | tf_op jit(solution)/shard_map/dot_general | solution.py:89
  474.3 6.6 %fusion.3 = bf16[1,1,192,4096]{3,2,1,0:T(8,128)(2,1)} fusion(bf16[640,192]{0,1:T(8,128)(2,1)S(1)} %get-tuple-element.9, f32[640,4096]{1,0:T(8,128)} %reshape.111, f32[640]{0:T(1024)S(1)} %reshape.112), kind=kOutput, calls=%fused_computation.12 | convolution fusion | flops 1012662272 | bytes 12306944 | tf_op jit(solution)/shard_map/dot_general | solution.py:83
  480.9 8.2 %collective-permute-done = bf16[128,4096]{1,0:T(8,128)(2,1)S(1)} collective-permute-done((bf16[128,4096]{1,0:T(8,128)(2,1)}, bf16[128,4096]{1,0:T(8,128)(2,1)S(1)}, u32[]{:S(2)}, u32[]{:S(2)}) %collective-permute-start) | collective-permute-done | bytes 1048608 | tf_op jit(solution)/shard_map/ppermute | solution.py:10
  (70 shorter events, 38.9 us)
Async XLA Ops:
  7.2 209.8 %copy-start = (bf16[1,1,192,4096]{3,2,1,0:T(8,128)(2,1)S(1)}, bf16[1,1,192,4096]{3,2,1,0:T(8,128)(2,1)}, u32[]{:S(2)}) copy-start(bf16[1,1,192,4096]{3,2,1,0:T(8,128)(2,1)} %param.12) | copy-start | bytes 4718596
  7.2 128.0 %all-gather.6.cloned.1.call-start = ((), (), s32[]{:S(2)}) async-start(), calls=%async_computation.8 | async-start | bytes 6553600 | tf_op jit(solution)/shard_map/all_gather | solution.py:56
  75.9 118.9 %all-gather.4.cloned.1.call-start = ((), (), s32[]{:S(2)}) async-start(), calls=%async_computation.7 | async-start | bytes 6553600 | tf_op jit(solution)/shard_map/all_gather | solution.py:55
  133.1 2.0 copy-start.6
  134.9 110.6 %reduce-scatter.3.cloned.1.call-start = ((), (), s32[]{:S(2)}) async-start(), calls=%async_computation.9 | async-start | bytes 40960 | tf_op jit(solution)/shard_map/reduce_scatter | solution.py:69
  203.7 8.7 %copy-start.4 = (bf16[1,1,192,4096]{3,2,1,0:T(8,128)(2,1)S(1)}, bf16[1,1,192,4096]{3,2,1,0:T(8,128)(2,1)}, u32[]{:S(2)}) copy-start(bf16[1,1,192,4096]{3,2,1,0:T(8,128)(2,1)} %param.11) | copy-start | bytes 4718596
  212.4 9.2 %slice-start = ((s8[10485760]{0:T(1024)(128)(4,1)}), s8[4194304]{0:T(1024)(128)(4,1)S(1)}, s32[]{:S(2)}) async-start(s8[10485760]{0:T(1024)(128)(4,1)} %bitcast.64), calls=%async_computation.11 | async-start | bytes 8388608
  212.4 9.2 %slice-start.1 = ((s8[10485760]{0:T(1024)(128)(4,1)}), s8[4194304]{0:T(1024)(128)(4,1)S(1)}, s32[]{:S(2)}) async-start(s8[10485760]{0:T(1024)(128)(4,1)} %bitcast.64), calls=%async_computation.12 | async-start | bytes 8388608
  216.9 4.6 copy-start.7
  216.9 4.6 slice-start.2
  216.9 4.6 copy-start.3
  245.5 16.9 %all-to-all-start.2 = ((f32[16,1,10]{2,1,0:T(1,128)}), f32[16,1,10]{2,1,0:T(1,128)S(1)}, u32[]{:S(2)}, u32[]{:S(2)}) async-start(f32[16,1,10]{2,1,0:T(1,128)} %bitcast.68), calls=%async_computation.3 | async-start | bytes 16384 | tf_op jit(solution)/shard_map/all_to_all | solution.py:72
  255.4 147.1 %reduce-scatter.5.cloned.1.call-start = ((), (), s32[]{:S(2)}) async-start(), calls=%async_computation.10 | async-start | bytes 10485760 | tf_op jit(solution)/shard_map/reduce_scatter | solution.py:95
  294.1 8.7 %copy-start.8 = (f32[640,192]{0,1:T(8,128)S(1)}, f32[640,192]{0,1:T(8,128)}, u32[]{:S(2)}) copy-start(f32[640,192]{0,1:T(8,128)} %copy-done.7) | copy-start | bytes 1474564
  302.8 5.0 %copy-start.5 = (bf16[1,1,192,4096]{3,2,1,0:T(8,128)(2,1)S(1)}, bf16[1,1,192,4096]{3,2,1,0:T(8,128)(2,1)}, u32[]{:S(2)}) copy-start(bf16[1,1,192,4096]{3,2,1,0:T(8,128)(2,1)} %param.11) | copy-start | bytes 4718596
  307.8 1.6 copy-start.1
  402.5 56.7 %all-to-all-start.4 = ((bf16[16,10,4096]{2,1,0:T(8,128)(2,1)}), bf16[16,10,4096]{2,1,0:T(8,128)(2,1)}, u32[]{:S(2)}, u32[]{:S(2)}) async-start(bf16[16,10,4096]{2,1,0:T(8,128)(2,1)} %bitcast.66), calls=%async_computation.6 | async-start | bytes 4194304 | tf_op jit(solution)/shard_map/all_to_all | solution.py:97
  462.4 6.9 %copy-start.2 = (bf16[640,192]{0,1:T(8,128)(2,1)S(1)}, bf16[640,192]{0,1:T(8,128)(2,1)}, u32[]{:S(2)}) copy-start(bf16[640,192]{0,1:T(8,128)(2,1)} %copy-done.1) | copy-start | bytes 737284
  462.4 26.6 %collective-permute-start = (bf16[128,4096]{1,0:T(8,128)(2,1)}, bf16[128,4096]{1,0:T(8,128)(2,1)S(1)}, u32[]{:S(2)}, u32[]{:S(2)}) collective-permute-start(bf16[128,4096]{1,0:T(8,128)(2,1)} %convolution_convert_fusion.4), channel_id=1, source_target_pairs={{64,0},{128,64},{192,128},{65,1},{129,65},{193,129},{66,2},{130,66... | collective-permute-start | bytes 3145736 | tf_op jit(solution)/shard_map/ppermute | solution.py:10
Sparse Core Ops, SparseCore 0:
  76.0 56.2 all-gather.5
  135.1 59.6 all-gather.3
  224.3 21.1 reduce-scatter.2
  321.8 80.6 reduce-scatter.4

commit v2 on v1

--- a/solution.py
+++ b/solution.py
@@ -23,6 +23,10 @@
     return (weights, gate, table)
 
 
+def dense_chunks(rows, chunks):
+    return rows.reshape(chunks, -1, 1024)
+
+
 def per_device(inputs, routes, router_scores, cotangent, w_gate, w_up, w_down):
     tokens_in = inputs[0]
     upstream = cotangent[0]
@@ -33,31 +37,27 @@
     down_mat = w_down[0, 0]
     experts = lax.axis_size("expert")
     groups = lax.axis_size("dp")
+    my_expert = lax.axis_index("expert")
+    my_group = lax.axis_index("dp")
     token_count, model_width = tokens_in.shape
     capacity = max(2, token_count * 5 // (4 * experts))
     weights, gate, table = route_tables(route_col, score_rows, experts, capacity)
     table_half = table.astype(jnp.bfloat16)
     token_contract = (((0,), (0,)), ((), ()))
     feature_contract = (((1,), (1,)), ((), ()))
+    scaled = (gate[:, None] * upstream.astype(jnp.float32)).astype(jnp.bfloat16)
     local_x = lax.dot_general(
         table_half, tokens_in, token_contract, preferred_element_type=jnp.float32
-    )
-    local_x = local_x.astype(jnp.bfloat16).reshape(experts, capacity, model_width)
-    local_up = lax.dot_general(
-        table_half, upstream, token_contract, preferred_element_type=jnp.float32
-    )
-    local_up = local_up.astype(jnp.bfloat16).reshape(experts, capacity, model_width)
-    local_gate = jnp.sum(jnp.where(table, gate[:, None], jnp.float32(0.0)), axis=0)
-    local_gate = local_gate.astype(jnp.bfloat16).reshape(experts, capacity)
-    x_e = lax.all_to_all(local_x, "expert", 0, 0, tiled=True)
-    up_e = lax.all_to_all(local_up, "expert", 0, 0, tiled=True)
-    gate_e = lax.all_to_all(local_gate, "expert", 0, 0, tiled=True)
-    rows_x = lax.all_gather(x_e, "dp", axis=0, tiled=True).reshape(-1, model_width)
-    rows_up = lax.all_gather(up_e, "dp", axis=0, tiled=True).reshape(-1, model_width)
-    rows_gate = lax.all_gather(gate_e, "dp", axis=0, tiled=True).reshape(-1)
-    rows_grad = (rows_gate.astype(jnp.float32)[:, None] * rows_up.astype(jnp.float32)).astype(
-        jnp.bfloat16
-    )
+    ).astype(jnp.bfloat16)
+    local_dy = lax.dot_general(
+        table_half, scaled, token_contract, preferred_element_type=jnp.float32
+    ).astype(jnp.bfloat16)
+    x_e = lax.all_to_all(dense_chunks(local_x, experts), "expert", 0, 0, tiled=True)
+    x_e = x_e.reshape(experts * capacity, model_width)
+    rows_x = lax.all_gather(x_e, "dp", axis=0, tiled=True)
+    dy_e = lax.all_to_all(dense_chunks(local_dy, experts), "expert", 0, 0, tiled=True)
+    dy_e = dy_e.reshape(experts * capacity, model_width)
+    rows_grad = lax.all_gather(dy_e, "dp", axis=0, tiled=True)
     gate_pre = lax.dot_general(
         rows_x, gate_mat, feature_contract, preferred_element_type=jnp.float32
     )
@@ -65,12 +65,15 @@
     gate_sig = jax.nn.sigmoid(gate_pre)
     activated = (gate_pre * gate_sig * up_pre).astype(jnp.bfloat16)
     partial_out = jnp.dot(activated, down_mat, preferred_element_type=jnp.float32)
-    row_score = jnp.sum(partial_out * rows_up.astype(jnp.float32), axis=1)
-    row_score = lax.psum_scatter(
-        row_score.reshape(groups, experts, capacity), "dp", scatter_dimension=0, tiled=True
-    ).reshape(experts, capacity)
-    slot_score = lax.all_to_all(row_score, "expert", 0, 0, tiled=True).reshape(-1)
-    gate_grad = jnp.sum(jnp.where(table, slot_score[None, :], jnp.float32(0.0)), axis=1)
+    row_score = jnp.sum(partial_out * rows_grad.astype(jnp.float32), axis=1)
+    all_scores = lax.all_gather(row_score, ("expert", "dp"), axis=0, tiled=False)
+    all_scores = jnp.sum(all_scores.reshape(experts, groups, -1), axis=1)
+    all_scores = all_scores.reshape(experts, groups, experts, capacity)
+    mine = lax.dynamic_index_in_dim(all_scores, my_group, axis=1, keepdims=False)
+    mine = lax.dynamic_index_in_dim(mine, my_expert, axis=1, keepdims=False)
+    slot_score = mine.reshape(-1)
+    picked = jnp.sum(jnp.where(table, slot_score[None, :], jnp.float32(0.0)), axis=1)
+    gate_grad = picked / gate
     is_first = (jnp.arange(score_rows.shape[1]) == 0).astype(jnp.float32)
     score_grad = gate_grad[:, None] * weights[:, 0:1] * (is_first - weights)
     hidden_grad = lax.dot_general(
@@ -91,10 +94,9 @@
     ).astype(jnp.bfloat16)
     partial_in = jnp.dot(pre_gate, gate_mat, preferred_element_type=jnp.float32)
     partial_in = partial_in + jnp.dot(pre_up, up_mat, preferred_element_type=jnp.float32)
-    outgoing = partial_in.astype(jnp.bfloat16).reshape(groups, experts, capacity, model_width)
-    summed = lax.psum_scatter(outgoing, "dp", scatter_dimension=0, tiled=True)
-    summed = summed.reshape(experts, capacity, model_width)
-    flat_in = lax.all_to_all(summed, "expert", 0, 0, tiled=True).reshape(-1, model_width)
+    summed = lax.psum_scatter(partial_in.astype(jnp.bfloat16), "dp", scatter_dimension=0, tiled=True)
+    back = lax.all_to_all(dense_chunks(summed, experts), "expert", 0, 0, tiled=True)
+    flat_in = back.reshape(experts * capacity, model_width)
     input_grad = jnp.dot(table_half, flat_in, preferred_element_type=jnp.float32).astype(
         jnp.bfloat16
     )

time: 498 us -> 406 us (0.82)
  local copies, waits for them, and re-layouts: 76.7 us -> 19.7 us
  waiting for transfers between devices: 200 us -> 144 us
  blocking collectives: 134 us -> 171 us
  starting transfers between devices: 19.8 us -> 9.04 us
    all_gather x1, blocking collectives: 9.03 us -> 89.3 us  [per_device(): lax.all_gather(row_score, ('expert', 'dp'), axis=0, tiled=False)]
    all_to_all x2 -> x1, waiting for transfers between devices: 55.1 us -> 0.01 us  [per_device(): lax.all_to_all(dense_chunks(summed, experts), 'expert', 0, 0, tiled=True)]
    all_to_all x3 -> x2, blocking collectives: 125 us -> 81.2 us  [the longest x1 44.1 us: per_device(): lax.all_to_all(dense_chunks(local_x, experts), 'expert', 0, 0, tiled=True)]
    reduce_scatter x2 -> x1, waiting for transfers between devices: 102 us -> 58.7 us  [per_device(): lax.psum_scatter(partial_in.astype(jnp.bfloat16), 'dp', scatter_dimension...]
    convert_element_type x7 -> x0, local copies, waits for them, and re-layouts: 39.9 us -> none  [the longest x2 24.5 us: per_device(): row_score = jnp.sum(partial_out * rows_up.astype(jnp.float32), axis=1)]
    all_gather x2, waiting for transfers between devices: 35 us -> 69 us  [the longest x1 55.5 us: per_device(): rows_grad = lax.all_gather(dy_e, 'dp', axis=0, tiled=True)]
    all_to_all x2 -> x1, starting transfers between devices: 17.6 us -> 7.63 us  [per_device(): lax.all_to_all(dense_chunks(summed, experts), 'expert', 0, 0, tiled=True)]
    all_gather x1 -> x0, local copies, waits for them, and re-layouts: 8.94 us -> none  [per_device(): lax.all_gather(x_e, 'dp', axis=0, tiled=True).reshape(-1, model_width)]
  transfers between devices with their start and end apart: 7 -> 5, of which waited for: 6 -> 4; matrix products, arithmetic and copies ran while one was open for 9% -> 9% of each run, Pallas kernels for 0% -> 0%
where the time goes in v2:
time: 406 us; the launch traced here: 405 us
  blocking collectives  171 us (42%)
  waiting for transfers between devices  144 us (35%)
  matrix products  42.2 us (10%)
  local copies, waits for them, and re-layouts  19.7 us (5%)
  between operations  13.9 us (3%)
  starting transfers between devices  9.04 us (2%)
  other arithmetic  5.6 us (1%)
    all_gather x1, blocking collectives, per_device(): lax.all_gather(row_score, ('expert', 'dp'), axis=0, tiled=False)  89.3 us
    reduce_scatter x1, waiting for transfers between devices, per_device(): lax.psum_scatter(partial_in.astype(jnp.bfloat16), 'dp', scatter_dimension...  58.7 us
    all_gather x1, waiting for transfers between devices, per_device(): rows_grad = lax.all_gather(dy_e, 'dp', axis=0, tiled=True)  55.5 us
    all_to_all x1, blocking collectives, per_device(): lax.all_to_all(dense_chunks(local_x, experts), 'expert', 0, 0, tiled=True)  44.1 us
    all_to_all x1, blocking collectives, per_device(): lax.all_to_all(dense_chunks(local_dy, experts), 'expert', 0, 0, tiled=True)  37.1 us
    ppermute x1, waiting for transfers between devices, from_behind(): return lax.ppermute(shard, axis, pairs)  16.2 us
    all_gather x1, waiting for transfers between devices, per_device(): rows_x = lax.all_gather(x_e, 'dp', axis=0, tiled=True)  13.4 us
  transfers between devices with their start and end apart: 5, of which 4 were waited for; matrix products, arithmetic and copies ran while one was open for 9% of the time, Pallas kernels for 0%

profile of v2, /device:TPU:1, one launch (start us, length us, event | category | flops | bytes accessed | tf_op | source)
XLA Modules:
  0.0 404.9 jit_solution(13463296433817005410)
XLA Ops:
  9.8 2.8 convolution_convert_fusion.4
  12.5 2.5 reshape.75
  15.0 44.1 %all_to_all.15 = bf16[16,40,1024]{2,1,0:T(8,128)(2,1)} all-to-all(bf16[16,40,1024]{2,1,0:T(8,128)(2,1)S(1)} %reshape.75), channel_id=1, replica_groups=mesh['pipe'=4,'expert'=16,'dp'=4] {'expert'}, dimensions={0} | all-to-all | bytes 2621440 | tf_op jit(solution)/shard_map/all_to_all | solution.py:55
  59.1 3.4 reshape.76
  63.1 1.8 convolution_convert_fusion.3
  65.0 1.6 reshape.77
  66.6 37.1 %all_to_all.16 = bf16[16,40,1024]{2,1,0:T(8,128)(2,1)S(1)} all-to-all(bf16[16,40,1024]{2,1,0:T(8,128)(2,1)} %reshape.77), channel_id=1, replica_groups=mesh['pipe'=4,'expert'=16,'dp'=4] {'expert'}, dimensions={0} | all-to-all | bytes 2621440 | tf_op jit(solution)/shard_map/all_to_all | solution.py:58
  105.5 13.4 %all-gather.5.cloned.1.call-done = bf16[640,4096]{1,0:T(8,128)(2,1)} async-done(((bf16[160,4096]{1,0:T(8,128)(2,1)}), bf16[640,4096]{1,0:T(8,128)(2,1)}) %all-gather.5.cloned.1.call-update) | async-done | bytes 5242896 | tf_op jit(solution)/shard_map/all_gather | solution.py:57
  118.9 5.0 %fusion.8 = f32[640,192]{0,1:T(8,128)S(1)} fusion(bf16[640,4096]{1,0:T(8,128)(2,1)} %all-gather.5.cloned.1.call-done, bf16[1,1,192,4096]{3,2,1,0:T(8,128)(2,1)} %param.12), kind=kOutput, calls=%fused_computation.17 | convolution fusion | flops 1006632960 | bytes 7307264 | tf_op jit(solution)/shard_map/dot_general | solution.py:64
  123.9 1.9 fusion.12
  125.8 55.5 %all-gather.7.cloned.1.call-done = bf16[640,4096]{1,0:T(8,128)(2,1)} async-done(((bf16[160,4096]{1,0:T(8,128)(2,1)}), bf16[640,4096]{1,0:T(8,128)(2,1)}) %all-gather.7.cloned.1.call-update) | async-done | bytes 5242896 | tf_op jit(solution)/shard_map/all_gather | solution.py:60
  181.4 5.6 %multiply_convert_fusion = (bf16[640,192]{0,1:T(8,128)(2,1)S(1)}, bf16[640,192]{0,1:T(8,128)(2,1)S(1)}, bf16[640,192]{0,1:T(8,128)(2,1)}) fusion(f32[640,192]{0,1:T(8,128)S(1)} %fusion.12, f32[640,192]{0,1:T(8,128)S(1)} %fusion.8, bf16[640,4096]{1,0:T(8,128)(2,1)} %all-gather.7.cloned.1.call-done, bf16[1,1,192,4096]{3,2,1,0:T(8,128)(2,1)} %param.13), kind=kOutput, calls=%fused_computation.26 | convolution fusion | flops 1008599040 | bytes 8536064 | tf_op jit(solution)/shard_map/dot_general | solution.py:79
  188.6 4.0 add_convert_fusion
  192.6 58.7 %reduce-scatter.2.cloned.1.call-done = bf16[160,4096]{1,0:T(8,128)(2,1)} async-done(((bf16[640,4096]{1,0:T(8,128)(2,1)}), bf16[160,4096]{1,0:T(8,128)(2,1)}) %reduce-scatter.2.cloned.1.call-update) | async-done | bytes 1310736 | tf_op jit(solution)/shard_map/reduce_scatter | solution.py:97
  251.3 3.4 reshape.81
  254.7 7.6 %all-to-all-start.2 = ((bf16[16,40,1024]{2,1,0:T(8,128)(2,1)}), bf16[16,40,1024]{2,1,0:T(8,128)(2,1)S(1)}, u32[]{:S(2)}, u32[]{:S(2)}) async-start(bf16[16,40,1024]{2,1,0:T(8,128)(2,1)} %reshape.81), calls=%async_computation.3 | async-start | bytes 2621440 | tf_op jit(solution)/shard_map/all_to_all | solution.py:98
  262.8 4.7 %multiply_reduce_fusion = f32[640]{0:T(1024)S(1)} fusion(bf16[640,4096]{1,0:T(8,128)(2,1)} %all-gather.7.cloned.1.call-done, bf16[640,192]{0,1:T(8,128)(2,1)} %get-tuple-element.7, bf16[1,1,192,4096]{3,2,1,0:T(8,128)(2,1)} %param.13), kind=kOutput, calls=%fused_computation.1 | convolution fusion | flops 1014496640 | bytes 7064064 | tf_op jit(solution)/shard_map/dot_general | solution.py:67
  267.5 89.3 %all-gather.1 = f32[64,1,640]{2,1,0:T(1,128)S(1)} all-gather(f32[1,1,640]{2,1,0:T(1,128)S(1)} %reshape.86), channel_id=2, replica_groups=mesh['pipe'=4,'expert'=16,'dp'=4] {'expert','dp'}, dimensions={0}, use_global_device_ids=true | all-gather | bytes 166400 | tf_op jit(solution)/shard_map/all_gather | solution.py:69
  359.6 2.1 reshape.80
  362.7 5.2 %fusion.2 = bf16[1,1,192,4096]{3,2,1,0:T(8,128)(2,1)} fusion(bf16[640,192]{0,1:T(8,128)(2,1)} %get-tuple-element.7, bf16[640,4096]{1,0:T(8,128)(2,1)} %all-gather.7.cloned.1.call-done), kind=kOutput, calls=%fused_computation.10 | convolution fusion | flops 1007419392 | bytes 7061504 | tf_op jit(solution)/shard_map/dot_general | solution.py:86
  369.6 1.9 convolution_convert_fusion.5
  373.5 5.1 %fusion.1 = bf16[1,1,192,4096]{3,2,1,0:T(8,128)(2,1)} fusion(bf16[640,192]{0,1:T(8,128)(2,1)S(1)} %get-tuple-element.5, bf16[640,4096]{1,0:T(8,128)(2,1)} %all-gather.5.cloned.1.call-done), kind=kOutput, calls=%fused_computation.9 | convolution fusion | flops 1007419392 | bytes 7061504 | tf_op jit(solution)/shard_map/dot_general | solution.py:92
  378.7 2.6 fusion
  381.3 16.2 %collective-permute-done = bf16[128,4096]{1,0:T(8,128)(2,1)S(1)} collective-permute-done((bf16[128,4096]{1,0:T(8,128)(2,1)S(1)}, bf16[128,4096]{1,0:T(8,128)(2,1)S(1)}, u32[]{:S(2)}, u32[]{:S(2)}) %collective-permute-start) | collective-permute-done | bytes 1048608 | tf_op jit(solution)/shard_map/ppermute | solution.py:10
  (49 shorter events, 15.4 us)
Async XLA Ops:
  7.2 116.7 %copy-start = (bf16[1,1,192,4096]{3,2,1,0:T(8,128)(2,1)S(1)}, bf16[1,1,192,4096]{3,2,1,0:T(8,128)(2,1)}, u32[]{:S(2)}) copy-start(bf16[1,1,192,4096]{3,2,1,0:T(8,128)(2,1)} %param.11) | copy-start | bytes 4718596
  7.2 111.7 %all-gather.5.cloned.1.call-start = ((), (), s32[]{:S(2)}) async-start(), calls=%async_computation.4 | async-start | bytes 6553600 | tf_op jit(solution)/shard_map/all_gather | solution.py:57
  59.1 3.5 copy-start.3
  62.5 118.9 %all-gather.7.cloned.1.call-start = ((), (), s32[]{:S(2)}) async-start(), calls=%async_computation.5 | async-start | bytes 6553600 | tf_op jit(solution)/shard_map/all_gather | solution.py:60
  62.6 0.5 copy-start.5
  105.4 145.9 %reduce-scatter.2.cloned.1.call-start = ((), (), s32[]{:S(2)}) async-start(), calls=%async_computation.6 | async-start | bytes 6553600 | tf_op jit(solution)/shard_map/reduce_scatter | solution.py:97
  118.9 5.0 %copy-start.1 = (bf16[640,4096]{1,0:T(8,128)(2,1)S(1)}, bf16[640,4096]{1,0:T(8,128)(2,1)}, u32[]{:S(2)}) copy-start(bf16[640,4096]{1,0:T(8,128)(2,1)} %all-gather.5.cloned.1.call-done) | copy-start | bytes 15728644
  187.0 1.6 copy-start.2
  254.7 113.2 %all-to-all-start.2 = ((bf16[16,40,1024]{2,1,0:T(8,128)(2,1)}), bf16[16,40,1024]{2,1,0:T(8,128)(2,1)S(1)}, u32[]{:S(2)}, u32[]{:S(2)}) async-start(bf16[16,40,1024]{2,1,0:T(8,128)(2,1)} %reshape.81), calls=%async_computation.3 | async-start | bytes 2621440 | tf_op jit(solution)/shard_map/all_to_all | solution.py:98
  367.9 4.9 %copy-start.6 = (bf16[128]{0:T(256)(128)(2,1)S(1)}, bf16[128]{0:T(256)(128)(2,1)}, u32[]{:S(2)}) copy-start(bf16[128]{0:T(256)(128)(2,1)} %copy-done.5) | copy-start | bytes 772
  367.9 4.9 %copy-start.4 = (f32[8]{0:T(128)S(1)}, f32[8]{0:T(128)}, u32[]{:S(2)}) copy-start(f32[8]{0:T(128)} %compare_convert_fusion) | copy-start | bytes 100
  369.6 9.1 %slice-start = ((s8[5242880]{0:T(1024)(128)(4,1)}), s8[4194304]{0:T(1024)(128)(4,1)S(1)}, s32[]{:S(2)}) async-start(s8[5242880]{0:T(1024)(128)(4,1)} %bitcast.58), calls=%async_computation.7 | async-start | bytes 8388608
  371.5 25.9 %collective-permute-start = (bf16[128,4096]{1,0:T(8,128)(2,1)S(1)}, bf16[128,4096]{1,0:T(8,128)(2,1)S(1)}, u32[]{:S(2)}, u32[]{:S(2)}) collective-permute-start(bf16[128,4096]{1,0:T(8,128)(2,1)S(1)} %convolution_convert_fusion.5), channel_id=1, source_target_pairs={{64,0},{128,64},{192,128},{65,1},{129,65},{193,129},{66,2},{130,66... | collective-permute-start | bytes 3145736 | tf_op jit(solution)/shard_map/ppermute | solution.py:10
  373.5 5.1 %slice-start.1 = ((s8[5242880]{0:T(1024)(128)(4,1)}), s8[1048576]{0:T(1024)(128)(4,1)S(1)}, s32[]{:S(2)}) async-start(s8[5242880]{0:T(1024)(128)(4,1)} %bitcast.58), calls=%async_computation.8 | async-start | bytes 2097152
Sparse Core Ops, SparseCore 0:
  62.6 56.2 all-gather.4
  121.3 60.0 all-gather.6
  192.7 58.5 reduce-scatter.1

commit v3 on v2

--- a/solution.py
+++ b/solution.py
@@ -52,54 +52,83 @@
     local_dy = lax.dot_general(
         table_half, scaled, token_contract, preferred_element_type=jnp.float32
     ).astype(jnp.bfloat16)
-    x_e = lax.all_to_all(dense_chunks(local_x, experts), "expert", 0, 0, tiled=True)
-    x_e = x_e.reshape(experts * capacity, model_width)
-    rows_x = lax.all_gather(x_e, "dp", axis=0, tiled=True)
-    dy_e = lax.all_to_all(dense_chunks(local_dy, experts), "expert", 0, 0, tiled=True)
-    dy_e = dy_e.reshape(experts * capacity, model_width)
-    rows_grad = lax.all_gather(dy_e, "dp", axis=0, tiled=True)
-    gate_pre = lax.dot_general(
-        rows_x, gate_mat, feature_contract, preferred_element_type=jnp.float32
-    )
-    up_pre = lax.dot_general(rows_x, up_mat, feature_contract, preferred_element_type=jnp.float32)
+    pieces = 2
+    width = model_width // pieces
+    rows_x = []
+    rows_grad = []
+    for q in range(pieces):
+        cols = slice(q * width, (q + 1) * width)
+        x_e = lax.all_to_all(dense_chunks(local_x[:, cols], experts), "expert", 0, 0, tiled=True)
+        x_e = x_e.reshape(experts * capacity, width)
+        rows_x.append(lax.all_gather(x_e, "dp", axis=0, tiled=True))
+    for q in range(pieces):
+        cols = slice(q * width, (q + 1) * width)
+        dy_e = lax.all_to_all(dense_chunks(local_dy[:, cols], experts), "expert", 0, 0, tiled=True)
+        dy_e = dy_e.reshape(experts * capacity, width)
+        rows_grad.append(lax.all_gather(dy_e, "dp", axis=0, tiled=True))
+    gate_pre = 0.0
+    up_pre = 0.0
+    for q in range(pieces):
+        cols = slice(q * width, (q + 1) * width)
+        gate_pre = gate_pre + lax.dot_general(
+            rows_x[q], gate_mat[:, cols], feature_contract, preferred_element_type=jnp.float32
+        )
+        up_pre = up_pre + lax.dot_general(
+            rows_x[q], up_mat[:, cols], feature_contract, preferred_element_type=jnp.float32
+        )
     gate_sig = jax.nn.sigmoid(gate_pre)
     activated = (gate_pre * gate_sig * up_pre).astype(jnp.bfloat16)
-    partial_out = jnp.dot(activated, down_mat, preferred_element_type=jnp.float32)
-    row_score = jnp.sum(partial_out * rows_grad.astype(jnp.float32), axis=1)
-    all_scores = lax.all_gather(row_score, ("expert", "dp"), axis=0, tiled=False)
-    all_scores = jnp.sum(all_scores.reshape(experts, groups, -1), axis=1)
-    all_scores = all_scores.reshape(experts, groups, experts, capacity)
-    mine = lax.dynamic_index_in_dim(all_scores, my_group, axis=1, keepdims=False)
-    mine = lax.dynamic_index_in_dim(mine, my_expert, axis=1, keepdims=False)
-    slot_score = mine.reshape(-1)
-    picked = jnp.sum(jnp.where(table, slot_score[None, :], jnp.float32(0.0)), axis=1)
+    row_score = 0.0
+    hidden_grad = 0.0
+    for q in range(pieces):
+        cols = slice(q * width, (q + 1) * width)
+        partial_out = jnp.dot(activated, down_mat[:, cols], preferred_element_type=jnp.float32)
+        row_score = row_score + jnp.sum(partial_out * rows_grad[q].astype(jnp.float32), axis=1)
+        hidden_grad = hidden_grad + lax.dot_general(
+            rows_grad[q], down_mat[:, cols], feature_contract, preferred_element_type=jnp.float32
+        )
+    row_score = lax.psum(row_score, "dp").reshape(groups, experts * capacity)
+    row_score = lax.dynamic_index_in_dim(row_score, my_group, axis=0, keepdims=False)
+    all_scores = lax.all_gather(row_score, "expert", axis=0, tiled=True)
+    all_scores = all_scores.reshape(experts, experts, capacity)
+    slot_score = lax.dynamic_index_in_dim(all_scores, my_expert, axis=1, keepdims=False)
+    picked = jnp.sum(jnp.where(table, slot_score.reshape(-1)[None, :], jnp.float32(0.0)), axis=1)
     gate_grad = picked / gate
     is_first = (jnp.arange(score_rows.shape[1]) == 0).astype(jnp.float32)
     score_grad = gate_grad[:, None] * weights[:, 0:1] * (is_first - weights)
-    hidden_grad = lax.dot_general(
-        rows_grad, down_mat, feature_contract, preferred_element_type=jnp.float32
-    )
     pre_gate = (hidden_grad * up_pre * gate_sig * (1.0 + gate_pre * (1.0 - gate_sig))).astype(
         jnp.bfloat16
     )
     pre_up = (hidden_grad * gate_pre * gate_sig).astype(jnp.bfloat16)
-    grad_down = lax.dot_general(
-        activated, rows_grad, token_contract, preferred_element_type=jnp.float32
-    ).astype(jnp.bfloat16)
-    grad_gate = lax.dot_general(
-        pre_gate, rows_x, token_contract, preferred_element_type=jnp.float32
-    ).astype(jnp.bfloat16)
-    grad_up = lax.dot_general(
-        pre_up, rows_x, token_contract, preferred_element_type=jnp.float32
-    ).astype(jnp.bfloat16)
-    partial_in = jnp.dot(pre_gate, gate_mat, preferred_element_type=jnp.float32)
-    partial_in = partial_in + jnp.dot(pre_up, up_mat, preferred_element_type=jnp.float32)
-    summed = lax.psum_scatter(partial_in.astype(jnp.bfloat16), "dp", scatter_dimension=0, tiled=True)
-    back = lax.all_to_all(dense_chunks(summed, experts), "expert", 0, 0, tiled=True)
-    flat_in = back.reshape(experts * capacity, model_width)
-    input_grad = jnp.dot(table_half, flat_in, preferred_element_type=jnp.float32).astype(
-        jnp.bfloat16
-    )
+    grad_down = []
+    grad_gate = []
+    grad_up = []
+    grads_in = []
+    for q in range(pieces):
+        cols = slice(q * width, (q + 1) * width)
+        grad_down.append(lax.dot_general(
+            activated, rows_grad[q], token_contract, preferred_element_type=jnp.float32
+        ).astype(jnp.bfloat16))
+        grad_gate.append(lax.dot_general(
+            pre_gate, rows_x[q], token_contract, preferred_element_type=jnp.float32
+        ).astype(jnp.bfloat16))
+        grad_up.append(lax.dot_general(
+            pre_up, rows_x[q], token_contract, preferred_element_type=jnp.float32
+        ).astype(jnp.bfloat16))
+        partial_in = jnp.dot(pre_gate, gate_mat[:, cols], preferred_element_type=jnp.float32)
+        partial_in = partial_in + jnp.dot(pre_up, up_mat[:, cols], preferred_element_type=jnp.float32)
+        summed = lax.psum_scatter(
+            partial_in.astype(jnp.bfloat16), "dp", scatter_dimension=0, tiled=True
+        )
+        back = lax.all_to_all(dense_chunks(summed, experts), "expert", 0, 0, tiled=True)
+        flat_in = back.reshape(experts * capacity, width)
+        grads_in.append(jnp.dot(table_half, flat_in, preferred_element_type=jnp.float32).astype(
+            jnp.bfloat16
+        ))
+    grad_down = jnp.concatenate(grad_down, axis=1)
+    grad_gate = jnp.concatenate(grad_gate, axis=1)
+    grad_up = jnp.concatenate(grad_up, axis=1)
+    input_grad = jnp.concatenate(grads_in, axis=1)
     handed = from_behind(input_grad, "pipe", -1)
     return (
         score_grad[None],

time: 406 us -> 376 us (0.926)
  waiting for transfers between devices: 144 us -> 107 us
  starting transfers between devices: 9.04 us -> 15.6 us
  blocking collectives: 171 us -> 166 us
  matrix products: 42.2 us -> 47.1 us
    all_gather x1 -> x0, blocking collectives: 89.3 us -> none  [per_device(): lax.all_gather(row_score, ('expert', 'dp'), axis=0, tiled=False)]
    reduce_scatter x1 -> x2, waiting for transfers between devices: 58.7 us -> 0.01 us  [per_device(): lax.psum_scatter(partial_in.astype(jnp.bfloat16), 'dp', scatter_dimension...]
    unnamed x0 -> x1, blocking collectives: none -> 48.5 us
    all_to_all x1 -> x2, waiting for transfers between devices: 0.01 us -> 28.9 us  [per_device(): lax.all_to_all(dense_chunks(summed, experts), 'expert', 0, 0, tiled=True)]
    all_to_all x2 -> x4, blocking collectives: 81.2 us -> 110 us  [the longest x2 58.3 us: per_device(): lax.all_to_all(dense_chunks(local_x[:, cols], experts), 'expert', 0, 0, t...]
    all_gather x2 -> x4, waiting for transfers between devices: 69 us -> 57.2 us  [the longest x2 34.3 us: per_device(): rows_grad.append(lax.all_gather(dy_e, 'dp', axis=0, tiled=True))]
    dot_general x9 -> x18, matrix products: 35.7 us -> 45.3 us  [the longest x2 7.9 us: per_device(): lax.dot_general(rows_x[q], up_mat[:, cols], feature_contract, preferred_e...]
    psum x0 -> x1, blocking collectives: none -> 7.39 us  [per_device(): row_score = lax.psum(row_score, 'dp').reshape(groups, experts * capacity)]
  transfers between devices with their start and end apart: 5 -> 9, of which waited for: 4 -> 5; matrix products, arithmetic and copies ran while one was open for 9% -> 15% of each run, Pallas kernels for 0% -> 0%
where the time goes in v3:
time: 376 us; the launch traced here: 375 us
  blocking collectives  166 us (44%)
  waiting for transfers between devices  107 us (28%)
  matrix products  47.1 us (13%)
  local copies, waits for them, and re-layouts  17.4 us (5%)
  starting transfers between devices  15.6 us (4%)
  between operations  15.2 us (4%)
  other arithmetic  7.13 us (2%)
    all_to_all x2, blocking collectives, per_device(): lax.all_to_all(dense_chunks(local_x[:, cols], experts), 'expert', 0, 0, t...  58.3 us
    all_to_all x2, blocking collectives, per_device(): lax.all_to_all(dense_chunks(local_dy[:, cols], experts), 'expert', 0, 0,...  51.3 us
    unnamed x1, blocking collectives  48.5 us
    all_gather x2, waiting for transfers between devices, per_device(): rows_grad.append(lax.all_gather(dy_e, 'dp', axis=0, tiled=True))  34.3 us
    all_to_all x2, waiting for transfers between devices, per_device(): lax.all_to_all(dense_chunks(summed, experts), 'expert', 0, 0, tiled=True)  28.9 us
    all_gather x2, waiting for transfers between devices, per_device(): rows_x.append(lax.all_gather(x_e, 'dp', axis=0, tiled=True))  22.9 us
    ppermute x1, waiting for transfers between devices, from_behind(): return lax.ppermute(shard, axis, pairs)  21.1 us
    all_to_all x2, starting transfers between devices, per_device(): lax.all_to_all(dense_chunks(summed, experts), 'expert', 0, 0, tiled=True)  13.7 us
  transfers between devices with their start and end apart: 9, of which 5 were waited for; matrix products, arithmetic and copies ran while one was open for 15% of the time, Pallas kernels for 0%

profile of v3, /device:TPU:1, one launch (start us, length us, event | category | flops | bytes accessed | tf_op | source)
XLA Modules:
  0.0 375.1 jit_solution(8144769554985618803)
XLA Ops:
  10.6 32.7 %all_to_all.30 = bf16[16,20,1024]{2,1,0:T(8,128)(2,1)S(1)} all-to-all(bf16[16,20,1024]{2,1,0:T(8,128)(2,1)S(1)} %reshape.91), channel_id=1, replica_groups=mesh['pipe'=4,'expert'=16,'dp'=4] {'expert'}, dimensions={0} | all-to-all | bytes 1310720 | tf_op jit(solution)/shard_map/all_to_all | solution.py:61
  45.6 25.6 %all_to_all.31 = bf16[16,20,1024]{2,1,0:T(8,128)(2,1)S(1)} all-to-all(bf16[16,20,1024]{2,1,0:T(8,128)(2,1)S(1)} %reshape.95), channel_id=1, replica_groups=mesh['pipe'=4,'expert'=16,'dp'=4] {'expert'}, dimensions={0} | all-to-all | bytes 1310720 | tf_op jit(solution)/shard_map/all_to_all | solution.py:66
  72.8 25.6 %all_to_all.32 = bf16[16,20,1024]{2,1,0:T(8,128)(2,1)S(1)} all-to-all(bf16[16,20,1024]{2,1,0:T(8,128)(2,1)S(1)} %reshape.93), channel_id=1, replica_groups=mesh['pipe'=4,'expert'=16,'dp'=4] {'expert'}, dimensions={0} | all-to-all | bytes 1310720 | tf_op jit(solution)/shard_map/all_to_all | solution.py:61
  99.9 25.6 %all_to_all.33 = bf16[16,20,1024]{2,1,0:T(8,128)(2,1)S(1)} all-to-all(bf16[16,20,1024]{2,1,0:T(8,128)(2,1)S(1)} %reshape.97), channel_id=1, replica_groups=mesh['pipe'=4,'expert'=16,'dp'=4] {'expert'}, dimensions={0} | all-to-all | bytes 1310720 | tf_op jit(solution)/shard_map/all_to_all | solution.py:66
  126.8 3.9 %fusion.13 = f32[640,192]{0,1:T(8,128)} fusion(bf16[640,2048]{1,0:T(8,128)(2,1)} %all-gather.6.cloned.1.call-done, bf16[192,4096]{1,0:T(8,128)(2,1)} %bitcast.63), kind=kOutput, calls=%fused_computation.34 | convolution fusion | flops 503316480 | bytes 3899392 | tf_op jit(solution)/shard_map/dot_general | solution.py:76
  130.7 2.1 fusion.20
  132.8 4.0 %fusion.7 = f32[640,192]{0,1:T(8,128)} fusion(bf16[640,2048]{1,0:T(8,128)(2,1)} %all-gather.10.cloned.1.call-done, bf16[192,4096]{1,0:T(8,128)(2,1)} %bitcast.71), kind=kOutput, calls=%fused_computation.28 | convolution fusion | flops 503316480 | bytes 3899392 | tf_op jit(solution)/shard_map/dot_general | solution.py:87
  136.8 22.9 %all-gather.8.cloned.1.call-done = bf16[640,2048]{1,0:T(8,128)(2,1)} async-done(((bf16[160,2048]{1,0:T(8,128)(2,1)}), bf16[640,2048]{1,0:T(8,128)(2,1)}) %all-gather.8.cloned.1.call-update) | async-done | bytes 2621456 | tf_op jit(solution)/shard_map/all_gather | solution.py:63
  159.8 4.0 %convolution_add_fusion.1 = f32[640,192]{0,1:T(8,128)} fusion(f32[640,192]{0,1:T(8,128)} %fusion.13, bf16[640,2048]{1,0:T(8,128)(2,1)} %all-gather.8.cloned.1.call-done, bf16[192,4096]{1,0:T(8,128)(2,1)} %bitcast.64), kind=kOutput, calls=%fused_computation.20 | convolution fusion | flops 503439360 | bytes 4390912 | tf_op jit(solution)/shard_map/dot_general | solution.py:76
  165.7 34.3 %all-gather.12.cloned.1.call-done = bf16[640,2048]{1,0:T(8,128)(2,1)} async-done(((bf16[160,2048]{1,0:T(8,128)(2,1)}), bf16[640,2048]{1,0:T(8,128)(2,1)}) %all-gather.12.cloned.1.call-update) | async-done | bytes 2621456 | tf_op jit(solution)/shard_map/all_gather | solution.py:68
  199.9 3.7 multiply_convert_fusion
  205.0 2.5 add_convert_fusion
  209.9 2.4 add_convert_fusion.1
  214.2 3.1 multiply_reduce_fusion
  218.5 7.4 %psum.7 = f32[4,160]{1,0:T(4,128)S(1)} all-reduce(f32[4,160]{1,0:T(4,128)S(1)} %reshape.99), channel_id=1, replica_groups=mesh['pipe'=4,'expert'=16,'dp'=4] {'dp'}, use_global_device_ids=true, to_apply=%region_5.6 | all-reduce | flops 640 | bytes 5120 | tf_op jit(solution)/shard_map/psum | solution.py:90
  226.3 48.5 %all-reduce.1 = f32[16,16,10]{2,1,0:T(8,128)} all-reduce(f32[16,16,10]{2,1,0:T(8,128)S(1)} %reshape.100), channel_id=2, replica_groups=mesh['pipe'=4,'expert'=16,'dp'=4] {'expert'}, use_global_device_ids=true, to_apply=%add | all-reduce | flops 2560 | bytes 20480
  275.9 3.4 convolution_convert_fusion.2
  279.3 2.1 reshape.103
  281.4 9.6 %all-to-all-start.5 = ((bf16[16,20,1024]{2,1,0:T(8,128)(2,1)}), bf16[16,20,1024]{2,1,0:T(8,128)(2,1)}, u32[]{:S(2)}, u32[]{:S(2)}) async-start(bf16[16,20,1024]{2,1,0:T(8,128)(2,1)} %reshape.103), calls=%async_computation.7 | async-start | bytes 1572864 | tf_op jit(solution)/shard_map/all_to_all | solution.py:123
  291.0 3.7 convolution_convert_fusion.3
  301.9 11.9 %all-to-all-done.5 = bf16[16,20,1024]{2,1,0:T(8,128)(2,1)} async-done(((bf16[16,20,1024]{2,1,0:T(8,128)(2,1)}), bf16[16,20,1024]{2,1,0:T(8,128)(2,1)}, u32[]{:S(2)}, u32[]{:S(2)}) %all-to-all-start.5) | async-done | bytes 655392 | tf_op jit(solution)/shard_map/all_to_all | solution.py:123
  313.8 4.2 %all-to-all-start.4 = ((bf16[16,20,1024]{2,1,0:T(8,128)(2,1)}), bf16[16,20,1024]{2,1,0:T(8,128)(2,1)}, u32[]{:S(2)}, u32[]{:S(2)}) async-start(bf16[16,20,1024]{2,1,0:T(8,128)(2,1)} %reshape.101), calls=%async_computation.5 | async-start | bytes 1572864 | tf_op jit(solution)/shard_map/all_to_all | solution.py:123
  322.7 17.0 %all-to-all-done.4 = bf16[16,20,1024]{2,1,0:T(8,128)(2,1)} async-done(((bf16[16,20,1024]{2,1,0:T(8,128)(2,1)}), bf16[16,20,1024]{2,1,0:T(8,128)(2,1)}, u32[]{:S(2)}, u32[]{:S(2)}) %all-to-all-start.4) | async-done | bytes 655392 | tf_op jit(solution)/shard_map/all_to_all | solution.py:123
  346.2 21.1 %collective-permute-done = bf16[128,4096]{1,0:T(8,128)(2,1)S(1)} collective-permute-done((bf16[128,4096]{1,0:T(8,128)(2,1)S(1)}, bf16[128,4096]{1,0:T(8,128)(2,1)S(1)}, u32[]{:S(2)}, u32[]{:S(2)}) %collective-permute-start) | collective-permute-done | bytes 1048608 | tf_op jit(solution)/shard_map/ppermute | solution.py:10
  (108 shorter events, 38.7 us)
Async XLA Ops:
  7.2 2.6 copy-start
  7.2 119.6 %all-gather.6.cloned.1.call-start = ((), (), s32[]{:S(2)}) async-start(), calls=%async_computation.8 | async-start | bytes 3276800 | tf_op jit(solution)/shard_map/all_gather | solution.py:63
  10.3 34.2 %copy-start.17 = (f32[1,128,8]{1,2,0:T(8,128)S(1)}, f32[1,128,8]{1,2,0:T(8,128)}, u32[]{:S(2)}) copy-start(f32[1,128,8]{1,2,0:T(8,128)} %param.9) | copy-start | bytes 12292
  10.3 34.3 %copy-start.16 = (bf16[1,128,4096]{2,1,0:T(8,128)(2,1)S(1)}, bf16[1,128,4096]{2,1,0:T(8,128)(2,1)}, u32[]{:S(2)}) copy-start(bf16[1,128,4096]{2,1,0:T(8,128)(2,1)} %param.10) | copy-start | bytes 3145732
  44.5 88.3 %all-gather.10.cloned.1.call-start = ((), (), s32[]{:S(2)}) async-start(), calls=%async_computation.10 | async-start | bytes 3276800 | tf_op jit(solution)/shard_map/all_gather | solution.py:68
  72.4 87.3 %all-gather.8.cloned.1.call-start = ((), (), s32[]{:S(2)}) async-start(), calls=%async_computation.9 | async-start | bytes 3276800 | tf_op jit(solution)/shard_map/all_gather | solution.py:63
  99.6 100.4 %all-gather.12.cloned.1.call-start = ((), (), s32[]{:S(2)}) async-start(), calls=%async_computation.11 | async-start | bytes 3276800 | tf_op jit(solution)/shard_map/all_gather | solution.py:68
  126.7 152.6 %reduce-scatter.5.cloned.1.call-start = ((), (), s32[]{:S(2)}) async-start(), calls=%async_computation.13 | async-start | bytes 3276800 | tf_op jit(solution)/shard_map/reduce_scatter | solution.py:120
  126.8 3.9 %copy-start.2 = (bf16[640,2048]{1,0:T(8,128)(2,1)S(1)}, bf16[640,2048]{1,0:T(8,128)(2,1)}, u32[]{:S(2)}) copy-start(bf16[640,2048]{1,0:T(8,128)(2,1)} %all-gather.6.cloned.1.call-done) | copy-start | bytes 7864324
  159.8 4.0 %copy-start.3 = (bf16[640,2048]{1,0:T(8,128)(2,1)S(1)}, bf16[640,2048]{1,0:T(8,128)(2,1)}, u32[]{:S(2)}) copy-start(bf16[640,2048]{1,0:T(8,128)(2,1)} %all-gather.8.cloned.1.call-done) | copy-start | bytes 7864324
  159.8 4.0 %copy-start.12 = (bf16[1,1,192,4096]{3,2,1,0:T(8,128)(2,1)S(1)}, bf16[1,1,192,4096]{3,2,1,0:T(8,128)(2,1)}, u32[]{:S(2)}) copy-start(bf16[1,1,192,4096]{3,2,1,0:T(8,128)(2,1)} %param.11) | copy-start | bytes 4718596
  199.9 3.7 copy-start.13
  207.5 92.2 %reduce-scatter.3.cloned.1.call-start = ((), (), s32[]{:S(2)}) async-start(), calls=%async_computation.12 | async-start | bytes 3276800 | tf_op jit(solution)/shard_map/reduce_scatter | solution.py:120
  214.2 3.1 copy-start.11
  214.2 3.2 copy-start.18
  281.4 32.3 %all-to-all-start.5 = ((bf16[16,20,1024]{2,1,0:T(8,128)(2,1)}), bf16[16,20,1024]{2,1,0:T(8,128)(2,1)}, u32[]{:S(2)}, u32[]{:S(2)}) async-start(bf16[16,20,1024]{2,1,0:T(8,128)(2,1)} %reshape.103), calls=%async_computation.7 | async-start | bytes 1572864 | tf_op jit(solution)/shard_map/all_to_all | solution.py:123
  291.0 3.7 copy-start.4
  313.8 25.9 %all-to-all-start.4 = ((bf16[16,20,1024]{2,1,0:T(8,128)(2,1)}), bf16[16,20,1024]{2,1,0:T(8,128)(2,1)}, u32[]{:S(2)}, u32[]{:S(2)}) async-start(bf16[16,20,1024]{2,1,0:T(8,128)(2,1)} %reshape.101), calls=%async_computation.5 | async-start | bytes 1572864 | tf_op jit(solution)/shard_map/all_to_all | solution.py:123
  322.7 21.0 %copy-start.7 = (bf16[192,2048]{1,0:T(8,128)(2,1)S(1)}, bf16[192,2048]{1,0:T(8,128)(2,1)}, u32[]{:S(2)}) copy-start(bf16[192,2048]{1,0:T(8,128)(2,1)} %convolution_convert_fusion.6) | copy-start | bytes 2359300
  322.7 21.0 %copy-start.10 = (bf16[192,2048]{1,0:T(8,128)(2,1)S(1)}, bf16[192,2048]{1,0:T(8,128)(2,1)}, u32[]{:S(2)}) copy-start(bf16[192,2048]{1,0:T(8,128)(2,1)} %convolution_convert_fusion.7) | copy-start | bytes 2359300
  341.5 3.5 copy-start.5
  341.5 3.5 copy-start.6
  341.6 25.7 %collective-permute-start = (bf16[128,4096]{1,0:T(8,128)(2,1)S(1)}, bf16[128,4096]{1,0:T(8,128)(2,1)S(1)}, u32[]{:S(2)}, u32[]{:S(2)}) collective-permute-start(bf16[128,4096]{1,0:T(8,128)(2,1)S(1)} %pad_maximum_fusion), channel_id=1, source_target_pairs={{64,0},{128,64},{192,128},{65,1},{129,65},{193,129},{66,2},{130,66... | collective-permute-start | bytes 3145736 | tf_op jit(solution)/shard_map/ppermute | solution.py:10
  343.7 24.6 %copy-start.1 = (bf16[1,128,4096]{2,1,0:T(8,128)(2,1)S(1)}, bf16[1,128,4096]{2,1,0:T(8,128)(2,1)}, u32[]{:S(2)}) copy-start(bf16[1,128,4096]{2,1,0:T(8,128)(2,1)} %param.7) | copy-start | bytes 3145732
  (5 other events, 7.6 us)
Sparse Core Ops, SparseCore 0:
  44.6 34.4 all-gather.5
  81.5 37.8 all-gather.9
  121.8 37.8 all-gather.7
  162.0 37.8 all-gather.11
  207.6 36.8 reduce-scatter.4
  246.9 36.1 reduce-scatter.2

commit v4 on v3

--- a/solution.py
+++ b/solution.py
@@ -52,7 +52,7 @@
     local_dy = lax.dot_general(
         table_half, scaled, token_contract, preferred_element_type=jnp.float32
     ).astype(jnp.bfloat16)
-    pieces = 2
+    pieces = 1
     width = model_width // pieces
     rows_x = []
     rows_grad = []
@@ -87,11 +87,11 @@
         hidden_grad = hidden_grad + lax.dot_general(
             rows_grad[q], down_mat[:, cols], feature_contract, preferred_element_type=jnp.float32
         )
-    row_score = lax.psum(row_score, "dp").reshape(groups, experts * capacity)
-    row_score = lax.dynamic_index_in_dim(row_score, my_group, axis=0, keepdims=False)
-    all_scores = lax.all_gather(row_score, "expert", axis=0, tiled=True)
-    all_scores = all_scores.reshape(experts, experts, capacity)
-    slot_score = lax.dynamic_index_in_dim(all_scores, my_expert, axis=1, keepdims=False)
+    row_score = row_score.reshape(groups, experts, 1, capacity)
+    onehot_e = (jnp.arange(experts) == my_expert).astype(jnp.float32)
+    spread = row_score * onehot_e[None, None, :, None]
+    spread = jnp.swapaxes(spread, 0, 1).reshape(experts * groups, experts, capacity)
+    slot_score = lax.psum_scatter(spread, ("expert", "dp"), scatter_dimension=0, tiled=True)
     picked = jnp.sum(jnp.where(table, slot_score.reshape(-1)[None, :], jnp.float32(0.0)), axis=1)
     gate_grad = picked / gate
     is_first = (jnp.arange(score_rows.shape[1]) == 0).astype(jnp.float32)

time: 376 us -> 417 us (1.11)
  waiting for transfers between devices: 107 us -> 244 us
  blocking collectives: 166 us -> 81.2 us
  starting transfers between devices: 15.6 us -> 9.23 us
  matrix products: 47.1 us -> 42.2 us
    reduce_scatter x0 -> x1, waiting for transfers between devices: none -> 93.3 us  [per_device(): lax.psum_scatter(spread, ('expert', 'dp'), scatter_dimension=0, tiled=True)]
    reduce_scatter x2 -> x1, waiting for transfers between devices: 0.01 us -> 58.7 us  [per_device(): lax.psum_scatter(partial_in.astype(jnp.bfloat16), 'dp', scatter_dimension...]
    unnamed x1 -> x0, blocking collectives: 48.5 us -> none
    all_gather x2 -> x1, waiting for transfers between devices: 34.3 us -> 55.5 us  [per_device(): rows_grad.append(lax.all_gather(dy_e, 'dp', axis=0, tiled=True))]
    ppermute x1, waiting for transfers between devices: 21.1 us -> 0.01 us  [from_behind(): return lax.ppermute(shard, axis, pairs)]
    all_to_all x2 -> x1, blocking collectives: 58.3 us -> 44.1 us  [per_device(): lax.all_to_all(dense_chunks(local_x[:, cols], experts), 'expert', 0, 0, t...]
    all_to_all x2 -> x1, blocking collectives: 51.3 us -> 37.1 us  [per_device(): lax.all_to_all(dense_chunks(local_dy[:, cols], experts), 'expert', 0, 0,...]
    all_gather x2 -> x1, waiting for transfers between devices: 22.9 us -> 14 us  [per_device(): rows_x.append(lax.all_gather(x_e, 'dp', axis=0, tiled=True))]
  transfers between devices with their start and end apart: 9 -> 6, of which waited for: 5 -> 5; matrix products, arithmetic and copies ran while one was open for 15% -> 9% of each run, Pallas kernels for 0% -> 0%
where the time goes in v4:
time: 417 us; the launch traced here: 412 us
  waiting for transfers between devices  244 us (59%)
  blocking collectives  81.2 us (19%)
  matrix products  42.2 us (10%)
  local copies, waits for them, and re-layouts  17.4 us (4%)
  between operations  13.9 us (3%)
  starting transfers between devices  9.23 us (2%)
  other arithmetic  4.24 us (1%)
    reduce_scatter x1, waiting for transfers between devices, per_device(): lax.psum_scatter(spread, ('expert', 'dp'), scatter_dimension=0, tiled=True)  93.3 us
    reduce_scatter x1, waiting for transfers between devices, per_device(): lax.psum_scatter(partial_in.astype(jnp.bfloat16), 'dp', scatter_dimension...  58.7 us
    all_gather x1, waiting for transfers between devices, per_device(): rows_grad.append(lax.all_gather(dy_e, 'dp', axis=0, tiled=True))  55.5 us
    all_to_all x1, blocking collectives, per_device(): lax.all_to_all(dense_chunks(local_x[:, cols], experts), 'expert', 0, 0, t...  44.1 us
    all_to_all x1, blocking collectives, per_device(): lax.all_to_all(dense_chunks(local_dy[:, cols], experts), 'expert', 0, 0,...  37.1 us
    all_to_all x1, waiting for transfers between devices, per_device(): lax.all_to_all(dense_chunks(summed, experts), 'expert', 0, 0, tiled=True)  22.2 us
    all_gather x1, waiting for transfers between devices, per_device(): rows_x.append(lax.all_gather(x_e, 'dp', axis=0, tiled=True))  14 us
  transfers between devices with their start and end apart: 6, of which 5 were waited for; matrix products, arithmetic and copies ran while one was open for 9% of the time, Pallas kernels for 0%

profile of v4, /device:TPU:1, one launch (start us, length us, event | category | flops | bytes accessed | tf_op | source)
XLA Modules:
  0.0 412.0 jit_solution(12123131402447223506)
XLA Ops:
  9.8 2.8 convolution_convert_fusion.4
  12.5 2.5 reshape.75
  15.0 44.1 %all_to_all.15 = bf16[16,40,1024]{2,1,0:T(8,128)(2,1)} all-to-all(bf16[16,40,1024]{2,1,0:T(8,128)(2,1)S(1)} %reshape.75), channel_id=1, replica_groups=mesh['pipe'=4,'expert'=16,'dp'=4] {'expert'}, dimensions={0} | all-to-all | bytes 2621440 | tf_op jit(solution)/shard_map/all_to_all | solution.py:61
  59.1 3.4 reshape.76
  62.6 1.8 convolution_convert_fusion.3
  64.4 1.6 reshape.77
  66.1 37.1 %all_to_all.16 = bf16[16,40,1024]{2,1,0:T(8,128)(2,1)S(1)} all-to-all(bf16[16,40,1024]{2,1,0:T(8,128)(2,1)} %reshape.77), channel_id=1, replica_groups=mesh['pipe'=4,'expert'=16,'dp'=4] {'expert'}, dimensions={0} | all-to-all | bytes 2621440 | tf_op jit(solution)/shard_map/all_to_all | solution.py:66
  104.9 14.0 %all-gather.3.cloned.1.call-done = bf16[640,4096]{1,0:T(8,128)(2,1)} async-done(((bf16[160,4096]{1,0:T(8,128)(2,1)}), bf16[640,4096]{1,0:T(8,128)(2,1)}) %all-gather.3.cloned.1.call-update) | async-done | bytes 5242896 | tf_op jit(solution)/shard_map/all_gather | solution.py:63
  118.9 5.0 %fusion.8 = f32[640,192]{0,1:T(8,128)S(1)} fusion(bf16[640,4096]{1,0:T(8,128)(2,1)} %all-gather.3.cloned.1.call-done, bf16[1,1,192,4096]{3,2,1,0:T(8,128)(2,1)} %param.12), kind=kOutput, calls=%fused_computation.17 | convolution fusion | flops 1006632960 | bytes 7307264 | tf_op jit(solution)/shard_map/dot_general | solution.py:76
  123.9 1.9 fusion.12
  125.9 55.5 %all-gather.5.cloned.1.call-done = bf16[640,4096]{1,0:T(8,128)(2,1)} async-done(((bf16[160,4096]{1,0:T(8,128)(2,1)}), bf16[640,4096]{1,0:T(8,128)(2,1)}) %all-gather.5.cloned.1.call-update) | async-done | bytes 5242896 | tf_op jit(solution)/shard_map/all_gather | solution.py:68
  181.4 5.6 %multiply_convert_fusion = (bf16[640,192]{0,1:T(8,128)(2,1)S(1)}, bf16[640,192]{0,1:T(8,128)(2,1)S(1)}, bf16[640,192]{0,1:T(8,128)(2,1)}) fusion(f32[640,192]{0,1:T(8,128)S(1)} %fusion.12, f32[640,192]{0,1:T(8,128)S(1)} %fusion.8, bf16[640,4096]{1,0:T(8,128)(2,1)} %all-gather.5.cloned.1.call-done, bf16[1,1,192,4096]{3,2,1,0:T(8,128)(2,1)} %param.13), kind=kOutput, calls=%fused_computation.26 | convolution fusion | flops 1008599040 | bytes 8536064 | tf_op jit(solution)/shard_map/dot_general | solution.py:87
  188.6 4.0 add_convert_fusion
  192.6 58.7 %reduce-scatter.5.cloned.1.call-done = bf16[160,4096]{1,0:T(8,128)(2,1)} async-done(((bf16[640,4096]{1,0:T(8,128)(2,1)}), bf16[160,4096]{1,0:T(8,128)(2,1)}) %reduce-scatter.5.cloned.1.call-update) | async-done | bytes 1310736 | tf_op jit(solution)/shard_map/reduce_scatter | solution.py:120
  251.3 3.4 reshape.79
  254.7 7.7 %all-to-all-start.2 = ((bf16[16,40,1024]{2,1,0:T(8,128)(2,1)}), bf16[16,40,1024]{2,1,0:T(8,128)(2,1)S(1)}, u32[]{:S(2)}, u32[]{:S(2)}) async-start(bf16[16,40,1024]{2,1,0:T(8,128)(2,1)} %reshape.79), calls=%async_computation.4 | async-start | bytes 2621440 | tf_op jit(solution)/shard_map/all_to_all | solution.py:123
  262.4 4.7 %multiply_reduce_fusion = f32[640]{0:T(1024)S(1)} fusion(bf16[640,4096]{1,0:T(8,128)(2,1)} %all-gather.5.cloned.1.call-done, bf16[640,192]{0,1:T(8,128)(2,1)} %get-tuple-element.7, bf16[1,1,192,4096]{3,2,1,0:T(8,128)(2,1)} %param.13), kind=kOutput, calls=%fused_computation.1 | convolution fusion | flops 1014496640 | bytes 7064064 | tf_op jit(solution)/shard_map/dot_general | solution.py:85
  268.2 5.2 %fusion.2 = bf16[1,1,192,4096]{3,2,1,0:T(8,128)(2,1)} fusion(bf16[640,192]{0,1:T(8,128)(2,1)} %get-tuple-element.7, bf16[640,4096]{1,0:T(8,128)(2,1)} %all-gather.5.cloned.1.call-done), kind=kOutput, calls=%fused_computation.10 | convolution fusion | flops 1007419392 | bytes 7061504 | tf_op jit(solution)/shard_map/dot_general | solution.py:109
  273.4 22.2 %all-to-all-done.2 = bf16[16,40,1024]{2,1,0:T(8,128)(2,1)S(1)} async-done(((bf16[16,40,1024]{2,1,0:T(8,128)(2,1)}), bf16[16,40,1024]{2,1,0:T(8,128)(2,1)S(1)}, u32[]{:S(2)}, u32[]{:S(2)}) %all-to-all-start.2) | async-done | bytes 1310752 | tf_op jit(solution)/shard_map/all_to_all | solution.py:123
  297.2 2.0 convolution_convert_fusion.5
  300.6 5.1 %fusion.1 = bf16[1,1,192,4096]{3,2,1,0:T(8,128)(2,1)} fusion(bf16[640,192]{0,1:T(8,128)(2,1)S(1)} %get-tuple-element.5, bf16[640,4096]{1,0:T(8,128)(2,1)} %all-gather.3.cloned.1.call-done), kind=kOutput, calls=%fused_computation.9 | convolution fusion | flops 1007419392 | bytes 7061504 | tf_op jit(solution)/shard_map/dot_general | solution.py:115
  305.7 2.6 fusion
  308.2 93.3 %reduce-scatter.3.cloned.1.call-done = f32[1,16,10]{2,1,0:T(8,128)} async-done(((f32[64,16,10]{2,1,0:T(8,128)}), f32[1,16,10]{2,1,0:T(8,128)}) %reduce-scatter.3.cloned.1.call-update) | async-done | bytes 656 | tf_op jit(solution)/shard_map/reduce_scatter | solution.py:94
  403.1 2.3 copy.15
  (43 shorter events, 11.7 us)
Async XLA Ops:
  7.2 116.7 %copy-start = (bf16[1,1,192,4096]{3,2,1,0:T(8,128)(2,1)S(1)}, bf16[1,1,192,4096]{3,2,1,0:T(8,128)(2,1)}, u32[]{:S(2)}) copy-start(bf16[1,1,192,4096]{3,2,1,0:T(8,128)(2,1)} %param.11) | copy-start | bytes 4718596
  7.2 111.7 %all-gather.3.cloned.1.call-start = ((), (), s32[]{:S(2)}) async-start(), calls=%async_computation.5 | async-start | bytes 6553600 | tf_op jit(solution)/shard_map/all_gather | solution.py:63
  59.1 3.5 copy-start.3
  62.5 118.9 %all-gather.5.cloned.1.call-start = ((), (), s32[]{:S(2)}) async-start(), calls=%async_computation.6 | async-start | bytes 6553600 | tf_op jit(solution)/shard_map/all_gather | solution.py:68
  104.9 146.4 %reduce-scatter.5.cloned.1.call-start = ((), (), s32[]{:S(2)}) async-start(), calls=%async_computation.8 | async-start | bytes 6553600 | tf_op jit(solution)/shard_map/reduce_scatter | solution.py:120
  118.9 5.0 %copy-start.1 = (bf16[640,4096]{1,0:T(8,128)(2,1)S(1)}, bf16[640,4096]{1,0:T(8,128)(2,1)}, u32[]{:S(2)}) copy-start(bf16[640,4096]{1,0:T(8,128)(2,1)} %all-gather.3.cloned.1.call-done) | copy-start | bytes 15728644
  187.0 1.6 copy-start.2
  254.7 40.9 %all-to-all-start.2 = ((bf16[16,40,1024]{2,1,0:T(8,128)(2,1)}), bf16[16,40,1024]{2,1,0:T(8,128)(2,1)S(1)}, u32[]{:S(2)}, u32[]{:S(2)}) async-start(bf16[16,40,1024]{2,1,0:T(8,128)(2,1)} %reshape.79), calls=%async_computation.4 | async-start | bytes 2621440 | tf_op jit(solution)/shard_map/all_to_all | solution.py:123
  262.3 139.2 %reduce-scatter.3.cloned.1.call-start = ((), (), s32[]{:S(2)}) async-start(), calls=%async_computation.7 | async-start | bytes 532480 | tf_op jit(solution)/shard_map/reduce_scatter | solution.py:94
  297.2 8.5 %slice-start = ((s8[5242880]{0:T(1024)(128)(4,1)}), s8[4194304]{0:T(1024)(128)(4,1)S(1)}, s32[]{:S(2)}) async-start(s8[5242880]{0:T(1024)(128)(4,1)} %bitcast.60), calls=%async_computation.9 | async-start | bytes 8388608
  299.1 6.5 %slice-start.1 = ((s8[5242880]{0:T(1024)(128)(4,1)}), s8[1048576]{0:T(1024)(128)(4,1)S(1)}, s32[]{:S(2)}) async-start(s8[5242880]{0:T(1024)(128)(4,1)} %bitcast.60), calls=%async_computation.10 | async-start | bytes 2097152
  299.1 104.0 %collective-permute-start = (bf16[128,4096]{1,0:T(8,128)(2,1)S(1)}, bf16[128,4096]{1,0:T(8,128)(2,1)}, u32[]{:S(2)}, u32[]{:S(2)}) collective-permute-start(bf16[128,4096]{1,0:T(8,128)(2,1)S(1)} %convolution_convert_fusion.5), channel_id=1, source_target_pairs={{64,0},{128,64},{192,128},{65,1},{129,65},{193,129},{66,2},{130,66... | collective-permute-start | bytes 3145736 | tf_op jit(solution)/shard_map/ppermute | solution.py:10
Sparse Core Ops, SparseCore 0:
  62.6 56.2 all-gather.2
  121.3 60.0 all-gather.4
  192.7 58.5 reduce-scatter.4
  268.3 133.1 reduce-scatter.2

commit v5 on v4

--- a/solution.py
+++ b/solution.py
@@ -87,15 +87,6 @@
         hidden_grad = hidden_grad + lax.dot_general(
             rows_grad[q], down_mat[:, cols], feature_contract, preferred_element_type=jnp.float32
         )
-    row_score = row_score.reshape(groups, experts, 1, capacity)
-    onehot_e = (jnp.arange(experts) == my_expert).astype(jnp.float32)
-    spread = row_score * onehot_e[None, None, :, None]
-    spread = jnp.swapaxes(spread, 0, 1).reshape(experts * groups, experts, capacity)
-    slot_score = lax.psum_scatter(spread, ("expert", "dp"), scatter_dimension=0, tiled=True)
-    picked = jnp.sum(jnp.where(table, slot_score.reshape(-1)[None, :], jnp.float32(0.0)), axis=1)
-    gate_grad = picked / gate
-    is_first = (jnp.arange(score_rows.shape[1]) == 0).astype(jnp.float32)
-    score_grad = gate_grad[:, None] * weights[:, 0:1] * (is_first - weights)
     pre_gate = (hidden_grad * up_pre * gate_sig * (1.0 + gate_pre * (1.0 - gate_sig))).astype(
         jnp.bfloat16
     )
@@ -117,11 +108,15 @@
         ).astype(jnp.bfloat16))
         partial_in = jnp.dot(pre_gate, gate_mat[:, cols], preferred_element_type=jnp.float32)
         partial_in = partial_in + jnp.dot(pre_up, up_mat[:, cols], preferred_element_type=jnp.float32)
-        summed = lax.psum_scatter(
-            partial_in.astype(jnp.bfloat16), "dp", scatter_dimension=0, tiled=True
-        )
-        back = lax.all_to_all(dense_chunks(summed, experts), "expert", 0, 0, tiled=True)
-        flat_in = back.reshape(experts * capacity, width)
+        score_cols = jnp.pad(row_score[:, None], ((0, 0), (0, 127)))
+        outgoing = jnp.concatenate([partial_in, score_cols], axis=1).astype(jnp.bfloat16)
+        summed = lax.psum_scatter(outgoing, "dp", scatter_dimension=0, tiled=True)
+        body = summed[:, :width].reshape(experts, 8, capacity * width // 8)
+        tail = summed[:, width].reshape(experts, 1, capacity)
+        tail = jnp.pad(tail, ((0, 0), (0, 7), (0, 128 - capacity)))
+        back = lax.all_to_all(jnp.concatenate([body, tail], axis=2), "expert", 0, 0, tiled=True)
+        flat_in = back[:, :, : capacity * width // 8].reshape(experts * capacity, width)
+        slot_score = back[:, 0, capacity * width // 8 : capacity * width // 8 + capacity]
         grads_in.append(jnp.dot(table_half, flat_in, preferred_element_type=jnp.float32).astype(
             jnp.bfloat16
         ))
@@ -129,6 +124,11 @@
     grad_gate = jnp.concatenate(grad_gate, axis=1)
     grad_up = jnp.concatenate(grad_up, axis=1)
     input_grad = jnp.concatenate(grads_in, axis=1)
+    slot_score = slot_score.astype(jnp.float32).reshape(-1)
+    picked = jnp.sum(jnp.where(table, slot_score[None, :], jnp.float32(0.0)), axis=1)
+    gate_grad = picked / gate
+    is_first = (jnp.arange(score_rows.shape[1]) == 0).astype(jnp.float32)
+    score_grad = gate_grad[:, None] * weights[:, 0:1] * (is_first - weights)
     handed = from_behind(input_grad, "pipe", -1)
     return (
         score_grad[None],

time: 417 us -> 341 us (0.82); the launches traced: 412 us -> 341 us
  waiting for transfers between devices: 244 us -> 173 us
  matrix products: 42.2 us -> 37 us
    reduce_scatter x2 -> x1, waiting for transfers between devices: 152 us -> 60 us  [per_device(): summed = lax.psum_scatter(outgoing, 'dp', scatter_dimension=0, tiled=True)]
    ppermute x1, waiting for transfers between devices: 0.01 us -> 18.5 us  [from_behind(): return lax.ppermute(shard, axis, pairs)]
  transfers between devices with their start and end apart: 6 -> 5, of which waited for: 5 -> 5; matrix products, arithmetic and copies ran while one was open for 9% -> 8% of each run, Pallas kernels for 0% -> 0%
where the time goes in v5:
time: 341 us
  waiting for transfers between devices  173 us (51%)
  blocking collectives  81.2 us (24%)
  matrix products  37 us (11%)
  local copies, waits for them, and re-layouts  18 us (5%)
  between operations  14 us (4%)
  starting transfers between devices  9.37 us (3%)
  other arithmetic  8.09 us (2%)
    reduce_scatter x1, waiting for transfers between devices, per_device(): summed = lax.psum_scatter(outgoing, 'dp', scatter_dimension=0, tiled=True)  60 us
    all_gather x1, waiting for transfers between devices, per_device(): rows_grad.append(lax.all_gather(dy_e, 'dp', axis=0, tiled=True))  54.4 us
    all_to_all x1, blocking collectives, per_device(): lax.all_to_all(dense_chunks(local_x[:, cols], experts), 'expert', 0, 0, t...  44.1 us
    all_to_all x1, blocking collectives, per_device(): lax.all_to_all(dense_chunks(local_dy[:, cols], experts), 'expert', 0, 0,...  37.1 us
    all_to_all x1, waiting for transfers between devices, per_device(): lax.all_to_all(jnp.concatenate([body, tail], axis=2), 'expert', 0, 0, til...  26.1 us
    ppermute x1, waiting for transfers between devices, from_behind(): return lax.ppermute(shard, axis, pairs)  18.5 us
    all_gather x1, waiting for transfers between devices, per_device(): rows_x.append(lax.all_gather(x_e, 'dp', axis=0, tiled=True))  13.8 us
    all_to_all x1, starting transfers between devices, per_device(): lax.all_to_all(jnp.concatenate([body, tail], axis=2), 'expert', 0, 0, til...  7.79 us
  transfers between devices with their start and end apart: 5, of which 5 were waited for; matrix products, arithmetic and copies ran while one was open for 8% of the time, Pallas kernels for 0%

profile of v5, /device:TPU:1, one launch (start us, length us, event | category | flops | bytes accessed | tf_op | source)
XLA Modules:
  0.0 340.5 jit_solution(16690009162822666893)
XLA Ops:
  9.8 2.8 convolution_convert_fusion.3
  12.5 2.5 reshape.74
  15.0 44.1 %all_to_all.15 = bf16[16,40,1024]{2,1,0:T(8,128)(2,1)} all-to-all(bf16[16,40,1024]{2,1,0:T(8,128)(2,1)S(1)} %reshape.74), channel_id=1, replica_groups=mesh['pipe'=4,'expert'=16,'dp'=4] {'expert'}, dimensions={0} | all-to-all | bytes 2621440 | tf_op jit(solution)/shard_map/all_to_all | solution.py:61
  59.1 3.4 reshape.75
  62.6 1.8 convolution_convert_fusion.4
  64.4 1.6 reshape.72
  66.1 37.1 %all_to_all.16 = bf16[16,40,1024]{2,1,0:T(8,128)(2,1)S(1)} all-to-all(bf16[16,40,1024]{2,1,0:T(8,128)(2,1)} %reshape.72), channel_id=1, replica_groups=mesh['pipe'=4,'expert'=16,'dp'=4] {'expert'}, dimensions={0} | all-to-all | bytes 2621440 | tf_op jit(solution)/shard_map/all_to_all | solution.py:66
  103.2 1.6 reshape.73
  105.1 13.8 %all-gather.5.cloned.1.call-done = bf16[640,4096]{1,0:T(8,128)(2,1)} async-done(((bf16[160,4096]{1,0:T(8,128)(2,1)}), bf16[640,4096]{1,0:T(8,128)(2,1)}) %all-gather.5.cloned.1.call-update) | async-done | bytes 5242896 | tf_op jit(solution)/shard_map/all_gather | solution.py:63
  118.9 5.3 %fusion.9 = f32[640,192]{0,1:T(8,128)} fusion(bf16[640,4096]{1,0:T(8,128)(2,1)} %all-gather.5.cloned.1.call-done, bf16[1,1,192,4096]{3,2,1,0:T(8,128)(2,1)S(1)} %copy-done), kind=kOutput, calls=%fused_computation.20 | convolution fusion | flops 1006632960 | bytes 7307264 | tf_op jit(solution)/shard_map/dot_general | solution.py:73
  124.2 2.7 fusion.12
  127.0 54.4 %all-gather.3.cloned.1.call-done = bf16[640,4096]{1,0:T(8,128)(2,1)} async-done(((bf16[160,4096]{1,0:T(8,128)(2,1)}), bf16[640,4096]{1,0:T(8,128)(2,1)}) %all-gather.3.cloned.1.call-update) | async-done | bytes 5242896 | tf_op jit(solution)/shard_map/all_gather | solution.py:68
  181.4 5.3 %multiply_convert_fusion.1 = (bf16[640,192]{0,1:T(8,128)(2,1)S(1)}, bf16[640,192]{0,1:T(8,128)(2,1)S(1)}, bf16[640,192]{0,1:T(8,128)(2,1)S(1)}) fusion(f32[640,192]{0,1:T(8,128)} %fusion.9, f32[640,192]{0,1:T(8,128)} %fusion.12, bf16[640,4096]{1,0:T(8,128)(2,1)} %all-gather.3.cloned.1.call-done, bf16[1,1,192,4096]{3,2,1,0:T(8,128)(2,1)} %param.13), kind=kOutput, calls=%fused_computation.33 | convolution fusion | flops 1008599040 | bytes 8536064 | tf_op jit(solution)/shard_map/dot_general | solution.py:87
  186.7 1.7 multiply_reduce_fusion
  190.1 1.6 add_convert_fusion
  191.7 2.8 fusion.1
  194.5 60.0 %reduce-scatter.2.cloned.1.call-done = bf16[160,4224]{1,0:T(8,128)(2,1)} async-done(((bf16[640,4224]{1,0:T(8,128)(2,1)}), bf16[160,4224]{1,0:T(8,128)(2,1)}) %reduce-scatter.2.cloned.1.call-update) | async-done | bytes 1351696 | tf_op jit(solution)/shard_map/reduce_scatter | solution.py:113
  259.5 7.8 %all-to-all-start.2 = ((bf16[16,8,5248]{2,1,0:T(8,128)(2,1)}), bf16[16,8,5248]{2,1,0:T(8,128)(2,1)S(1)}, u32[]{:S(2)}, u32[]{:S(2)}) async-start(bf16[16,8,5248]{2,1,0:T(8,128)(2,1)} %fusion.17), calls=%async_computation.3 | async-start | bytes 2686976 | tf_op jit(solution)/shard_map/all_to_all | solution.py:117
  267.3 5.2 %fusion.4 = bf16[1,1,192,4096]{3,2,1,0:T(8,128)(2,1)} fusion(bf16[640,192]{0,1:T(8,128)(2,1)S(1)} %copy-done.8, bf16[640,4096]{1,0:T(8,128)(2,1)} %all-gather.3.cloned.1.call-done), kind=kOutput, calls=%fused_computation.13 | convolution fusion | flops 1007419392 | bytes 7061504 | tf_op jit(solution)/shard_map/dot_general | solution.py:100
  272.5 2.5 fusion.3
  275.0 26.1 %all-to-all-done.2 = bf16[16,8,5248]{2,1,0:T(8,128)(2,1)S(1)} async-done(((bf16[16,8,5248]{2,1,0:T(8,128)(2,1)}), bf16[16,8,5248]{2,1,0:T(8,128)(2,1)S(1)}, u32[]{:S(2)}, u32[]{:S(2)}) %all-to-all-start.2) | async-done | bytes 1343520 | tf_op jit(solution)/shard_map/all_to_all | solution.py:117
  302.4 2.5 reshape.77
  307.7 5.1 %fusion.2 = bf16[1,1,192,4096]{3,2,1,0:T(8,128)(2,1)} fusion(bf16[640,192]{0,1:T(8,128)(2,1)S(1)} %get-tuple-element.6, bf16[640,4096]{1,0:T(8,128)(2,1)} %all-gather.5.cloned.1.call-done), kind=kOutput, calls=%fused_computation.11 | convolution fusion | flops 1007419392 | bytes 7061504 | tf_op jit(solution)/shard_map/dot_general | solution.py:103
  314.5 18.5 %collective-permute-done = bf16[128,4096]{1,0:T(8,128)(2,1)S(1)} collective-permute-done((bf16[128,4096]{1,0:T(8,128)(2,1)}, bf16[128,4096]{1,0:T(8,128)(2,1)S(1)}, u32[]{:S(2)}, u32[]{:S(2)}) %collective-permute-start) | collective-permute-done | bytes 1048608 | tf_op jit(solution)/shard_map/ppermute | solution.py:10
  (59 shorter events, 16.2 us)
Async XLA Ops:
  7.2 111.8 %copy-start = (bf16[1,1,192,4096]{3,2,1,0:T(8,128)(2,1)S(1)}, bf16[1,1,192,4096]{3,2,1,0:T(8,128)(2,1)}, u32[]{:S(2)}) copy-start(bf16[1,1,192,4096]{3,2,1,0:T(8,128)(2,1)} %param.11) | copy-start | bytes 4718596
  7.2 111.7 %all-gather.5.cloned.1.call-start = ((), (), s32[]{:S(2)}) async-start(), calls=%async_computation.5 | async-start | bytes 6553600 | tf_op jit(solution)/shard_map/all_gather | solution.py:63
  59.1 3.5 %copy-start.9 = (f32[1,128,8]{1,2,0:T(8,128)S(1)}, f32[1,128,8]{1,2,0:T(8,128)}, u32[]{:S(2)}) copy-start(f32[1,128,8]{1,2,0:T(8,128)} %param.9) | copy-start | bytes 12292
  62.5 118.9 %all-gather.3.cloned.1.call-start = ((), (), s32[]{:S(2)}) async-start(), calls=%async_computation.4 | async-start | bytes 6553600 | tf_op jit(solution)/shard_map/all_gather | solution.py:68
  104.9 19.3 %copy-start.5 = (bf16[1,1,192,4096]{3,2,1,0:T(8,128)(2,1)S(1)}, bf16[1,1,192,4096]{3,2,1,0:T(8,128)(2,1)}, u32[]{:S(2)}) copy-start(bf16[1,1,192,4096]{3,2,1,0:T(8,128)(2,1)} %param.12) | copy-start | bytes 4718596
  104.9 149.7 %reduce-scatter.2.cloned.1.call-start = ((), (), s32[]{:S(2)}) async-start(), calls=%async_computation.6 | async-start | bytes 6758400 | tf_op jit(solution)/shard_map/reduce_scatter | solution.py:113
  118.9 5.3 %copy-start.2 = (bf16[640,4096]{1,0:T(8,128)(2,1)S(1)}, bf16[640,4096]{1,0:T(8,128)(2,1)}, u32[]{:S(2)}) copy-start(bf16[640,4096]{1,0:T(8,128)(2,1)} %all-gather.5.cloned.1.call-done) | copy-start | bytes 15728644
  181.4 5.3 %copy-start.3 = (bf16[640,4096]{1,0:T(8,128)(2,1)S(1)}, bf16[640,4096]{1,0:T(8,128)(2,1)}, u32[]{:S(2)}) copy-start(bf16[640,4096]{1,0:T(8,128)(2,1)} %all-gather.3.cloned.1.call-done) | copy-start | bytes 15728644
  181.4 5.3 %copy-start.10 = (bf16[1,1,192,4096]{3,2,1,0:T(8,128)(2,1)S(1)}, bf16[1,1,192,4096]{3,2,1,0:T(8,128)(2,1)}, u32[]{:S(2)}) copy-start(bf16[1,1,192,4096]{3,2,1,0:T(8,128)(2,1)} %param.13) | copy-start | bytes 4718596
  186.6 1.7 copy-start.7
  188.5 1.6 copy-start.6
  254.6 1.3 slice-start.2
  258.3 9.0 %copy-start.8 = (bf16[640,192]{0,1:T(8,128)(2,1)S(1)}, bf16[640,192]{0,1:T(8,128)(2,1)}, u32[]{:S(2)}) copy-start(bf16[640,192]{0,1:T(8,128)(2,1)} %copy-done.7) | copy-start | bytes 737284
  259.5 13.0 %slice-start = ((s8[5242880]{0:T(1024)(128)(4,1)}), s8[1048576]{0:T(1024)(128)(4,1)S(1)}, s32[]{:S(2)}) async-start(s8[5242880]{0:T(1024)(128)(4,1)} %bitcast.58), calls=%async_computation.7 | async-start | bytes 2097152
  259.5 41.6 %all-to-all-start.2 = ((bf16[16,8,5248]{2,1,0:T(8,128)(2,1)}), bf16[16,8,5248]{2,1,0:T(8,128)(2,1)S(1)}, u32[]{:S(2)}, u32[]{:S(2)}) async-start(bf16[16,8,5248]{2,1,0:T(8,128)(2,1)} %fusion.17), calls=%async_computation.3 | async-start | bytes 2686976 | tf_op jit(solution)/shard_map/all_to_all | solution.py:117
  267.3 5.2 %slice-start.1 = ((s8[5242880]{0:T(1024)(128)(4,1)}), s8[4194304]{0:T(1024)(128)(4,1)S(1)}, s32[]{:S(2)}) async-start(s8[5242880]{0:T(1024)(128)(4,1)} %bitcast.58), calls=%async_computation.8 | async-start | bytes 8388608
  301.1 3.8 %copy-start.4 = (bf16[16,8,5248]{2,1,0:T(8,128)(2,1)}, bf16[16,8,5248]{2,1,0:T(8,128)(2,1)S(1)}, u32[]{:S(2)}) copy-start(bf16[16,8,5248]{2,1,0:T(8,128)(2,1)S(1)} %all-to-all-done.2) | copy-start | bytes 4030468
  306.4 26.6 %collective-permute-start = (bf16[128,4096]{1,0:T(8,128)(2,1)}, bf16[128,4096]{1,0:T(8,128)(2,1)S(1)}, u32[]{:S(2)}, u32[]{:S(2)}) collective-permute-start(bf16[128,4096]{1,0:T(8,128)(2,1)} %convolution_convert_fusion.5), channel_id=1, source_target_pairs={{64,0},{128,64},{192,128},{65,1},{129,65},{193,129},{66,2},{130,66... | collective-permute-start | bytes 3145736 | tf_op jit(solution)/shard_map/ppermute | solution.py:10
  307.7 26.3 %copy-start.1 = (bf16[1,1,192,4096]{3,2,1,0:T(8,128)(2,1)S(1)}, bf16[1,1,192,4096]{3,2,1,0:T(8,128)(2,1)}, u32[]{:S(2)}) copy-start(bf16[1,1,192,4096]{3,2,1,0:T(8,128)(2,1)} %param.11) | copy-start | bytes 4718596
Sparse Core Ops, SparseCore 0:
  62.6 56.2 all-gather.4
  121.3 60.0 all-gather.2
  194.7 59.8 reduce-scatter.1

commit v6 on v5

--- a/solution.py
+++ b/solution.py
@@ -60,7 +60,16 @@
         cols = slice(q * width, (q + 1) * width)
         x_e = lax.all_to_all(dense_chunks(local_x[:, cols], experts), "expert", 0, 0, tiled=True)
         x_e = x_e.reshape(experts * capacity, width)
-        rows_x.append(lax.all_gather(x_e, "dp", axis=0, tiled=True))
+        whole = jnp.zeros((groups * experts * capacity, width), x_e.dtype)
+        for shift in range(groups):
+            if shift == 0:
+                got = x_e
+            else:
+                pairs = [(k, (k + shift) % groups) for k in range(groups)]
+                got = lax.ppermute(x_e, "dp", pairs)
+            origin = (my_group - shift) % groups
+            whole = lax.dynamic_update_slice_in_dim(whole, got, origin * experts * capacity, 0)
+        rows_x.append(whole)
     for q in range(pieces):
         cols = slice(q * width, (q + 1) * width)
         dy_e = lax.all_to_all(dense_chunks(local_dy[:, cols], experts), "expert", 0, 0, tiled=True)

time: 341 us -> 341 us (level)
  waiting for transfers between devices: 173 us -> 163 us
  local copies, waits for them, and re-layouts: 18 us -> 23.4 us
  starting transfers between devices: 9.37 us -> 14.3 us
    ppermute x0 -> x3, waiting for transfers between devices: none -> 60.7 us  [per_device(): got = lax.ppermute(x_e, 'dp', pairs)]
    all_gather x1, waiting for transfers between devices: 54.4 us -> 0.01 us  [per_device(): rows_grad.append(lax.all_gather(dy_e, 'dp', axis=0, tiled=True))]
    all_gather x1 -> x0, waiting for transfers between devices: 13.8 us -> none  [per_device(): rows_x.append(lax.all_gather(x_e, 'dp', axis=0, tiled=True))]
    all_to_all x1, blocking collectives: 44.1 us -> 36.9 us  [per_device(): lax.all_to_all(dense_chunks(local_x[:, cols], experts), 'expert', 0, 0, t...]
    all_to_all x1, blocking collectives: 37.1 us -> 44.2 us  [per_device(): lax.all_to_all(dense_chunks(local_dy[:, cols], experts), 'expert', 0, 0,...]
    ppermute x0 -> x3, starting transfers between devices: none -> 5.06 us  [per_device(): got = lax.ppermute(x_e, 'dp', pairs)]
  transfers between devices with their start and end apart: 5 -> 7, of which waited for: 5 -> 5; matrix products, arithmetic and copies ran while one was open for 8% -> 8% of each run, Pallas kernels for 0% -> 0%
where the time goes in v6:
time: 341 us; the launch traced here: 340 us
  waiting for transfers between devices  163 us (48%)
  blocking collectives  81.1 us (24%)
  matrix products  34.2 us (10%)
  local copies, waits for them, and re-layouts  23.4 us (7%)
  between operations  14.4 us (4%)
  starting transfers between devices  14.3 us (4%)
  other arithmetic  9.47 us (3%)
    ppermute x3, waiting for transfers between devices, per_device(): got = lax.ppermute(x_e, 'dp', pairs)  60.7 us
    reduce_scatter x1, waiting for transfers between devices, per_device(): summed = lax.psum_scatter(outgoing, 'dp', scatter_dimension=0, tiled=True)  58.2 us
    all_to_all x1, blocking collectives, per_device(): lax.all_to_all(dense_chunks(local_dy[:, cols], experts), 'expert', 0, 0,...  44.2 us
    all_to_all x1, blocking collectives, per_device(): lax.all_to_all(dense_chunks(local_x[:, cols], experts), 'expert', 0, 0, t...  36.9 us
    all_to_all x1, waiting for transfers between devices, per_device(): lax.all_to_all(jnp.concatenate([body, tail], axis=2), 'expert', 0, 0, til...  26.1 us
    ppermute x1, waiting for transfers between devices, from_behind(): return lax.ppermute(shard, axis, pairs)  18.5 us
    all_to_all x1, starting transfers between devices, per_device(): lax.all_to_all(jnp.concatenate([body, tail], axis=2), 'expert', 0, 0, til...  7.77 us
  transfers between devices with their start and end apart: 7, of which 5 were waited for; matrix products, arithmetic and copies ran while one was open for 8% of the time, Pallas kernels for 0%

profile of v6, /device:TPU:1, one launch (start us, length us, event | category | flops | bytes accessed | tf_op | source)
XLA Modules:
  0.0 340.2 jit_solution(12535880980614678808)
XLA Ops:
  11.2 1.8 convolution_convert_fusion.4
  13.0 1.6 reshape.72
  14.6 44.2 %all_to_all.15 = bf16[16,40,1024]{2,1,0:T(8,128)(2,1)S(1)} all-to-all(bf16[16,40,1024]{2,1,0:T(8,128)(2,1)} %reshape.72), channel_id=1, replica_groups=mesh['pipe'=4,'expert'=16,'dp'=4] {'expert'}, dimensions={0} | all-to-all | bytes 2621440 | tf_op jit(solution)/shard_map/all_to_all | solution.py:75
  60.5 2.8 convolution_convert_fusion.3
  63.3 2.5 reshape.74
  65.8 36.9 %all_to_all.16 = bf16[16,40,1024]{2,1,0:T(8,128)(2,1)} all-to-all(bf16[16,40,1024]{2,1,0:T(8,128)(2,1)S(1)} %reshape.74), channel_id=1, replica_groups=mesh['pipe'=4,'expert'=16,'dp'=4] {'expert'}, dimensions={0} | all-to-all | bytes 2621440 | tf_op jit(solution)/shard_map/all_to_all | solution.py:61
  102.7 2.5 reshape.75
  106.6 2.6 collective-permute-start.1
  111.1 33.8 %collective-permute-done = bf16[160,4096]{1,0:T(8,128)(2,1)} collective-permute-done((bf16[160,4096]{1,0:T(8,128)(2,1)S(1)}, bf16[160,4096]{1,0:T(8,128)(2,1)}, u32[]{:S(2)}, u32[]{:S(2)}) %collective-permute-start) | collective-permute-done | bytes 1310752 | tf_op jit(solution)/shard_map/ppermute | solution.py:69
  146.3 26.9 %collective-permute-done.1 = bf16[160,4096]{1,0:T(8,128)(2,1)} collective-permute-done((bf16[160,4096]{1,0:T(8,128)(2,1)S(1)}, bf16[160,4096]{1,0:T(8,128)(2,1)}, u32[]{:S(2)}, u32[]{:S(2)}) %collective-permute-start.1) | collective-permute-done | bytes 1310752 | tf_op jit(solution)/shard_map/ppermute | solution.py:69
  174.8 2.4 copy-done.2
  177.2 2.7 fusion.12
  179.9 4.5 %fusion.15 = f32[640,192]{0,1:T(8,128)S(1)} fusion(bf16[640,4096]{1,0:T(8,128)(2,1)} %all-gather.2.cloned.1.call-done, bf16[1,1,192,4096]{3,2,1,0:T(8,128)(2,1)S(1)} %copy-done.10), kind=kOutput, calls=%fused_computation.26 | convolution fusion | flops 1006632960 | bytes 7307264 | tf_op jit(solution)/shard_map/dot_general | solution.py:96
  184.5 3.3 multiply_convert_fusion.1
  187.8 1.7 multiply_reduce_fusion
  192.8 2.8 fusion.1
  195.6 58.2 %reduce-scatter.2.cloned.1.call-done = bf16[160,4224]{1,0:T(8,128)(2,1)} async-done(((bf16[640,4224]{1,0:T(8,128)(2,1)}), bf16[160,4224]{1,0:T(8,128)(2,1)}) %reduce-scatter.2.cloned.1.call-update) | async-done | bytes 1351696 | tf_op jit(solution)/shard_map/reduce_scatter | solution.py:122
  258.7 7.8 %all-to-all-start.2 = ((bf16[16,8,5248]{2,1,0:T(8,128)(2,1)}), bf16[16,8,5248]{2,1,0:T(8,128)(2,1)S(1)}, u32[]{:S(2)}, u32[]{:S(2)}) async-start(bf16[16,8,5248]{2,1,0:T(8,128)(2,1)} %fusion.17), calls=%async_computation.3 | async-start | bytes 2686976 | tf_op jit(solution)/shard_map/all_to_all | solution.py:126
  266.5 5.2 %fusion.3 = bf16[1,1,192,4096]{3,2,1,0:T(8,128)(2,1)} fusion(bf16[640,192]{0,1:T(8,128)(2,1)S(1)} %get-tuple-element.5, bf16[640,4096]{1,0:T(8,128)(2,1)} %copy-done.2), kind=kOutput, calls=%fused_computation.12 | convolution fusion | flops 1007419392 | bytes 7061504 | tf_op jit(solution)/shard_map/dot_general | solution.py:115
  271.7 2.5 fusion.2
  274.2 26.1 %all-to-all-done.2 = bf16[16,8,5248]{2,1,0:T(8,128)(2,1)S(1)} async-done(((bf16[16,8,5248]{2,1,0:T(8,128)(2,1)}), bf16[16,8,5248]{2,1,0:T(8,128)(2,1)S(1)}, u32[]{:S(2)}, u32[]{:S(2)}) %all-to-all-start.2) | async-done | bytes 1343520 | tf_op jit(solution)/shard_map/all_to_all | solution.py:126
  301.6 2.6 reshape.77
  307.1 5.1 %fusion.4 = bf16[1,1,192,4096]{3,2,1,0:T(8,128)(2,1)} fusion(bf16[640,192]{0,1:T(8,128)(2,1)S(1)} %copy-done.8, bf16[640,4096]{1,0:T(8,128)(2,1)} %all-gather.2.cloned.1.call-done), kind=kOutput, calls=%fused_computation.13 | convolution fusion | flops 1007419392 | bytes 7061504 | tf_op jit(solution)/shard_map/dot_general | solution.py:109
  313.9 18.5 %collective-permute-done.3 = bf16[128,4096]{1,0:T(8,128)(2,1)S(1)} collective-permute-done((bf16[128,4096]{1,0:T(8,128)(2,1)}, bf16[128,4096]{1,0:T(8,128)(2,1)S(1)}, u32[]{:S(2)}, u32[]{:S(2)}) %collective-permute-start.3) | collective-permute-done | bytes 1048608 | tf_op jit(solution)/shard_map/ppermute | solution.py:10
  (74 shorter events, 27.0 us)
Async XLA Ops:
  7.2 177.2 %copy-start = (bf16[1,1,192,4096]{3,2,1,0:T(8,128)(2,1)S(1)}, bf16[1,1,192,4096]{3,2,1,0:T(8,128)(2,1)}, u32[]{:S(2)}) copy-start(bf16[1,1,192,4096]{3,2,1,0:T(8,128)(2,1)} %param.11) | copy-start | bytes 4718596
  7.2 172.7 %all-gather.2.cloned.1.call-start = ((), (), s32[]{:S(2)}) async-start(), calls=%async_computation.4 | async-start | bytes 6553600 | tf_op jit(solution)/shard_map/all_gather | solution.py:77
  60.4 193.4 %reduce-scatter.2.cloned.1.call-start = ((), (), s32[]{:S(2)}) async-start(), calls=%async_computation.5 | async-start | bytes 6758400 | tf_op jit(solution)/shard_map/reduce_scatter | solution.py:122
  105.2 39.7 %collective-permute-start = (bf16[160,4096]{1,0:T(8,128)(2,1)S(1)}, bf16[160,4096]{1,0:T(8,128)(2,1)}, u32[]{:S(2)}, u32[]{:S(2)}) collective-permute-start(bf16[160,4096]{1,0:T(8,128)(2,1)S(1)} %reshape.75), channel_id=1, source_target_pairs={{0,1},{1,2},{2,3},{3,0},{4,5},{5,6},{6,7},{7,4},{8,9},{9,10},{10,1... | collective-permute-start | bytes 3932168 | tf_op jit(solution)/shard_map/ppermute | solution.py:69
  106.6 66.6 %collective-permute-start.1 = (bf16[160,4096]{1,0:T(8,128)(2,1)S(1)}, bf16[160,4096]{1,0:T(8,128)(2,1)}, u32[]{:S(2)}, u32[]{:S(2)}) collective-permute-start(bf16[160,4096]{1,0:T(8,128)(2,1)S(1)} %reshape.75), channel_id=1, source_target_pairs={{0,2},{1,3},{2,0},{3,1},{4,6},{5,7},{6,4},{7,5},{8,10},{9,11},{10,... | collective-permute-start | bytes 3932168 | tf_op jit(solution)/shard_map/ppermute | solution.py:69
  109.2 65.5 %collective-permute-start.2 = (bf16[160,4096]{1,0:T(8,128)(2,1)S(1)}, bf16[160,4096]{1,0:T(8,128)(2,1)S(1)}, u32[]{:S(2)}, u32[]{:S(2)}) collective-permute-start(bf16[160,4096]{1,0:T(8,128)(2,1)S(1)} %reshape.75), channel_id=1, source_target_pairs={{0,3},{1,0},{2,1},{3,2},{4,7},{5,4},{6,5},{7,6},{8,11},{9,8},{10,9... | collective-permute-start | bytes 3932168 | tf_op jit(solution)/shard_map/ppermute | solution.py:69
  146.3 30.9 %copy-start.5 = (bf16[1,1,192,4096]{3,2,1,0:T(8,128)(2,1)S(1)}, bf16[1,1,192,4096]{3,2,1,0:T(8,128)(2,1)}, u32[]{:S(2)}) copy-start(bf16[1,1,192,4096]{3,2,1,0:T(8,128)(2,1)} %param.12) | copy-start | bytes 4718596
  174.8 2.4 copy-start.2
  177.2 2.7 copy-start.10
  179.9 4.5 %copy-start.3 = (bf16[640,4096]{1,0:T(8,128)(2,1)S(1)}, bf16[640,4096]{1,0:T(8,128)(2,1)}, u32[]{:S(2)}) copy-start(bf16[640,4096]{1,0:T(8,128)(2,1)} %copy-done.2) | copy-start | bytes 15728644
  179.9 7.8 %slice-start.2 = ((s8[5242880]{0:T(1024)(128)(4,1)}), s8[4194304]{0:T(1024)(128)(4,1)S(1)}, s32[]{:S(2)}) async-start(s8[5242880]{0:T(1024)(128)(4,1)} %bitcast.60), calls=%async_computation.8 | async-start | bytes 8388608
  184.4 3.3 slice-start.3
  184.4 3.3 copy-start.11
  187.7 1.7 copy-start.7
  189.6 1.6 copy-start.6
  253.8 1.3 slice-start.4
  258.7 13.0 %slice-start = ((s8[5242880]{0:T(1024)(128)(4,1)}), s8[1048576]{0:T(1024)(128)(4,1)S(1)}, s32[]{:S(2)}) async-start(s8[5242880]{0:T(1024)(128)(4,1)} %bitcast.58), calls=%async_computation.6 | async-start | bytes 2097152
  258.7 41.6 %all-to-all-start.2 = ((bf16[16,8,5248]{2,1,0:T(8,128)(2,1)}), bf16[16,8,5248]{2,1,0:T(8,128)(2,1)S(1)}, u32[]{:S(2)}, u32[]{:S(2)}) async-start(bf16[16,8,5248]{2,1,0:T(8,128)(2,1)} %fusion.17), calls=%async_computation.3 | async-start | bytes 2686976 | tf_op jit(solution)/shard_map/all_to_all | solution.py:126
  266.5 5.2 %slice-start.1 = ((s8[5242880]{0:T(1024)(128)(4,1)}), s8[4194304]{0:T(1024)(128)(4,1)S(1)}, s32[]{:S(2)}) async-start(s8[5242880]{0:T(1024)(128)(4,1)} %bitcast.58), calls=%async_computation.7 | async-start | bytes 8388608
  300.3 3.9 %copy-start.4 = (bf16[16,8,5248]{2,1,0:T(8,128)(2,1)}, bf16[16,8,5248]{2,1,0:T(8,128)(2,1)S(1)}, u32[]{:S(2)}) copy-start(bf16[16,8,5248]{2,1,0:T(8,128)(2,1)S(1)} %all-to-all-done.2) | copy-start | bytes 4030468
  301.6 5.5 %copy-start.8 = (bf16[640,192]{0,1:T(8,128)(2,1)S(1)}, bf16[640,192]{0,1:T(8,128)(2,1)}, u32[]{:S(2)}) copy-start(bf16[640,192]{0,1:T(8,128)(2,1)} %copy-done.7) | copy-start | bytes 737284
  305.6 7.6 %copy-start.9 = (f32[1,128,8]{1,2,0:T(8,128)S(1)}, f32[1,128,8]{1,2,0:T(8,128)}, u32[]{:S(2)}) copy-start(f32[1,128,8]{1,2,0:T(8,128)} %param.9) | copy-start | bytes 12292
  305.6 26.7 %collective-permute-start.3 = (bf16[128,4096]{1,0:T(8,128)(2,1)}, bf16[128,4096]{1,0:T(8,128)(2,1)S(1)}, u32[]{:S(2)}, u32[]{:S(2)}) collective-permute-start(bf16[128,4096]{1,0:T(8,128)(2,1)} %convolution_convert_fusion.5), channel_id=1, source_target_pairs={{64,0},{128,64},{192,128},{65,1},{129,65},{193,129},{66,2},{130,66... | collective-permute-start | bytes 3145736 | tf_op jit(solution)/shard_map/ppermute | solution.py:10
  307.1 26.3 %copy-start.1 = (bf16[1,1,192,4096]{3,2,1,0:T(8,128)(2,1)S(1)}, bf16[1,1,192,4096]{3,2,1,0:T(8,128)(2,1)}, u32[]{:S(2)}) copy-start(bf16[1,1,192,4096]{3,2,1,0:T(8,128)(2,1)} %param.11) | copy-start | bytes 4718596
Sparse Core Ops, SparseCore 0:
  60.6 83.6 all-gather.1
  195.8 57.9 reduce-scatter.1

commit v7 on v5

--- a/solution.py
+++ b/solution.py
@@ -8,6 +8,49 @@
     length = lax.axis_size(axis)
     pairs = [(i, i + by) for i in range(length) if 0 <= i + by < length]
     return lax.ppermute(shard, axis, pairs)
+
+
+def ring_gather(piece, axis, me):
+    size = lax.axis_size(axis)
+    rows = piece.shape[0]
+    half = rows // 2
+    fwd = [(k, (k + 1) % size) for k in range(size)]
+    bwd = [(k, (k - 1) % size) for k in range(size)]
+    from_left = lax.ppermute(piece, axis, fwd)
+    from_right = lax.ppermute(piece, axis, bwd)
+    far_top = lax.ppermute(from_left[:half], axis, fwd)
+    far_bottom = lax.ppermute(from_right[half:], axis, bwd)
+    whole = jnp.zeros((size * rows,) + piece.shape[1:], piece.dtype)
+    whole = lax.dynamic_update_slice_in_dim(whole, piece, me * rows, 0)
+    whole = lax.dynamic_update_slice_in_dim(whole, from_left, ((me - 1) % size) * rows, 0)
+    whole = lax.dynamic_update_slice_in_dim(whole, from_right, ((me + 1) % size) * rows, 0)
+    far = jnp.concatenate([far_top, far_bottom], axis=0)
+    whole = lax.dynamic_update_slice_in_dim(whole, far, ((me + 2) % size) * rows, 0)
+    return whole
+
+
+def ring_reduce_scatter(parts, axis, me):
+    size = lax.axis_size(axis)
+    rows = parts.shape[0] // size
+    half = rows // 2
+    fwd = [(k, (k + 1) % size) for k in range(size)]
+    bwd = [(k, (k - 1) % size) for k in range(size)]
+
+    def block(t):
+        return lax.dynamic_slice_in_dim(parts, (t % size) * rows, rows, 0)
+
+    far = block(me + 2)
+    got_top = lax.ppermute(far[:half], axis, fwd)
+    got_bottom = lax.ppermute(far[half:], axis, bwd)
+    to_right = block(me + 1).astype(jnp.float32)
+    to_right = jnp.concatenate([to_right[:half] + got_top.astype(jnp.float32), to_right[half:]])
+    to_left = block(me - 1).astype(jnp.float32)
+    to_left = jnp.concatenate([to_left[:half], to_left[half:] + got_bottom.astype(jnp.float32)])
+    from_left = lax.ppermute(to_right.astype(jnp.bfloat16), axis, fwd)
+    from_right = lax.ppermute(to_left.astype(jnp.bfloat16), axis, bwd)
+    total = block(me).astype(jnp.float32) + from_left.astype(jnp.float32)
+    total = total + from_right.astype(jnp.float32)
+    return total.astype(jnp.bfloat16)
 
 
 def route_tables(route_col, score_rows, experts, capacity):
@@ -60,12 +103,12 @@
         cols = slice(q * width, (q + 1) * width)
         x_e = lax.all_to_all(dense_chunks(local_x[:, cols], experts), "expert", 0, 0, tiled=True)
         x_e = x_e.reshape(experts * capacity, width)
-        rows_x.append(lax.all_gather(x_e, "dp", axis=0, tiled=True))
+        rows_x.append(ring_gather(x_e, "dp", my_group))
     for q in range(pieces):
         cols = slice(q * width, (q + 1) * width)
         dy_e = lax.all_to_all(dense_chunks(local_dy[:, cols], experts), "expert", 0, 0, tiled=True)
         dy_e = dy_e.reshape(experts * capacity, width)
-        rows_grad.append(lax.all_gather(dy_e, "dp", axis=0, tiled=True))
+        rows_grad.append(ring_gather(dy_e, "dp", my_group))
     gate_pre = 0.0
     up_pre = 0.0
     for q in range(pieces):
@@ -110,7 +153,7 @@
         partial_in = partial_in + jnp.dot(pre_up, up_mat[:, cols], preferred_element_type=jnp.float32)
         score_cols = jnp.pad(row_score[:, None], ((0, 0), (0, 127)))
         outgoing = jnp.concatenate([partial_in, score_cols], axis=1).astype(jnp.bfloat16)
-        summed = lax.psum_scatter(outgoing, "dp", scatter_dimension=0, tiled=True)
+        summed = ring_reduce_scatter(outgoing, "dp", my_group)
         body = summed[:, :width].reshape(experts, 8, capacity * width // 8)
         tail = summed[:, width].reshape(experts, 1, capacity)
         tail = jnp.pad(tail, ((0, 0), (0, 7), (0, 128 - capacity)))

time: 341 us -> 298 us (0.87)
  blocking collectives: 81.2 us -> 0 us
  starting transfers between devices: 9.37 us -> 38.9 us
  local copies, waits for them, and re-layouts: 18 us -> 32.7 us
  between operations: 14 us -> 1.05 us
  waiting for transfers between devices: 173 us -> 181 us
  matrix products: 37 us -> 29.6 us
  other arithmetic: 8.09 us -> 13 us
    all_to_all x2 -> x0, blocking collectives: 81.2 us -> none  [the longest x1 44.1 us: per_device(): lax.all_to_all(dense_chunks(local_x[:, cols], experts), 'expert', 0, 0, t...]
    ppermute x0 -> x12, waiting for transfers between devices: none -> 81.1 us  [the longest x1 26.9 us: ring_reduce_scatter(): from_right = lax.ppermute(to_left.astype(jnp.bfloat16), axis, bwd)]
    all_gather x2 -> x0, waiting for transfers between devices: 68.2 us -> none  [the longest x1 54.4 us: per_device(): rows_grad.append(lax.all_gather(dy_e, 'dp', axis=0, tiled=True))]
    reduce_scatter x1 -> x0, waiting for transfers between devices: 60 us -> none  [per_device(): summed = lax.psum_scatter(outgoing, 'dp', scatter_dimension=0, tiled=True)]
    all_to_all x0 -> x2, waiting for transfers between devices: none -> 55.4 us  [the longest x1 28.5 us: per_device(): lax.all_to_all(dense_chunks(local_dy[:, cols], experts), 'expert', 0, 0,...]
    ppermute x0 -> x12, starting transfers between devices: none -> 17 us  [the longest x2 6.24 us: ring_gather(): far_bottom = lax.ppermute(from_right[half:], axis, bwd)]
    all_to_all x0 -> x2, starting transfers between devices: none -> 14.3 us  [the longest x1 9.98 us: per_device(): lax.all_to_all(dense_chunks(local_x[:, cols], experts), 'expert', 0, 0, t...]
    dynamic_update_slice x0 -> x6, local copies, waits for them, and re-layouts: none -> 7.48 us  [the longest x2 2.93 us: ring_gather(): lax.dynamic_update_slice_in_dim(whole, from_left, (me - 1) % size * rows, 0)]
  transfers between devices with their start and end apart: 5 -> 16, of which waited for: 5 -> 12; matrix products, arithmetic and copies ran while one was open for 8% -> 15% of each run, Pallas kernels for 0% -> 0%
where the time goes in v7:
time: 298 us; the launch traced here: 296 us
  waiting for transfers between devices  181 us (61%)
  starting transfers between devices  38.9 us (13%)
  local copies, waits for them, and re-layouts  32.7 us (11%)
  matrix products  29.6 us (10%)
  other arithmetic  13 us (4%)
    all_to_all x1, waiting for transfers between devices, per_device(): lax.all_to_all(dense_chunks(local_dy[:, cols], experts), 'expert', 0, 0,...  28.5 us
    ppermute x1, waiting for transfers between devices, ring_reduce_scatter(): from_right = lax.ppermute(to_left.astype(jnp.bfloat16), axis, bwd)  26.9 us
    all_to_all x1, waiting for transfers between devices, per_device(): lax.all_to_all(dense_chunks(local_x[:, cols], experts), 'expert', 0, 0, t...  26.9 us
    all_to_all x1, waiting for transfers between devices, per_device(): lax.all_to_all(jnp.concatenate([body, tail], axis=2), 'expert', 0, 0, til...  26.1 us
    ppermute x2, waiting for transfers between devices, ring_gather(): from_right = lax.ppermute(piece, axis, bwd)  20.5 us
    ppermute x1, waiting for transfers between devices, from_behind(): return lax.ppermute(shard, axis, pairs)  18.5 us
    ppermute x1, waiting for transfers between devices, ring_reduce_scatter(): got_top = lax.ppermute(far[:half], axis, fwd)  15.2 us
    all_to_all x1, starting transfers between devices, per_device(): lax.all_to_all(dense_chunks(local_x[:, cols], experts), 'expert', 0, 0, t...  9.98 us
  transfers between devices with their start and end apart: 16, of which 12 were waited for; matrix products, arithmetic and copies ran while one was open for 15% of the time, Pallas kernels for 0%

profile of v7, /device:TPU:1, one launch (start us, length us, event | category | flops | bytes accessed | tf_op | source)
XLA Modules:
  0.0 296.4 jit_solution(12490142758694735751)
XLA Ops:
  6.6 10.0 %all-to-all-start.1 = ((bf16[16,40,1024]{2,1,0:T(8,128)(2,1)}), bf16[16,40,1024]{2,1,0:T(8,128)(2,1)S(1)}, u32[]{:S(2)}, u32[]{:S(2)}) async-start(bf16[16,40,1024]{2,1,0:T(8,128)(2,1)} %reshape.74), calls=%async_computation.1 | async-start | bytes 2621440 | tf_op jit(solution)/shard_map/all_to_all | solution.py:104
  16.6 2.9 convolution_convert_fusion.4
  19.5 3.4 %reshape.72 = bf16[16,40,1024]{2,1,0:T(8,128)(2,1)} reshape(bf16[160,4096]{1,0:T(8,128)(2,1)} %convolution_convert_fusion.4) | data formatting | bytes 2621440 | tf_op jit(solution)/shard_map/reshape | solution.py:70
  22.9 26.9 %all-to-all-done.1 = bf16[16,40,1024]{2,1,0:T(8,128)(2,1)S(1)} async-done(((bf16[16,40,1024]{2,1,0:T(8,128)(2,1)}), bf16[16,40,1024]{2,1,0:T(8,128)(2,1)S(1)}, u32[]{:S(2)}, u32[]{:S(2)}) %all-to-all-start.1) | async-done | bytes 1310752 | tf_op jit(solution)/shard_map/all_to_all | solution.py:104
  49.7 4.3 %all-to-all-start = ((bf16[16,40,1024]{2,1,0:T(8,128)(2,1)}), bf16[16,40,1024]{2,1,0:T(8,128)(2,1)}, u32[]{:S(2)}, u32[]{:S(2)}) async-start(bf16[16,40,1024]{2,1,0:T(8,128)(2,1)} %reshape.72), calls=%async_computation | async-start | bytes 2621440 | tf_op jit(solution)/shard_map/all_to_all | solution.py:109
  55.7 2.7 collective-permute-start.5
  58.4 28.5 %all-to-all-done = bf16[16,40,1024]{2,1,0:T(8,128)(2,1)} async-done(((bf16[16,40,1024]{2,1,0:T(8,128)(2,1)}), bf16[16,40,1024]{2,1,0:T(8,128)(2,1)}, u32[]{:S(2)}, u32[]{:S(2)}) %all-to-all-start) | async-done | bytes 1310752 | tf_op jit(solution)/shard_map/all_to_all | solution.py:109
  89.4 2.8 collective-permute-start.1
  96.3 2.8 collective-permute-start.7
  100.3 20.5 %collective-permute-done.1 = bf16[160,4096]{1,0:T(8,128)(2,1)} collective-permute-done((bf16[160,4096]{1,0:T(8,128)(2,1)S(1)}, bf16[160,4096]{1,0:T(8,128)(2,1)}, u32[]{:S(2)}, u32[]{:S(2)}) %collective-permute-start.1) | collective-permute-done | bytes 1310752 | tf_op jit(solution)/shard_map/ppermute | solution.py:20
  121.9 3.5 %collective-permute-start.3 = (bf16[80,4096]{1,0:T(8,128)(2,1)S(1)}, bf16[80,4096]{1,0:T(8,128)(2,1)S(1)}, u32[]{:S(2)}, u32[]{:S(2)}) collective-permute-start(bf16[80,4096]{1,0:T(8,128)(2,1)S(1)} %slice.72), channel_id=1, source_target_pairs={{0,3},{1,0},{2,1},{3,2},{4,7},{5,4},{6,5},{7,6},{8,11},{9,8},{10,9... | collective-permute-start | bytes 1966088 | tf_op jit(solution)/shard_map/ppermute | solution.py:22
  134.8 3.5 %collective-permute-done.6 = bf16[80,4096]{1,0:T(8,128)(2,1)S(1)} collective-permute-done((bf16[80,4096]{1,0:T(8,128)(2,1)S(1)}, bf16[80,4096]{1,0:T(8,128)(2,1)S(1)}, u32[]{:S(2)}, u32[]{:S(2)}) %collective-permute-start.6) | collective-permute-done | bytes 655392 | tf_op jit(solution)/shard_map/ppermute | solution.py:21
  142.9 5.5 %collective-permute-done.3 = bf16[80,4096]{1,0:T(8,128)(2,1)S(1)} collective-permute-done((bf16[80,4096]{1,0:T(8,128)(2,1)S(1)}, bf16[80,4096]{1,0:T(8,128)(2,1)S(1)}, u32[]{:S(2)}, u32[]{:S(2)}) %collective-permute-start.3) | collective-permute-done | bytes 655392 | tf_op jit(solution)/shard_map/ppermute | solution.py:22
  148.5 3.5 %collective-permute-done.2 = bf16[80,4096]{1,0:T(8,128)(2,1)S(1)} collective-permute-done((bf16[80,4096]{1,0:T(8,128)(2,1)S(1)}, bf16[80,4096]{1,0:T(8,128)(2,1)S(1)}, u32[]{:S(2)}, u32[]{:S(2)}) %collective-permute-start.2) | collective-permute-done | bytes 655392 | tf_op jit(solution)/shard_map/ppermute | solution.py:21
  162.5 2.7 collective-permute-start.10
  165.2 15.2 %collective-permute-done.8 = bf16[80,4224]{1,0:T(8,128)(2,1)} collective-permute-done((bf16[80,4224]{1,0:T(8,128)(2,1)}, bf16[80,4224]{1,0:T(8,128)(2,1)}, u32[]{:S(2)}, u32[]{:S(2)}) %collective-permute-start.8) | collective-permute-done | bytes 675872 | tf_op jit(solution)/shard_map/ppermute | solution.py:43
  186.9 26.9 %collective-permute-done.11 = bf16[160,4224]{1,0:T(8,128)(2,1)} collective-permute-done((bf16[160,4224]{1,0:T(8,128)(2,1)}, bf16[160,4224]{1,0:T(8,128)(2,1)}, u32[]{:S(2)}, u32[]{:S(2)}) %collective-permute-start.11) | collective-permute-done | bytes 1351712 | tf_op jit(solution)/shard_map/ppermute | solution.py:50
  213.8 3.9 %collective-permute-done.9 = bf16[160,4224]{1,0:T(8,128)(2,1)} collective-permute-done((bf16[160,4224]{1,0:T(8,128)(2,1)}, bf16[160,4224]{1,0:T(8,128)(2,1)}, u32[]{:S(2)}, u32[]{:S(2)}) %collective-permute-start.9) | collective-permute-done | bytes 1351712 | tf_op jit(solution)/shard_map/ppermute | solution.py:49
  217.7 2.6 add_convert_fusion.1
  223.3 6.4 %all-to-all-start.2 = ((bf16[16,8,5248]{2,1,0:T(8,128)(2,1)}), bf16[16,8,5248]{2,1,0:T(8,128)(2,1)S(1)}, u32[]{:S(2)}, u32[]{:S(2)}) async-start(bf16[16,8,5248]{2,1,0:T(8,128)(2,1)} %fusion.20), calls=%async_computation.2 | async-start | bytes 2686976 | tf_op jit(solution)/shard_map/all_to_all | solution.py:160
  229.7 5.2 %fusion.4 = bf16[1,1,192,4096]{3,2,1,0:T(8,128)(2,1)} fusion(bf16[640,192]{0,1:T(8,128)(2,1)S(1)} %copy-done.8, bf16[640,4096]{1,0:T(8,128)(2,1)} %copy-done.3), kind=kOutput, calls=%fused_computation.13 | convolution fusion | flops 1007419392 | bytes 7061504 | tf_op jit(solution)/shard_map/dot_general | solution.py:143
  237.5 26.1 %all-to-all-done.2 = bf16[16,8,5248]{2,1,0:T(8,128)(2,1)S(1)} async-done(((bf16[16,8,5248]{2,1,0:T(8,128)(2,1)}), bf16[16,8,5248]{2,1,0:T(8,128)(2,1)S(1)}, u32[]{:S(2)}, u32[]{:S(2)}) %all-to-all-start.2) | async-done | bytes 1343520 | tf_op jit(solution)/shard_map/all_to_all | solution.py:160
  270.2 5.1 %fusion.2 = bf16[1,1,192,4096]{3,2,1,0:T(8,128)(2,1)} fusion(bf16[640,192]{0,1:T(8,128)(2,1)S(1)} %get-tuple-element.12, bf16[640,4096]{1,0:T(8,128)(2,1)} %copy-done.2), kind=kOutput, calls=%fused_computation.11 | convolution fusion | flops 1007419392 | bytes 7061504 | tf_op jit(solution)/shard_map/dot_general | solution.py:146
  277.0 18.5 %collective-permute-done.12 = bf16[128,4096]{1,0:T(8,128)(2,1)S(1)} collective-permute-done((bf16[128,4096]{1,0:T(8,128)(2,1)}, bf16[128,4096]{1,0:T(8,128)(2,1)S(1)}, u32[]{:S(2)}, u32[]{:S(2)}) %collective-permute-start.12) | collective-permute-done | bytes 1048608 | tf_op jit(solution)/shard_map/ppermute | solution.py:10
  (94 shorter events, 62.1 us)
Async XLA Ops:
  0.6 137.8 %copy-start = (bf16[1,1,192,4096]{3,2,1,0:T(8,128)(2,1)S(1)}, bf16[1,1,192,4096]{3,2,1,0:T(8,128)(2,1)}, u32[]{:S(2)}) copy-start(bf16[1,1,192,4096]{3,2,1,0:T(8,128)(2,1)} %param.11) | copy-start | bytes 4718596
  4.9 11.6 %copy-start.9 = (f32[1,128,8]{1,2,0:T(8,128)S(1)}, f32[1,128,8]{1,2,0:T(8,128)}, u32[]{:S(2)}) copy-start(f32[1,128,8]{1,2,0:T(8,128)} %param.9) | copy-start | bytes 12292
  6.6 43.2 %all-to-all-start.1 = ((bf16[16,40,1024]{2,1,0:T(8,128)(2,1)}), bf16[16,40,1024]{2,1,0:T(8,128)(2,1)S(1)}, u32[]{:S(2)}, u32[]{:S(2)}) async-start(bf16[16,40,1024]{2,1,0:T(8,128)(2,1)} %reshape.74), calls=%async_computation.1 | async-start | bytes 2621440 | tf_op jit(solution)/shard_map/all_to_all | solution.py:104
  49.7 37.2 %all-to-all-start = ((bf16[16,40,1024]{2,1,0:T(8,128)(2,1)}), bf16[16,40,1024]{2,1,0:T(8,128)(2,1)}, u32[]{:S(2)}, u32[]{:S(2)}) async-start(bf16[16,40,1024]{2,1,0:T(8,128)(2,1)} %reshape.72), calls=%async_computation | async-start | bytes 2621440 | tf_op jit(solution)/shard_map/all_to_all | solution.py:109
  55.7 39.5 %collective-permute-start.5 = (bf16[160,4096]{1,0:T(8,128)(2,1)}, bf16[160,4096]{1,0:T(8,128)(2,1)}, u32[]{:S(2)}, u32[]{:S(2)}) collective-permute-start(bf16[160,4096]{1,0:T(8,128)(2,1)} %reshape.75), channel_id=1, source_target_pairs={{0,3},{1,0},{2,1},{3,2},{4,7},{5,4},{6,5},{7,6},{8,11},{9,8},{10,9... | collective-permute-start | bytes 3932168 | tf_op jit(solution)/shard_map/ppermute | solution.py:20
  58.4 40.6 %collective-permute-start.4 = (bf16[160,4096]{1,0:T(8,128)(2,1)}, bf16[160,4096]{1,0:T(8,128)(2,1)}, u32[]{:S(2)}, u32[]{:S(2)}) collective-permute-start(bf16[160,4096]{1,0:T(8,128)(2,1)} %reshape.75), channel_id=1, source_target_pairs={{0,1},{1,2},{2,3},{3,0},{4,5},{5,6},{6,7},{7,4},{8,9},{9,10},{10,1... | collective-permute-start | bytes 3932168 | tf_op jit(solution)/shard_map/ppermute | solution.py:19
  89.4 31.3 %collective-permute-start.1 = (bf16[160,4096]{1,0:T(8,128)(2,1)S(1)}, bf16[160,4096]{1,0:T(8,128)(2,1)}, u32[]{:S(2)}, u32[]{:S(2)}) collective-permute-start(bf16[160,4096]{1,0:T(8,128)(2,1)S(1)} %reshape.73), channel_id=1, source_target_pairs={{0,3},{1,0},{2,1},{3,2},{4,7},{5,4},{6,5},{7,6},{8,11},{9,8},{10,9... | collective-permute-start | bytes 3932168 | tf_op jit(solution)/shard_map/ppermute | solution.py:20
  92.2 33.1 %collective-permute-start = (bf16[160,4096]{1,0:T(8,128)(2,1)S(1)}, bf16[160,4096]{1,0:T(8,128)(2,1)}, u32[]{:S(2)}, u32[]{:S(2)}) collective-permute-start(bf16[160,4096]{1,0:T(8,128)(2,1)S(1)} %reshape.73), channel_id=1, source_target_pairs={{0,1},{1,2},{2,3},{3,0},{4,5},{5,6},{6,7},{7,4},{8,9},{9,10},{10,1... | collective-permute-start | bytes 3932168 | tf_op jit(solution)/shard_map/ppermute | solution.py:19
  96.3 38.5 %collective-permute-start.7 = (bf16[80,4096]{1,0:T(8,128)(2,1)S(1)}, bf16[80,4096]{1,0:T(8,128)(2,1)S(1)}, u32[]{:S(2)}, u32[]{:S(2)}) collective-permute-start(bf16[80,4096]{1,0:T(8,128)(2,1)S(1)} %slice.74), channel_id=1, source_target_pairs={{0,3},{1,0},{2,1},{3,2},{4,7},{5,4},{6,5},{7,6},{8,11},{9,8},{10,9... | collective-permute-start | bytes 1966088 | tf_op jit(solution)/shard_map/ppermute | solution.py:22
  100.2 38.1 %collective-permute-start.6 = (bf16[80,4096]{1,0:T(8,128)(2,1)S(1)}, bf16[80,4096]{1,0:T(8,128)(2,1)S(1)}, u32[]{:S(2)}, u32[]{:S(2)}) collective-permute-start(bf16[80,4096]{1,0:T(8,128)(2,1)S(1)} %slice.73), channel_id=1, source_target_pairs={{0,1},{1,2},{2,3},{3,0},{4,5},{5,6},{6,7},{7,4},{8,9},{9,10},{10,1... | collective-permute-start | bytes 1966088 | tf_op jit(solution)/shard_map/ppermute | solution.py:21
  121.9 26.6 %collective-permute-start.3 = (bf16[80,4096]{1,0:T(8,128)(2,1)S(1)}, bf16[80,4096]{1,0:T(8,128)(2,1)S(1)}, u32[]{:S(2)}, u32[]{:S(2)}) collective-permute-start(bf16[80,4096]{1,0:T(8,128)(2,1)S(1)} %slice.72), channel_id=1, source_target_pairs={{0,3},{1,0},{2,1},{3,2},{4,7},{5,4},{6,5},{7,6},{8,11},{9,8},{10,9... | collective-permute-start | bytes 1966088 | tf_op jit(solution)/shard_map/ppermute | solution.py:22
  126.5 25.4 %collective-permute-start.2 = (bf16[80,4096]{1,0:T(8,128)(2,1)S(1)}, bf16[80,4096]{1,0:T(8,128)(2,1)S(1)}, u32[]{:S(2)}, u32[]{:S(2)}) collective-permute-start(bf16[80,4096]{1,0:T(8,128)(2,1)S(1)} %slice.71), channel_id=1, source_target_pairs={{0,1},{1,2},{2,3},{3,0},{4,5},{5,6},{6,7},{7,4},{8,9},{9,10},{10,1... | collective-permute-start | bytes 1966088 | tf_op jit(solution)/shard_map/ppermute | solution.py:21
  142.9 9.2 %copy-start.10 = (bf16[1,1,192,4096]{3,2,1,0:T(8,128)(2,1)S(1)}, bf16[1,1,192,4096]{3,2,1,0:T(8,128)(2,1)}, u32[]{:S(2)}) copy-start(bf16[1,1,192,4096]{3,2,1,0:T(8,128)(2,1)} %param.13) | copy-start | bytes 4718596
  162.5 17.9 %collective-permute-start.8 = (bf16[80,4224]{1,0:T(8,128)(2,1)}, bf16[80,4224]{1,0:T(8,128)(2,1)}, u32[]{:S(2)}, u32[]{:S(2)}) collective-permute-start(bf16[80,4224]{1,0:T(8,128)(2,1)} %get-tuple-element.7), channel_id=1, source_target_pairs={{0,1},{1,2},{2,3},{3,0},{4,5},{5,6},{6,7},{7,4},{8,9},{9,10},{10,1... | collective-permute-start | bytes 2027528 | tf_op jit(solution)/shard_map/ppermute | solution.py:43
  162.5 17.9 %collective-permute-start.10 = (bf16[80,4224]{1,0:T(8,128)(2,1)S(1)}, bf16[80,4224]{1,0:T(8,128)(2,1)}, u32[]{:S(2)}, u32[]{:S(2)}) collective-permute-start(bf16[80,4224]{1,0:T(8,128)(2,1)S(1)} %get-tuple-element.9), channel_id=1, source_target_pairs={{0,3},{1,0},{2,1},{3,2},{4,7},{5,4},{6,5},{7,6},{8,11},{9,8},{10,9... | collective-permute-start | bytes 2027528 | tf_op jit(solution)/shard_map/ppermute | solution.py:44
  183.6 30.2 %collective-permute-start.11 = (bf16[160,4224]{1,0:T(8,128)(2,1)}, bf16[160,4224]{1,0:T(8,128)(2,1)}, u32[]{:S(2)}, u32[]{:S(2)}) collective-permute-start(bf16[160,4224]{1,0:T(8,128)(2,1)} %pad_maximum_fusion.1), channel_id=1, source_target_pairs={{0,3},{1,0},{2,1},{3,2},{4,7},{5,4},{6,5},{7,6},{8,11},{9,8},{10,9... | collective-permute-start | bytes 4055048 | tf_op jit(solution)/shard_map/ppermute | solution.py:50
  186.9 30.8 %collective-permute-start.9 = (bf16[160,4224]{1,0:T(8,128)(2,1)}, bf16[160,4224]{1,0:T(8,128)(2,1)}, u32[]{:S(2)}, u32[]{:S(2)}) collective-permute-start(bf16[160,4224]{1,0:T(8,128)(2,1)} %pad_maximum_fusion), channel_id=1, source_target_pairs={{0,1},{1,2},{2,3},{3,0},{4,5},{5,6},{6,7},{7,4},{8,9},{9,10},{10,1... | collective-permute-start | bytes 4055048 | tf_op jit(solution)/shard_map/ppermute | solution.py:49
  222.2 7.6 %copy-start.8 = (bf16[640,192]{0,1:T(8,128)(2,1)S(1)}, bf16[640,192]{0,1:T(8,128)(2,1)}, u32[]{:S(2)}) copy-start(bf16[640,192]{0,1:T(8,128)(2,1)} %copy-done.7) | copy-start | bytes 737284
  223.3 11.6 %slice-start = ((s8[5242880]{0:T(1024)(128)(4,1)}), s8[1048576]{0:T(1024)(128)(4,1)S(1)}, s32[]{:S(2)}) async-start(s8[5242880]{0:T(1024)(128)(4,1)} %bitcast.60), calls=%async_computation.3 | async-start | bytes 2097152
  223.3 40.3 %all-to-all-start.2 = ((bf16[16,8,5248]{2,1,0:T(8,128)(2,1)}), bf16[16,8,5248]{2,1,0:T(8,128)(2,1)S(1)}, u32[]{:S(2)}, u32[]{:S(2)}) async-start(bf16[16,8,5248]{2,1,0:T(8,128)(2,1)} %fusion.20), calls=%async_computation.2 | async-start | bytes 2686976 | tf_op jit(solution)/shard_map/all_to_all | solution.py:160
  229.7 5.2 %slice-start.1 = ((s8[5242880]{0:T(1024)(128)(4,1)}), s8[4194304]{0:T(1024)(128)(4,1)S(1)}, s32[]{:S(2)}) async-start(s8[5242880]{0:T(1024)(128)(4,1)} %bitcast.60), calls=%async_computation.4 | async-start | bytes 8388608
  263.6 3.8 %copy-start.5 = (bf16[16,8,5248]{2,1,0:T(8,128)(2,1)}, bf16[16,8,5248]{2,1,0:T(8,128)(2,1)S(1)}, u32[]{:S(2)}) copy-start(bf16[16,8,5248]{2,1,0:T(8,128)(2,1)S(1)} %all-to-all-done.2) | copy-start | bytes 4030468
  268.9 26.6 %collective-permute-start.12 = (bf16[128,4096]{1,0:T(8,128)(2,1)}, bf16[128,4096]{1,0:T(8,128)(2,1)S(1)}, u32[]{:S(2)}, u32[]{:S(2)}) collective-permute-start(bf16[128,4096]{1,0:T(8,128)(2,1)} %convolution_convert_fusion.5), channel_id=1, source_target_pairs={{64,0},{128,64},{192,128},{65,1},{129,65},{193,129},{66,2},{130,66... | collective-permute-start | bytes 3145736 | tf_op jit(solution)/shard_map/ppermute | solution.py:10
  270.2 26.3 %copy-start.1 = (bf16[1,1,192,4096]{3,2,1,0:T(8,128)(2,1)S(1)}, bf16[1,1,192,4096]{3,2,1,0:T(8,128)(2,1)}, u32[]{:S(2)}) copy-start(bf16[1,1,192,4096]{3,2,1,0:T(8,128)(2,1)} %param.11) | copy-start | bytes 4718596
  (5 other events, 11.8 us)

commit v8 on v7

--- a/solution.py
+++ b/solution.py
@@ -137,9 +137,7 @@
     grad_down = []
     grad_gate = []
     grad_up = []
-    grads_in = []
-    for q in range(pieces):
-        cols = slice(q * width, (q + 1) * width)
+    for q in range(pieces):
         grad_down.append(lax.dot_general(
             activated, rows_grad[q], token_contract, preferred_element_type=jnp.float32
         ).astype(jnp.bfloat16))
@@ -149,30 +147,40 @@
         grad_up.append(lax.dot_general(
             pre_up, rows_x[q], token_contract, preferred_element_type=jnp.float32
         ).astype(jnp.bfloat16))
-        partial_in = jnp.dot(pre_gate, gate_mat[:, cols], preferred_element_type=jnp.float32)
-        partial_in = partial_in + jnp.dot(pre_up, up_mat[:, cols], preferred_element_type=jnp.float32)
-        score_cols = jnp.pad(row_score[:, None], ((0, 0), (0, 127)))
-        outgoing = jnp.concatenate([partial_in, score_cols], axis=1).astype(jnp.bfloat16)
-        summed = ring_reduce_scatter(outgoing, "dp", my_group)
-        body = summed[:, :width].reshape(experts, 8, capacity * width // 8)
-        tail = summed[:, width].reshape(experts, 1, capacity)
-        tail = jnp.pad(tail, ((0, 0), (0, 7), (0, 128 - capacity)))
-        back = lax.all_to_all(jnp.concatenate([body, tail], axis=2), "expert", 0, 0, tiled=True)
-        flat_in = back[:, :, : capacity * width // 8].reshape(experts * capacity, width)
-        slot_score = back[:, 0, capacity * width // 8 : capacity * width // 8 + capacity]
-        grads_in.append(jnp.dot(table_half, flat_in, preferred_element_type=jnp.float32).astype(
-            jnp.bfloat16
-        ))
     grad_down = jnp.concatenate(grad_down, axis=1)
     grad_gate = jnp.concatenate(grad_gate, axis=1)
     grad_up = jnp.concatenate(grad_up, axis=1)
-    input_grad = jnp.concatenate(grads_in, axis=1)
+    back_pieces = 2
+    back_width = model_width // back_pieces
+    handed = []
+    for q in range(back_pieces):
+        cols = slice(q * back_width, (q + 1) * back_width)
+        partial_in = jnp.dot(pre_gate, gate_mat[:, cols], preferred_element_type=jnp.float32)
+        partial_in = partial_in + jnp.dot(pre_up, up_mat[:, cols], preferred_element_type=jnp.float32)
+        if q == 0:
+            score_cols = jnp.pad(row_score[:, None], ((0, 0), (0, 127)))
+            partial_in = jnp.concatenate([partial_in, score_cols], axis=1)
+        summed = ring_reduce_scatter(partial_in.astype(jnp.bfloat16), "dp", my_group)
+        span = capacity * back_width // 8
+        body = summed[:, :back_width].reshape(experts, 8, span)
+        if q == 0:
+            tail = summed[:, back_width].reshape(experts, 1, capacity)
+            tail = jnp.pad(tail, ((0, 0), (0, 7), (0, 128 - capacity)))
+            body = jnp.concatenate([body, tail], axis=2)
+        back = lax.all_to_all(body, "expert", 0, 0, tiled=True)
+        if q == 0:
+            slot_score = back[:, 0, span : span + capacity]
+        flat_in = back[:, :, :span].reshape(experts * capacity, back_width)
+        piece_grad = jnp.dot(table_half, flat_in, preferred_element_type=jnp.float32).astype(
+            jnp.bfloat16
+        )
+        handed.append(from_behind(piece_grad, "pipe", -1))
+    handed = jnp.concatenate(handed, axis=1)
     slot_score = slot_score.astype(jnp.float32).reshape(-1)
     picked = jnp.sum(jnp.where(table, slot_score[None, :], jnp.float32(0.0)), axis=1)
     gate_grad = picked / gate
     is_first = (jnp.arange(score_rows.shape[1]) == 0).astype(jnp.float32)
     score_grad = gate_grad[:, None] * weights[:, 0:1] * (is_first - weights)
-    handed = from_behind(input_grad, "pipe", -1)
     return (
         score_grad[None],
         handed[None],

time: 298 us -> 276 us (0.926)
  waiting for transfers between devices: 181 us -> 136 us
  starting transfers between devices: 38.9 us -> 60.1 us
    ppermute x1 -> x2, waiting for transfers between devices: 26.9 us -> 0.01 us  [ring_reduce_scatter(): from_right = lax.ppermute(to_left.astype(jnp.bfloat16), axis, bwd)]
    ppermute x2, waiting for transfers between devices: 0.01 us -> 21.1 us  [ring_gather(): from_left = lax.ppermute(piece, axis, fwd)]
    ppermute x2, waiting for transfers between devices: 20.5 us -> 0.01 us  [ring_gather(): from_right = lax.ppermute(piece, axis, bwd)]
    ppermute x1 -> x2, waiting for transfers between devices: 15.2 us -> 2.26 us  [ring_reduce_scatter(): got_top = lax.ppermute(far[:half], axis, fwd)]
    all_to_all x1 -> x2, waiting for transfers between devices: 26.1 us -> 14.9 us  [per_device(): back = lax.all_to_all(body, 'expert', 0, 0, tiled=True)]
    ppermute x1 -> x2, starting transfers between devices: 2.67 us -> 12.4 us  [ring_reduce_scatter(): got_bottom = lax.ppermute(far[half:], axis, bwd)]
    ppermute x1 -> x2, waiting for transfers between devices: 3.93 us -> 13.1 us  [ring_reduce_scatter(): from_left = lax.ppermute(to_right.astype(jnp.bfloat16), axis, fwd)]
    ppermute x2, waiting for transfers between devices: 7.64 us -> 0.55 us  [ring_gather(): far_bottom = lax.ppermute(from_right[half:], axis, bwd)]
  transfers between devices with their start and end apart: 16 -> 22, of which waited for: 12 -> 15; matrix products, arithmetic and copies ran while one was open for 15% -> 22% of each run, Pallas kernels for 0% -> 0%
where the time goes in v8:
time: 276 us; the launch traced here: 272 us
  waiting for transfers between devices  136 us (49%)
  starting transfers between devices  60.1 us (22%)
  local copies, waits for them, and re-layouts  32.4 us (12%)
  matrix products  26.8 us (10%)
  other arithmetic  15.4 us (6%)
    all_to_all x1, waiting for transfers between devices, per_device(): lax.all_to_all(dense_chunks(local_dy[:, cols], experts), 'expert', 0, 0,...  28.5 us
    all_to_all x1, waiting for transfers between devices, per_device(): lax.all_to_all(dense_chunks(local_x[:, cols], experts), 'expert', 0, 0, t...  26.9 us
    ppermute x2, waiting for transfers between devices, ring_gather(): from_left = lax.ppermute(piece, axis, fwd)  21.1 us
    all_to_all x2, waiting for transfers between devices, per_device(): back = lax.all_to_all(body, 'expert', 0, 0, tiled=True)  14.9 us
    ppermute x2, waiting for transfers between devices, from_behind(): return lax.ppermute(shard, axis, pairs)  13.9 us
    ppermute x2, waiting for transfers between devices, ring_reduce_scatter(): from_left = lax.ppermute(to_right.astype(jnp.bfloat16), axis, fwd)  13.1 us
    ppermute x2, starting transfers between devices, ring_reduce_scatter(): got_bottom = lax.ppermute(far[half:], axis, bwd)  12.4 us
    all_to_all x2, starting transfers between devices, per_device(): back = lax.all_to_all(body, 'expert', 0, 0, tiled=True)  12.3 us
  transfers between devices with their start and end apart: 22, of which 15 were waited for; matrix products, arithmetic and copies ran while one was open for 22% of the time, Pallas kernels for 0%

profile of v8, /device:TPU:1, one launch (start us, length us, event | category | flops | bytes accessed | tf_op | source)
XLA Modules:
  0.0 271.8 jit_solution(3918285637708261981)
XLA Ops:
  6.6 10.0 %all-to-all-start.1 = ((bf16[16,40,1024]{2,1,0:T(8,128)(2,1)}), bf16[16,40,1024]{2,1,0:T(8,128)(2,1)S(1)}, u32[]{:S(2)}, u32[]{:S(2)}) async-start(bf16[16,40,1024]{2,1,0:T(8,128)(2,1)} %reshape.80), calls=%async_computation.1 | async-start | bytes 2621440 | tf_op jit(solution)/shard_map/all_to_all | solution.py:104
  16.6 2.9 %convolution_convert_fusion.4 = bf16[160,4096]{1,0:T(8,128)(2,1)} fusion(bf16[1,128,4096]{2,1,0:T(8,128)(2,1)} %param.10, f32[128]{0:T(128)S(1)} %convert_element_type.127, s32[128]{0:T(128)S(1)} %multiply_add_fusion), kind=kOutput, calls=%fused_computation.9 | convolution fusion | flops 170020864 | bytes 2360320 | tf_op jit(solution)/shard_map/dot_general | solution.py:95
  19.5 3.4 %reshape.78 = bf16[16,40,1024]{2,1,0:T(8,128)(2,1)} reshape(bf16[160,4096]{1,0:T(8,128)(2,1)} %convolution_convert_fusion.4) | data formatting | bytes 2621440 | tf_op jit(solution)/shard_map/reshape | solution.py:70
  22.9 26.9 %all-to-all-done.1 = bf16[16,40,1024]{2,1,0:T(8,128)(2,1)S(1)} async-done(((bf16[16,40,1024]{2,1,0:T(8,128)(2,1)}), bf16[16,40,1024]{2,1,0:T(8,128)(2,1)S(1)}, u32[]{:S(2)}, u32[]{:S(2)}) %all-to-all-start.1) | async-done | bytes 1310752 | tf_op jit(solution)/shard_map/all_to_all | solution.py:104
  49.7 4.3 %all-to-all-start = ((bf16[16,40,1024]{2,1,0:T(8,128)(2,1)}), bf16[16,40,1024]{2,1,0:T(8,128)(2,1)}, u32[]{:S(2)}, u32[]{:S(2)}) async-start(bf16[16,40,1024]{2,1,0:T(8,128)(2,1)} %reshape.78), calls=%async_computation | async-start | bytes 2621440 | tf_op jit(solution)/shard_map/all_to_all | solution.py:109
  58.4 28.5 %all-to-all-done = bf16[16,40,1024]{2,1,0:T(8,128)(2,1)} async-done(((bf16[16,40,1024]{2,1,0:T(8,128)(2,1)}), bf16[16,40,1024]{2,1,0:T(8,128)(2,1)}, u32[]{:S(2)}, u32[]{:S(2)}) %all-to-all-start) | async-done | bytes 1310752 | tf_op jit(solution)/shard_map/all_to_all | solution.py:109
  97.6 2.7 %collective-permute-start.7 = (bf16[80,4096]{1,0:T(8,128)(2,1)S(1)}, bf16[80,4096]{1,0:T(8,128)(2,1)S(1)}, u32[]{:S(2)}, u32[]{:S(2)}) collective-permute-start(bf16[80,4096]{1,0:T(8,128)(2,1)S(1)} %slice.124), channel_id=1, source_target_pairs={{0,3},{1,0},{2,1},{3,2},{4,7},{5,4},{6,5},{7,6},{8,11},{9,8},{10,9... | collective-permute-start | bytes 1966088 | tf_op jit(solution)/shard_map/ppermute | solution.py:22
  100.4 21.1 %collective-permute-done = bf16[160,4096]{1,0:T(8,128)(2,1)} collective-permute-done((bf16[160,4096]{1,0:T(8,128)(2,1)S(1)}, bf16[160,4096]{1,0:T(8,128)(2,1)}, u32[]{:S(2)}, u32[]{:S(2)}) %collective-permute-start) | collective-permute-done | bytes 1310752 | tf_op jit(solution)/shard_map/ppermute | solution.py:19
  124.0 2.9 %collective-permute-start.3 = (bf16[80,4096]{1,0:T(8,128)(2,1)S(1)}, bf16[80,4096]{1,0:T(8,128)(2,1)S(1)}, u32[]{:S(2)}, u32[]{:S(2)}) collective-permute-start(bf16[80,4096]{1,0:T(8,128)(2,1)S(1)} %slice.122), channel_id=1, source_target_pairs={{0,3},{1,0},{2,1},{3,2},{4,7},{5,4},{6,5},{7,6},{8,11},{9,8},{10,9... | collective-permute-start | bytes 1966088 | tf_op jit(solution)/shard_map/ppermute | solution.py:22
  132.9 2.7 collective-permute-done.6
  140.3 8.6 %collective-permute-done.2 = bf16[80,4096]{1,0:T(8,128)(2,1)S(1)} collective-permute-done((bf16[80,4096]{1,0:T(8,128)(2,1)S(1)}, bf16[80,4096]{1,0:T(8,128)(2,1)S(1)}, u32[]{:S(2)}, u32[]{:S(2)}) %collective-permute-start.2) | collective-permute-done | bytes 655392 | tf_op jit(solution)/shard_map/ppermute | solution.py:21
  160.3 11.0 %collective-permute-start.10 = (bf16[80,2176]{1,0:T(8,128)(2,1)S(1)}, bf16[80,2176]{1,0:T(8,128)(2,1)S(1)}, u32[]{:S(2)}, u32[]{:S(2)}) collective-permute-start(bf16[80,2176]{1,0:T(8,128)(2,1)S(1)} %get-tuple-element.9), channel_id=1, source_target_pairs={{0,3},{1,0},{2,1},{3,2},{4,7},{5,4},{6,5},{7,6},{8,11},{9,8},{10,9... | collective-permute-start | bytes 1044488 | tf_op jit(solution)/shard_map/ppermute | solution.py:44
  175.4 3.3 %collective-permute-done.10 = bf16[80,2176]{1,0:T(8,128)(2,1)S(1)} collective-permute-done((bf16[80,2176]{1,0:T(8,128)(2,1)S(1)}, bf16[80,2176]{1,0:T(8,128)(2,1)S(1)}, u32[]{:S(2)}, u32[]{:S(2)}) %collective-permute-start.10) | collective-permute-done | bytes 348192 | tf_op jit(solution)/shard_map/ppermute | solution.py:44
  182.9 2.7 collective-permute-start.11
  185.6 9.5 %collective-permute-done.14 = bf16[160,2048]{1,0:T(8,128)(2,1)} collective-permute-done((bf16[160,2048]{1,0:T(8,128)(2,1)S(1)}, bf16[160,2048]{1,0:T(8,128)(2,1)}, u32[]{:S(2)}, u32[]{:S(2)}) %collective-permute-start.14) | collective-permute-done | bytes 655392 | tf_op jit(solution)/shard_map/ppermute | solution.py:49
  198.4 8.0 %all-to-all-start.3 = ((bf16[16,8,2560]{2,1,0:T(8,128)(2,1)}), bf16[16,8,2560]{2,1,0:T(8,128)(2,1)}, u32[]{:S(2)}, u32[]{:S(2)}) async-start(bf16[16,8,2560]{2,1,0:T(8,128)(2,1)} %reshape.84), calls=%async_computation.3 | async-start | bytes 1310720 | tf_op jit(solution)/shard_map/all_to_all | solution.py:170
  206.4 3.6 %collective-permute-done.9 = bf16[160,2176]{1,0:T(8,128)(2,1)} collective-permute-done((bf16[160,2176]{1,0:T(8,128)(2,1)}, bf16[160,2176]{1,0:T(8,128)(2,1)}, u32[]{:S(2)}, u32[]{:S(2)}) %collective-permute-start.9) | collective-permute-done | bytes 696352 | tf_op jit(solution)/shard_map/ppermute | solution.py:49
  217.5 9.1 %all-to-all-done.3 = bf16[16,8,2560]{2,1,0:T(8,128)(2,1)} async-done(((bf16[16,8,2560]{2,1,0:T(8,128)(2,1)}), bf16[16,8,2560]{2,1,0:T(8,128)(2,1)}, u32[]{:S(2)}, u32[]{:S(2)}) %all-to-all-start.3) | async-done | bytes 655392 | tf_op jit(solution)/shard_map/all_to_all | solution.py:170
  226.6 4.3 %all-to-all-start.2 = ((bf16[16,8,2688]{2,1,0:T(8,128)(2,1)}), bf16[16,8,2688]{2,1,0:T(8,128)(2,1)}, u32[]{:S(2)}, u32[]{:S(2)}) async-start(bf16[16,8,2688]{2,1,0:T(8,128)(2,1)} %fusion.23), calls=%async_computation.2 | async-start | bytes 1376256 | tf_op jit(solution)/shard_map/all_to_all | solution.py:170
  230.9 5.2 %fusion.2 = bf16[1,1,192,4096]{3,2,1,0:T(8,128)(2,1)} fusion(bf16[640,192]{0,1:T(8,128)(2,1)S(1)} %get-tuple-element.17, bf16[640,4096]{1,0:T(8,128)(2,1)} %copy-done.1), kind=kOutput, calls=%fused_computation.11 | convolution fusion | flops 1007419392 | bytes 7061504 | tf_op jit(solution)/shard_map/dot_general | solution.py:147
  238.6 2.6 fusion.3
  244.6 5.9 %all-to-all-done.2 = bf16[16,8,2688]{2,1,0:T(8,128)(2,1)} async-done(((bf16[16,8,2688]{2,1,0:T(8,128)(2,1)}), bf16[16,8,2688]{2,1,0:T(8,128)(2,1)}, u32[]{:S(2)}, u32[]{:S(2)}) %all-to-all-start.2) | async-done | bytes 688160 | tf_op jit(solution)/shard_map/all_to_all | solution.py:170
  255.6 3.5 %collective-permute-done.17 = bf16[128,2048]{1,0:T(8,128)(2,1)} collective-permute-done((bf16[128,2048]{1,0:T(8,128)(2,1)S(1)}, bf16[128,2048]{1,0:T(8,128)(2,1)}, u32[]{:S(2)}, u32[]{:S(2)}) %collective-permute-start.17) | collective-permute-done | bytes 524320 | tf_op jit(solution)/shard_map/ppermute | solution.py:10
  259.1 10.4 %collective-permute-done.12 = bf16[128,2048]{1,0:T(8,128)(2,1)S(1)} collective-permute-done((bf16[128,2048]{1,0:T(8,128)(2,1)S(1)}, bf16[128,2048]{1,0:T(8,128)(2,1)S(1)}, u32[]{:S(2)}, u32[]{:S(2)}) %collective-permute-start.12) | collective-permute-done | bytes 524320 | tf_op jit(solution)/shard_map/ppermute | solution.py:10
  (115 shorter events, 77.5 us)
Async XLA Ops:
  0.6 148.8 %copy-start = (bf16[1,1,192,4096]{3,2,1,0:T(8,128)(2,1)S(1)}, bf16[1,1,192,4096]{3,2,1,0:T(8,128)(2,1)}, u32[]{:S(2)}) copy-start(bf16[1,1,192,4096]{3,2,1,0:T(8,128)(2,1)} %param.13) | copy-start | bytes 4718596
  6.6 43.2 %all-to-all-start.1 = ((bf16[16,40,1024]{2,1,0:T(8,128)(2,1)}), bf16[16,40,1024]{2,1,0:T(8,128)(2,1)S(1)}, u32[]{:S(2)}, u32[]{:S(2)}) async-start(bf16[16,40,1024]{2,1,0:T(8,128)(2,1)} %reshape.80), calls=%async_computation.1 | async-start | bytes 2621440 | tf_op jit(solution)/shard_map/all_to_all | solution.py:104
  49.7 37.2 %all-to-all-start = ((bf16[16,40,1024]{2,1,0:T(8,128)(2,1)}), bf16[16,40,1024]{2,1,0:T(8,128)(2,1)}, u32[]{:S(2)}, u32[]{:S(2)}) async-start(bf16[16,40,1024]{2,1,0:T(8,128)(2,1)} %reshape.78), calls=%async_computation | async-start | bytes 2621440 | tf_op jit(solution)/shard_map/all_to_all | solution.py:109
  55.7 39.6 %collective-permute-start.4 = (bf16[160,4096]{1,0:T(8,128)(2,1)}, bf16[160,4096]{1,0:T(8,128)(2,1)}, u32[]{:S(2)}, u32[]{:S(2)}) collective-permute-start(bf16[160,4096]{1,0:T(8,128)(2,1)} %reshape.81), channel_id=1, source_target_pairs={{0,1},{1,2},{2,3},{3,0},{4,5},{5,6},{6,7},{7,4},{8,9},{9,10},{10,1... | collective-permute-start | bytes 3932168 | tf_op jit(solution)/shard_map/ppermute | solution.py:19
  57.0 39.5 %collective-permute-start.5 = (bf16[160,4096]{1,0:T(8,128)(2,1)}, bf16[160,4096]{1,0:T(8,128)(2,1)}, u32[]{:S(2)}, u32[]{:S(2)}) collective-permute-start(bf16[160,4096]{1,0:T(8,128)(2,1)} %reshape.81), channel_id=1, source_target_pairs={{0,3},{1,0},{2,1},{3,2},{4,7},{5,4},{6,5},{7,6},{8,11},{9,8},{10,9... | collective-permute-start | bytes 3932168 | tf_op jit(solution)/shard_map/ppermute | solution.py:20
  89.4 32.1 %collective-permute-start = (bf16[160,4096]{1,0:T(8,128)(2,1)S(1)}, bf16[160,4096]{1,0:T(8,128)(2,1)}, u32[]{:S(2)}, u32[]{:S(2)}) collective-permute-start(bf16[160,4096]{1,0:T(8,128)(2,1)S(1)} %reshape.79), channel_id=1, source_target_pairs={{0,1},{1,2},{2,3},{3,0},{4,5},{5,6},{6,7},{7,4},{8,9},{9,10},{10,1... | collective-permute-start | bytes 3932168 | tf_op jit(solution)/shard_map/ppermute | solution.py:19
  90.8 32.0 %collective-permute-start.1 = (bf16[160,4096]{1,0:T(8,128)(2,1)S(1)}, bf16[160,4096]{1,0:T(8,128)(2,1)}, u32[]{:S(2)}, u32[]{:S(2)}) collective-permute-start(bf16[160,4096]{1,0:T(8,128)(2,1)S(1)} %reshape.79), channel_id=1, source_target_pairs={{0,3},{1,0},{2,1},{3,2},{4,7},{5,4},{6,5},{7,6},{8,11},{9,8},{10,9... | collective-permute-start | bytes 3932168 | tf_op jit(solution)/shard_map/ppermute | solution.py:20
  96.4 39.2 %collective-permute-start.6 = (bf16[80,4096]{1,0:T(8,128)(2,1)S(1)}, bf16[80,4096]{1,0:T(8,128)(2,1)S(1)}, u32[]{:S(2)}, u32[]{:S(2)}) collective-permute-start(bf16[80,4096]{1,0:T(8,128)(2,1)S(1)} %slice.123), channel_id=1, source_target_pairs={{0,1},{1,2},{2,3},{3,0},{4,5},{5,6},{6,7},{7,4},{8,9},{9,10},{10,1... | collective-permute-start | bytes 1966088 | tf_op jit(solution)/shard_map/ppermute | solution.py:21
  97.6 38.0 %collective-permute-start.7 = (bf16[80,4096]{1,0:T(8,128)(2,1)S(1)}, bf16[80,4096]{1,0:T(8,128)(2,1)S(1)}, u32[]{:S(2)}, u32[]{:S(2)}) collective-permute-start(bf16[80,4096]{1,0:T(8,128)(2,1)S(1)} %slice.124), channel_id=1, source_target_pairs={{0,3},{1,0},{2,1},{3,2},{4,7},{5,4},{6,5},{7,6},{8,11},{9,8},{10,9... | collective-permute-start | bytes 1966088 | tf_op jit(solution)/shard_map/ppermute | solution.py:22
  122.6 26.2 %collective-permute-start.2 = (bf16[80,4096]{1,0:T(8,128)(2,1)S(1)}, bf16[80,4096]{1,0:T(8,128)(2,1)S(1)}, u32[]{:S(2)}, u32[]{:S(2)}) collective-permute-start(bf16[80,4096]{1,0:T(8,128)(2,1)S(1)} %slice.121), channel_id=1, source_target_pairs={{0,1},{1,2},{2,3},{3,0},{4,5},{5,6},{6,7},{7,4},{8,9},{9,10},{10,1... | collective-permute-start | bytes 1966088 | tf_op jit(solution)/shard_map/ppermute | solution.py:21
  124.0 25.3 %collective-permute-start.3 = (bf16[80,4096]{1,0:T(8,128)(2,1)S(1)}, bf16[80,4096]{1,0:T(8,128)(2,1)S(1)}, u32[]{:S(2)}, u32[]{:S(2)}) collective-permute-start(bf16[80,4096]{1,0:T(8,128)(2,1)S(1)} %slice.122), channel_id=1, source_target_pairs={{0,3},{1,0},{2,1},{3,2},{4,7},{5,4},{6,5},{7,6},{8,11},{9,8},{10,9... | collective-permute-start | bytes 1966088 | tf_op jit(solution)/shard_map/ppermute | solution.py:22
  154.4 17.1 %collective-permute-start.13 = (bf16[80,2048]{1,0:T(8,128)(2,1)S(1)}, bf16[80,2048]{1,0:T(8,128)(2,1)S(1)}, u32[]{:S(2)}, u32[]{:S(2)}) collective-permute-start(bf16[80,2048]{1,0:T(8,128)(2,1)S(1)} %get-tuple-element.13), channel_id=1, source_target_pairs={{0,1},{1,2},{2,3},{3,0},{4,5},{5,6},{6,7},{7,4},{8,9},{9,10},{10,1... | collective-permute-start | bytes 983048 | tf_op jit(solution)/shard_map/ppermute | solution.py:43
  155.8 15.7 %collective-permute-start.15 = (bf16[80,2048]{1,0:T(8,128)(2,1)S(1)}, bf16[80,2048]{1,0:T(8,128)(2,1)S(1)}, u32[]{:S(2)}, u32[]{:S(2)}) collective-permute-start(bf16[80,2048]{1,0:T(8,128)(2,1)S(1)} %get-tuple-element.15), channel_id=1, source_target_pairs={{0,3},{1,0},{2,1},{3,2},{4,7},{5,4},{6,5},{7,6},{8,11},{9,8},{10,9... | collective-permute-start | bytes 983048 | tf_op jit(solution)/shard_map/ppermute | solution.py:44
  160.2 20.7 %copy-start.3 = (bf16[640,2176]{1,0:T(8,128)(2,1)}, bf16[640,2176]{1,0:T(8,128)(2,1)S(1)}, u32[]{:S(2)}) copy-start(bf16[640,2176]{1,0:T(8,128)(2,1)S(1)} %fusion.4) | copy-start | bytes 8355844
  160.3 18.4 %collective-permute-start.10 = (bf16[80,2176]{1,0:T(8,128)(2,1)S(1)}, bf16[80,2176]{1,0:T(8,128)(2,1)S(1)}, u32[]{:S(2)}, u32[]{:S(2)}) collective-permute-start(bf16[80,2176]{1,0:T(8,128)(2,1)S(1)} %get-tuple-element.9), channel_id=1, source_target_pairs={{0,3},{1,0},{2,1},{3,2},{4,7},{5,4},{6,5},{7,6},{8,11},{9,8},{10,9... | collective-permute-start | bytes 1044488 | tf_op jit(solution)/shard_map/ppermute | solution.py:44
  171.3 9.6 %collective-permute-start.8 = (bf16[80,2176]{1,0:T(8,128)(2,1)S(1)}, bf16[80,2176]{1,0:T(8,128)(2,1)S(1)}, u32[]{:S(2)}, u32[]{:S(2)}) collective-permute-start(bf16[80,2176]{1,0:T(8,128)(2,1)S(1)} %get-tuple-element.7), channel_id=1, source_target_pairs={{0,1},{1,2},{2,3},{3,0},{4,5},{5,6},{6,7},{7,4},{8,9},{9,10},{10,1... | collective-permute-start | bytes 1044488 | tf_op jit(solution)/shard_map/ppermute | solution.py:43
  171.7 23.4 %collective-permute-start.14 = (bf16[160,2048]{1,0:T(8,128)(2,1)S(1)}, bf16[160,2048]{1,0:T(8,128)(2,1)}, u32[]{:S(2)}, u32[]{:S(2)}) collective-permute-start(bf16[160,2048]{1,0:T(8,128)(2,1)S(1)} %pad_maximum_fusion.2), channel_id=1, source_target_pairs={{0,1},{1,2},{2,3},{3,0},{4,5},{5,6},{6,7},{7,4},{8,9},{9,10},{10,1... | collective-permute-start | bytes 1966088 | tf_op jit(solution)/shard_map/ppermute | solution.py:49
  172.8 22.3 %collective-permute-start.16 = (bf16[160,2048]{1,0:T(8,128)(2,1)}, bf16[160,2048]{1,0:T(8,128)(2,1)}, u32[]{:S(2)}, u32[]{:S(2)}) collective-permute-start(bf16[160,2048]{1,0:T(8,128)(2,1)} %pad_maximum_fusion.3), channel_id=1, source_target_pairs={{0,3},{1,0},{2,1},{3,2},{4,7},{5,4},{6,5},{7,6},{8,11},{9,8},{10,9... | collective-permute-start | bytes 1966088 | tf_op jit(solution)/shard_map/ppermute | solution.py:50
  182.0 28.0 %collective-permute-start.9 = (bf16[160,2176]{1,0:T(8,128)(2,1)}, bf16[160,2176]{1,0:T(8,128)(2,1)}, u32[]{:S(2)}, u32[]{:S(2)}) collective-permute-start(bf16[160,2176]{1,0:T(8,128)(2,1)} %pad_maximum_fusion), channel_id=1, source_target_pairs={{0,1},{1,2},{2,3},{3,0},{4,5},{5,6},{6,7},{7,4},{8,9},{9,10},{10,1... | collective-permute-start | bytes 2088968 | tf_op jit(solution)/shard_map/ppermute | solution.py:49
  182.9 27.1 %collective-permute-start.11 = (bf16[160,2176]{1,0:T(8,128)(2,1)}, bf16[160,2176]{1,0:T(8,128)(2,1)}, u32[]{:S(2)}, u32[]{:S(2)}) collective-permute-start(bf16[160,2176]{1,0:T(8,128)(2,1)} %pad_maximum_fusion.1), channel_id=1, source_target_pairs={{0,3},{1,0},{2,1},{3,2},{4,7},{5,4},{6,5},{7,6},{8,11},{9,8},{10,9... | collective-permute-start | bytes 2088968 | tf_op jit(solution)/shard_map/ppermute | solution.py:50
  198.4 28.2 %all-to-all-start.3 = ((bf16[16,8,2560]{2,1,0:T(8,128)(2,1)}), bf16[16,8,2560]{2,1,0:T(8,128)(2,1)}, u32[]{:S(2)}, u32[]{:S(2)}) async-start(bf16[16,8,2560]{2,1,0:T(8,128)(2,1)} %reshape.84), calls=%async_computation.3 | async-start | bytes 1310720 | tf_op jit(solution)/shard_map/all_to_all | solution.py:170
  226.6 23.9 %all-to-all-start.2 = ((bf16[16,8,2688]{2,1,0:T(8,128)(2,1)}), bf16[16,8,2688]{2,1,0:T(8,128)(2,1)}, u32[]{:S(2)}, u32[]{:S(2)}) async-start(bf16[16,8,2688]{2,1,0:T(8,128)(2,1)} %fusion.23), calls=%async_computation.2 | async-start | bytes 1376256 | tf_op jit(solution)/shard_map/all_to_all | solution.py:170
  243.3 15.8 %collective-permute-start.17 = (bf16[128,2048]{1,0:T(8,128)(2,1)S(1)}, bf16[128,2048]{1,0:T(8,128)(2,1)}, u32[]{:S(2)}, u32[]{:S(2)}) collective-permute-start(bf16[128,2048]{1,0:T(8,128)(2,1)S(1)} %convolution_convert_fusion.5), channel_id=1, source_target_pairs={{64,0},{128,64},{192,128},{65,1},{129,65},{193,129},{66,2},{130,66... | collective-permute-start | bytes 1572872 | tf_op jit(solution)/shard_map/ppermute | solution.py:10
  252.6 16.9 %collective-permute-start.12 = (bf16[128,2048]{1,0:T(8,128)(2,1)S(1)}, bf16[128,2048]{1,0:T(8,128)(2,1)S(1)}, u32[]{:S(2)}, u32[]{:S(2)}) collective-permute-start(bf16[128,2048]{1,0:T(8,128)(2,1)S(1)} %convolution_convert_fusion.6), channel_id=1, source_target_pairs={{64,0},{128,64},{192,128},{65,1},{129,65},{193,129},{66,2},{130,66... | collective-permute-start | bytes 1572872 | tf_op jit(solution)/shard_map/ppermute | solution.py:10
  (10 other events, 71.9 us)

commit v9 on v8

--- a/solution.py
+++ b/solution.py
@@ -20,13 +20,8 @@
     from_right = lax.ppermute(piece, axis, bwd)
     far_top = lax.ppermute(from_left[:half], axis, fwd)
     far_bottom = lax.ppermute(from_right[half:], axis, bwd)
-    whole = jnp.zeros((size * rows,) + piece.shape[1:], piece.dtype)
-    whole = lax.dynamic_update_slice_in_dim(whole, piece, me * rows, 0)
-    whole = lax.dynamic_update_slice_in_dim(whole, from_left, ((me - 1) % size) * rows, 0)
-    whole = lax.dynamic_update_slice_in_dim(whole, from_right, ((me + 1) % size) * rows, 0)
     far = jnp.concatenate([far_top, far_bottom], axis=0)
-    whole = lax.dynamic_update_slice_in_dim(whole, far, ((me + 2) % size) * rows, 0)
-    return whole
+    return jnp.concatenate([piece, from_right, far, from_left], axis=0)
 
 
 def ring_reduce_scatter(parts, axis, me):
@@ -36,19 +31,19 @@
     fwd = [(k, (k + 1) % size) for k in range(size)]
     bwd = [(k, (k - 1) % size) for k in range(size)]
 
-    def block(t):
-        return lax.dynamic_slice_in_dim(parts, (t % size) * rows, rows, 0)
-
-    far = block(me + 2)
+    def block(offset):
+        return parts[offset * rows : (offset + 1) * rows]
+
+    far = block(2)
     got_top = lax.ppermute(far[:half], axis, fwd)
     got_bottom = lax.ppermute(far[half:], axis, bwd)
-    to_right = block(me + 1).astype(jnp.float32)
+    to_right = block(1).astype(jnp.float32)
     to_right = jnp.concatenate([to_right[:half] + got_top.astype(jnp.float32), to_right[half:]])
-    to_left = block(me - 1).astype(jnp.float32)
+    to_left = block(size - 1).astype(jnp.float32)
     to_left = jnp.concatenate([to_left[:half], to_left[half:] + got_bottom.astype(jnp.float32)])
     from_left = lax.ppermute(to_right.astype(jnp.bfloat16), axis, fwd)
     from_right = lax.ppermute(to_left.astype(jnp.bfloat16), axis, bwd)
-    total = block(me).astype(jnp.float32) + from_left.astype(jnp.float32)
+    total = block(0).astype(jnp.float32) + from_left.astype(jnp.float32)
     total = total + from_right.astype(jnp.float32)
     return total.astype(jnp.bfloat16)
 
@@ -109,16 +104,16 @@
         dy_e = lax.all_to_all(dense_chunks(local_dy[:, cols], experts), "expert", 0, 0, tiled=True)
         dy_e = dy_e.reshape(experts * capacity, width)
         rows_grad.append(ring_gather(dy_e, "dp", my_group))
-    gate_pre = 0.0
-    up_pre = 0.0
-    for q in range(pieces):
-        cols = slice(q * width, (q + 1) * width)
-        gate_pre = gate_pre + lax.dot_general(
-            rows_x[q], gate_mat[:, cols], feature_contract, preferred_element_type=jnp.float32
+    both_mat = jnp.concatenate([gate_mat, up_mat], axis=0)
+    hidden = gate_mat.shape[0]
+    both_pre = 0.0
+    for q in range(pieces):
+        cols = slice(q * width, (q + 1) * width)
+        both_pre = both_pre + lax.dot_general(
+            rows_x[q], both_mat[:, cols], feature_contract, preferred_element_type=jnp.float32
         )
-        up_pre = up_pre + lax.dot_general(
-            rows_x[q], up_mat[:, cols], feature_contract, preferred_element_type=jnp.float32
-        )
+    gate_pre = both_pre[:, :hidden]
+    up_pre = both_pre[:, hidden:]
     gate_sig = jax.nn.sigmoid(gate_pre)
     activated = (gate_pre * gate_sig * up_pre).astype(jnp.bfloat16)
     row_score = 0.0
@@ -134,6 +129,7 @@
         jnp.bfloat16
     )
     pre_up = (hidden_grad * gate_pre * gate_sig).astype(jnp.bfloat16)
+    pre_both = jnp.concatenate([pre_gate, pre_up], axis=1)
     grad_down = []
     grad_gate = []
     grad_up = []
@@ -141,12 +137,11 @@
         grad_down.append(lax.dot_general(
             activated, rows_grad[q], token_contract, preferred_element_type=jnp.float32
         ).astype(jnp.bfloat16))
-        grad_gate.append(lax.dot_general(
-            pre_gate, rows_x[q], token_contract, preferred_element_type=jnp.float32
-        ).astype(jnp.bfloat16))
-        grad_up.append(lax.dot_general(
-            pre_up, rows_x[q], token_contract, preferred_element_type=jnp.float32
-        ).astype(jnp.bfloat16))
+        grad_both = lax.dot_general(
+            pre_both, rows_x[q], token_contract, preferred_element_type=jnp.float32
+        ).astype(jnp.bfloat16)
+        grad_gate.append(grad_both[:hidden])
+        grad_up.append(grad_both[hidden:])
     grad_down = jnp.concatenate(grad_down, axis=1)
     grad_gate = jnp.concatenate(grad_gate, axis=1)
     grad_up = jnp.concatenate(grad_up, axis=1)
@@ -155,8 +150,7 @@
     handed = []
     for q in range(back_pieces):
         cols = slice(q * back_width, (q + 1) * back_width)
-        partial_in = jnp.dot(pre_gate, gate_mat[:, cols], preferred_element_type=jnp.float32)
-        partial_in = partial_in + jnp.dot(pre_up, up_mat[:, cols], preferred_element_type=jnp.float32)
+        partial_in = jnp.dot(pre_both, both_mat[:, cols], preferred_element_type=jnp.float32)
         if q == 0:
             score_cols = jnp.pad(row_score[:, None], ((0, 0), (0, 127)))
             partial_in = jnp.concatenate([partial_in, score_cols], axis=1)

time: 276 us -> 267 us (0.967); the launches traced: 272 us -> 266 us
  waiting for transfers between devices: 136 us -> 155 us
  starting transfers between devices: 60.1 us -> 47.9 us
  local copies, waits for them, and re-layouts: 32.4 us -> 25.7 us
  other arithmetic: 15.4 us -> 11.9 us
    ppermute x2, waiting for transfers between devices: 11.2 us -> 22.6 us  [ring_gather(): far_top = lax.ppermute(from_left[:half], axis, fwd)]
    ppermute x2, starting transfers between devices: 12.4 us -> 2.95 us  [ring_reduce_scatter(): got_bottom = lax.ppermute(far[half:], axis, bwd)]
    dynamic_update_slice x6 -> x0, local copies, waits for them, and re-layouts: 7.59 us -> none  [the longest x2 3.04 us: ring_gather(): lax.dynamic_update_slice_in_dim(whole, from_right, (me + 1) % size * rows...]
    all_to_all x2, waiting for transfers between devices: 14.9 us -> 20.6 us  [per_device(): back = lax.all_to_all(body, 'expert', 0, 0, tiled=True)]
    all_to_all x1, starting transfers between devices: 4.29 us -> 9.98 us  [per_device(): lax.all_to_all(dense_chunks(local_dy[:, cols], experts), 'expert', 0, 0,...]
    all_to_all x1, starting transfers between devices: 9.98 us -> 4.29 us  [per_device(): lax.all_to_all(dense_chunks(local_x[:, cols], experts), 'expert', 0, 0, t...]
    dot_general x8 -> x4, matrix products: 15.1 us -> 9.7 us  [the longest x1 3.98 us: per_device(): lax.dot_general(pre_both, rows_x[q], token_contract, preferred_element_ty...]
    unnamed x24, local copies, waits for them, and re-layouts: 0.68 us -> 4.51 us
  transfers between devices with their start and end apart: 22 -> 22, of which waited for: 15 -> 13; matrix products, arithmetic and copies ran while one was open for 22% -> 17% of each run, Pallas kernels for 0% -> 0%
where the time goes in v9:
time: 267 us; the launch traced here: 266 us
  waiting for transfers between devices  155 us (58%)
  starting transfers between devices  47.9 us (18%)
  local copies, waits for them, and re-layouts  25.7 us (10%)
  matrix products  24.6 us (9%)
  other arithmetic  11.9 us (4%)
    all_to_all x1, waiting for transfers between devices, per_device(): lax.all_to_all(dense_chunks(local_x[:, cols], experts), 'expert', 0, 0, t...  28.5 us
    all_to_all x1, waiting for transfers between devices, per_device(): lax.all_to_all(dense_chunks(local_dy[:, cols], experts), 'expert', 0, 0,...  27 us
    ppermute x2, waiting for transfers between devices, ring_gather(): far_top = lax.ppermute(from_left[:half], axis, fwd)  22.6 us
    ppermute x2, waiting for transfers between devices, ring_gather(): from_left = lax.ppermute(piece, axis, fwd)  22.5 us
    all_to_all x2, waiting for transfers between devices, per_device(): back = lax.all_to_all(body, 'expert', 0, 0, tiled=True)  20.6 us
    ppermute x2, waiting for transfers between devices, from_behind(): return lax.ppermute(shard, axis, pairs)  12.5 us
    ppermute x2, waiting for transfers between devices, ring_reduce_scatter(): from_left = lax.ppermute(to_right.astype(jnp.bfloat16), axis, fwd)  12.2 us
    all_to_all x1, starting transfers between devices, per_device(): lax.all_to_all(dense_chunks(local_dy[:, cols], experts), 'expert', 0, 0,...  9.98 us
  transfers between devices with their start and end apart: 22, of which 13 were waited for; matrix products, arithmetic and copies ran while one was open for 17% of the time, Pallas kernels for 0%

profile of v9, /device:TPU:1, one launch (start us, length us, event | category | flops | bytes accessed | tf_op | source)
XLA Modules:
  0.0 265.9 jit_solution(11331057853080204287)
XLA Ops:
  8.1 10.0 %all-to-all-start = ((bf16[16,40,1024]{2,1,0:T(8,128)(2,1)}), bf16[16,40,1024]{2,1,0:T(8,128)(2,1)S(1)}, u32[]{:S(2)}, u32[]{:S(2)}) async-start(bf16[16,40,1024]{2,1,0:T(8,128)(2,1)} %reshape.78), calls=%async_computation | async-start | bytes 2621440 | tf_op jit(solution)/shard_map/all_to_all | solution.py:104
  18.0 2.8 %convolution_convert_fusion.2 = bf16[160,4096]{1,0:T(8,128)(2,1)} fusion(bf16[1,128,4096]{2,1,0:T(8,128)(2,1)} %param.7, s32[128]{0:T(128)S(1)} %multiply_add_fusion), kind=kOutput, calls=%fused_computation.5 | convolution fusion | flops 168448000 | bytes 2359808 | tf_op jit(solution)/shard_map/dot_general | solution.py:87
  20.8 3.4 %reshape.80 = bf16[16,40,1024]{2,1,0:T(8,128)(2,1)} reshape(bf16[160,4096]{1,0:T(8,128)(2,1)} %convolution_convert_fusion.2) | data formatting | bytes 2621440 | tf_op jit(solution)/shard_map/reshape | solution.py:65
  24.2 27.0 %all-to-all-done = bf16[16,40,1024]{2,1,0:T(8,128)(2,1)S(1)} async-done(((bf16[16,40,1024]{2,1,0:T(8,128)(2,1)}), bf16[16,40,1024]{2,1,0:T(8,128)(2,1)S(1)}, u32[]{:S(2)}, u32[]{:S(2)}) %all-to-all-start) | async-done | bytes 1310752 | tf_op jit(solution)/shard_map/all_to_all | solution.py:104
  51.2 4.3 %all-to-all-start.1 = ((bf16[16,40,1024]{2,1,0:T(8,128)(2,1)}), bf16[16,40,1024]{2,1,0:T(8,128)(2,1)}, u32[]{:S(2)}, u32[]{:S(2)}) async-start(bf16[16,40,1024]{2,1,0:T(8,128)(2,1)} %reshape.80), calls=%async_computation.1 | async-start | bytes 2621440 | tf_op jit(solution)/shard_map/all_to_all | solution.py:99
  59.9 28.5 %all-to-all-done.1 = bf16[16,40,1024]{2,1,0:T(8,128)(2,1)} async-done(((bf16[16,40,1024]{2,1,0:T(8,128)(2,1)}), bf16[16,40,1024]{2,1,0:T(8,128)(2,1)}, u32[]{:S(2)}, u32[]{:S(2)}) %all-to-all-start.1) | async-done | bytes 1310752 | tf_op jit(solution)/shard_map/all_to_all | solution.py:99
  88.4 2.5 reshape.81
  97.8 2.7 %collective-permute-start.3 = (bf16[80,4096]{1,0:T(8,128)(2,1)S(1)}, bf16[80,4096]{1,0:T(8,128)(2,1)S(1)}, u32[]{:S(2)}, u32[]{:S(2)}) collective-permute-start(bf16[80,4096]{1,0:T(8,128)(2,1)S(1)} %slice.156), channel_id=1, source_target_pairs={{0,3},{1,0},{2,1},{3,2},{4,7},{5,4},{6,5},{7,6},{8,11},{9,8},{10,9... | collective-permute-start | bytes 1966088 | tf_op jit(solution)/shard_map/ppermute | solution.py:22
  100.5 22.5 %collective-permute-done.5 = bf16[160,4096]{1,0:T(8,128)(2,1)S(1)} collective-permute-done((bf16[160,4096]{1,0:T(8,128)(2,1)S(1)}, bf16[160,4096]{1,0:T(8,128)(2,1)S(1)}, u32[]{:S(2)}, u32[]{:S(2)}) %collective-permute-start.5) | collective-permute-done | bytes 1310752 | tf_op jit(solution)/shard_map/ppermute | solution.py:19
  123.2 2.9 %collective-permute-start.7 = (bf16[80,4096]{1,0:T(8,128)(2,1)S(1)}, bf16[80,4096]{1,0:T(8,128)(2,1)S(1)}, u32[]{:S(2)}, u32[]{:S(2)}) collective-permute-start(bf16[80,4096]{1,0:T(8,128)(2,1)S(1)} %slice.158), channel_id=1, source_target_pairs={{0,3},{1,0},{2,1},{3,2},{4,7},{5,4},{6,5},{7,6},{8,11},{9,8},{10,9... | collective-permute-start | bytes 1966088 | tf_op jit(solution)/shard_map/ppermute | solution.py:22
  127.7 22.6 %collective-permute-done.6 = bf16[80,4096]{1,0:T(8,128)(2,1)S(1)} collective-permute-done((bf16[80,4096]{1,0:T(8,128)(2,1)S(1)}, bf16[80,4096]{1,0:T(8,128)(2,1)S(1)}, u32[]{:S(2)}, u32[]{:S(2)}) %collective-permute-start.6) | collective-permute-done | bytes 655392 | tf_op jit(solution)/shard_map/ppermute | solution.py:21
  152.3 2.6 fusion.2
  168.1 3.9 %collective-permute-done.13 = bf16[80,2048]{1,0:T(8,128)(2,1)S(1)} collective-permute-done((bf16[80,2048]{1,0:T(8,128)(2,1)S(1)}, bf16[80,2048]{1,0:T(8,128)(2,1)S(1)}, u32[]{:S(2)}, u32[]{:S(2)}) %collective-permute-start.13) | collective-permute-done | bytes 327712 | tf_op jit(solution)/shard_map/ppermute | solution.py:38
  172.8 2.4 collective-permute-start.16
  175.2 3.3 %collective-permute-done.10 = bf16[80,2176]{1,0:T(8,128)(2,1)S(1)} collective-permute-done((bf16[80,2176]{1,0:T(8,128)(2,1)S(1)}, bf16[80,2176]{1,0:T(8,128)(2,1)S(1)}, u32[]{:S(2)}, u32[]{:S(2)}) %collective-permute-start.10) | collective-permute-done | bytes 348192 | tf_op jit(solution)/shard_map/ppermute | solution.py:39
  184.2 4.0 %convolution_convert_fusion = bf16[384,4096]{1,0:T(8,128)(2,1)} fusion(bf16[640,4096]{1,0:T(8,128)(2,1)S(1)} %constant_dynamic-update-slice_fusion.5, bf16[640,192]{0,1:T(8,128)(2,1)S(1)} %get-tuple-element.20, bf16[640,192]{0,1:T(8,128)(2,1)S(1)} %get-tuple-element.19), kind=kOutput, calls=%fused_computation.1 | convolution fusion | flops 2015821824 | bytes 8880128 | tf_op jit(solution)/shard_map/dot_general | solution.py:140
  188.1 5.4 %collective-permute-done.14 = bf16[160,2048]{1,0:T(8,128)(2,1)S(1)} collective-permute-done((bf16[160,2048]{1,0:T(8,128)(2,1)S(1)}, bf16[160,2048]{1,0:T(8,128)(2,1)S(1)}, u32[]{:S(2)}, u32[]{:S(2)}) %collective-permute-start.14) | collective-permute-done | bytes 655392 | tf_op jit(solution)/shard_map/ppermute | solution.py:44
  195.3 6.3 %all-to-all-start.3 = ((bf16[16,8,2560]{2,1,0:T(8,128)(2,1)}), bf16[16,8,2560]{2,1,0:T(8,128)(2,1)S(1)}, u32[]{:S(2)}, u32[]{:S(2)}) async-start(bf16[16,8,2560]{2,1,0:T(8,128)(2,1)} %reshape.84), calls=%async_computation.3 | async-start | bytes 1310720 | tf_op jit(solution)/shard_map/all_to_all | solution.py:164
  201.7 6.8 %collective-permute-done.9 = bf16[160,2176]{1,0:T(8,128)(2,1)S(1)} collective-permute-done((bf16[160,2176]{1,0:T(8,128)(2,1)}, bf16[160,2176]{1,0:T(8,128)(2,1)S(1)}, u32[]{:S(2)}, u32[]{:S(2)}) %collective-permute-start.9) | collective-permute-done | bytes 696352 | tf_op jit(solution)/shard_map/ppermute | solution.py:44
  211.7 10.0 %all-to-all-done.3 = bf16[16,8,2560]{2,1,0:T(8,128)(2,1)S(1)} async-done(((bf16[16,8,2560]{2,1,0:T(8,128)(2,1)}), bf16[16,8,2560]{2,1,0:T(8,128)(2,1)S(1)}, u32[]{:S(2)}, u32[]{:S(2)}) %all-to-all-start.3) | async-done | bytes 655392 | tf_op jit(solution)/shard_map/all_to_all | solution.py:164
  221.7 3.5 %all-to-all-start.2 = ((bf16[16,8,2688]{2,1,0:T(8,128)(2,1)}), bf16[16,8,2688]{2,1,0:T(8,128)(2,1)S(1)}, u32[]{:S(2)}, u32[]{:S(2)}) async-start(bf16[16,8,2688]{2,1,0:T(8,128)(2,1)} %fusion.20), calls=%async_computation.2 | async-start | bytes 1376256 | tf_op jit(solution)/shard_map/all_to_all | solution.py:164
  225.2 5.2 %fusion.1 = bf16[1,1,192,4096]{3,2,1,0:T(8,128)(2,1)} fusion(bf16[640,192]{0,1:T(8,128)(2,1)S(1)} %get-tuple-element.21, bf16[640,4096]{1,0:T(8,128)(2,1)} %copy-done.2), kind=kOutput, calls=%fused_computation.7 | convolution fusion | flops 1007419392 | bytes 7061504 | tf_op jit(solution)/shard_map/dot_general | solution.py:137
  234.7 10.6 %all-to-all-done.2 = bf16[16,8,2688]{2,1,0:T(8,128)(2,1)S(1)} async-done(((bf16[16,8,2688]{2,1,0:T(8,128)(2,1)}), bf16[16,8,2688]{2,1,0:T(8,128)(2,1)S(1)}, u32[]{:S(2)}, u32[]{:S(2)}) %all-to-all-start.2) | async-done | bytes 688160 | tf_op jit(solution)/shard_map/all_to_all | solution.py:164
  251.3 12.5 %collective-permute-done.12 = bf16[128,2048]{1,0:T(8,128)(2,1)S(1)} collective-permute-done((bf16[128,2048]{1,0:T(8,128)(2,1)}, bf16[128,2048]{1,0:T(8,128)(2,1)S(1)}, u32[]{:S(2)}, u32[]{:S(2)}) %collective-permute-start.12) | collective-permute-done | bytes 524320 | tf_op jit(solution)/shard_map/ppermute | solution.py:10
  (102 shorter events, 59.0 us)
Async XLA Ops:
  0.6 155.8 %copy-start = (bf16[1,1,192,4096]{3,2,1,0:T(8,128)(2,1)S(1)}, bf16[1,1,192,4096]{3,2,1,0:T(8,128)(2,1)}, u32[]{:S(2)}) copy-start(bf16[1,1,192,4096]{3,2,1,0:T(8,128)(2,1)} %param.13) | copy-start | bytes 4718596
  8.1 43.2 %all-to-all-start = ((bf16[16,40,1024]{2,1,0:T(8,128)(2,1)}), bf16[16,40,1024]{2,1,0:T(8,128)(2,1)S(1)}, u32[]{:S(2)}, u32[]{:S(2)}) async-start(bf16[16,40,1024]{2,1,0:T(8,128)(2,1)} %reshape.78), calls=%async_computation | async-start | bytes 2621440 | tf_op jit(solution)/shard_map/all_to_all | solution.py:104
  51.2 37.2 %all-to-all-start.1 = ((bf16[16,40,1024]{2,1,0:T(8,128)(2,1)}), bf16[16,40,1024]{2,1,0:T(8,128)(2,1)}, u32[]{:S(2)}, u32[]{:S(2)}) async-start(bf16[16,40,1024]{2,1,0:T(8,128)(2,1)} %reshape.80), calls=%async_computation.1 | async-start | bytes 2621440 | tf_op jit(solution)/shard_map/all_to_all | solution.py:99
  57.2 38.2 %collective-permute-start.1 = (bf16[160,4096]{1,0:T(8,128)(2,1)}, bf16[160,4096]{1,0:T(8,128)(2,1)}, u32[]{:S(2)}, u32[]{:S(2)}) collective-permute-start(bf16[160,4096]{1,0:T(8,128)(2,1)} %reshape.79), channel_id=1, source_target_pairs={{0,1},{1,2},{2,3},{3,0},{4,5},{5,6},{6,7},{7,4},{8,9},{9,10},{10,1... | collective-permute-start | bytes 3932168 | tf_op jit(solution)/shard_map/ppermute | solution.py:19
  58.5 38.1 %collective-permute-start = (bf16[160,4096]{1,0:T(8,128)(2,1)}, bf16[160,4096]{1,0:T(8,128)(2,1)}, u32[]{:S(2)}, u32[]{:S(2)}) collective-permute-start(bf16[160,4096]{1,0:T(8,128)(2,1)} %reshape.79), channel_id=1, source_target_pairs={{0,3},{1,0},{2,1},{3,2},{4,7},{5,4},{6,5},{7,6},{8,11},{9,8},{10,9... | collective-permute-start | bytes 3932168 | tf_op jit(solution)/shard_map/ppermute | solution.py:20
  90.9 32.1 %collective-permute-start.5 = (bf16[160,4096]{1,0:T(8,128)(2,1)S(1)}, bf16[160,4096]{1,0:T(8,128)(2,1)S(1)}, u32[]{:S(2)}, u32[]{:S(2)}) collective-permute-start(bf16[160,4096]{1,0:T(8,128)(2,1)S(1)} %reshape.81), channel_id=1, source_target_pairs={{0,1},{1,2},{2,3},{3,0},{4,5},{5,6},{6,7},{7,4},{8,9},{9,10},{10,1... | collective-permute-start | bytes 3932168 | tf_op jit(solution)/shard_map/ppermute | solution.py:19
  92.3 30.9 %collective-permute-start.4 = (bf16[160,4096]{1,0:T(8,128)(2,1)S(1)}, bf16[160,4096]{1,0:T(8,128)(2,1)S(1)}, u32[]{:S(2)}, u32[]{:S(2)}) collective-permute-start(bf16[160,4096]{1,0:T(8,128)(2,1)S(1)} %reshape.81), channel_id=1, source_target_pairs={{0,3},{1,0},{2,1},{3,2},{4,7},{5,4},{6,5},{7,6},{8,11},{9,8},{10,9... | collective-permute-start | bytes 3932168 | tf_op jit(solution)/shard_map/ppermute | solution.py:20
  96.5 54.5 %collective-permute-start.2 = (bf16[80,4096]{1,0:T(8,128)(2,1)S(1)}, bf16[80,4096]{1,0:T(8,128)(2,1)S(1)}, u32[]{:S(2)}, u32[]{:S(2)}) collective-permute-start(bf16[80,4096]{1,0:T(8,128)(2,1)S(1)} %slice.155), channel_id=1, source_target_pairs={{0,1},{1,2},{2,3},{3,0},{4,5},{5,6},{6,7},{7,4},{8,9},{9,10},{10,1... | collective-permute-start | bytes 1966088 | tf_op jit(solution)/shard_map/ppermute | solution.py:21
  97.8 57.2 %collective-permute-start.3 = (bf16[80,4096]{1,0:T(8,128)(2,1)S(1)}, bf16[80,4096]{1,0:T(8,128)(2,1)S(1)}, u32[]{:S(2)}, u32[]{:S(2)}) collective-permute-start(bf16[80,4096]{1,0:T(8,128)(2,1)S(1)} %slice.156), channel_id=1, source_target_pairs={{0,3},{1,0},{2,1},{3,2},{4,7},{5,4},{6,5},{7,6},{8,11},{9,8},{10,9... | collective-permute-start | bytes 1966088 | tf_op jit(solution)/shard_map/ppermute | solution.py:22
  123.1 27.3 %collective-permute-start.6 = (bf16[80,4096]{1,0:T(8,128)(2,1)S(1)}, bf16[80,4096]{1,0:T(8,128)(2,1)S(1)}, u32[]{:S(2)}, u32[]{:S(2)}) collective-permute-start(bf16[80,4096]{1,0:T(8,128)(2,1)S(1)} %slice.157), channel_id=1, source_target_pairs={{0,1},{1,2},{2,3},{3,0},{4,5},{5,6},{6,7},{7,4},{8,9},{9,10},{10,1... | collective-permute-start | bytes 1966088 | tf_op jit(solution)/shard_map/ppermute | solution.py:21
  123.2 27.6 %collective-permute-start.7 = (bf16[80,4096]{1,0:T(8,128)(2,1)S(1)}, bf16[80,4096]{1,0:T(8,128)(2,1)S(1)}, u32[]{:S(2)}, u32[]{:S(2)}) collective-permute-start(bf16[80,4096]{1,0:T(8,128)(2,1)S(1)} %slice.158), channel_id=1, source_target_pairs={{0,3},{1,0},{2,1},{3,2},{4,7},{5,4},{6,5},{7,6},{8,11},{9,8},{10,9... | collective-permute-start | bytes 1966088 | tf_op jit(solution)/shard_map/ppermute | solution.py:22
  161.7 10.4 %collective-permute-start.13 = (bf16[80,2048]{1,0:T(8,128)(2,1)S(1)}, bf16[80,2048]{1,0:T(8,128)(2,1)S(1)}, u32[]{:S(2)}, u32[]{:S(2)}) collective-permute-start(bf16[80,2048]{1,0:T(8,128)(2,1)S(1)} %get-tuple-element.15), channel_id=1, source_target_pairs={{0,1},{1,2},{2,3},{3,0},{4,5},{5,6},{6,7},{7,4},{8,9},{9,10},{10,1... | collective-permute-start | bytes 983048 | tf_op jit(solution)/shard_map/ppermute | solution.py:38
  162.1 9.9 %collective-permute-start.15 = (bf16[80,2048]{1,0:T(8,128)(2,1)S(1)}, bf16[80,2048]{1,0:T(8,128)(2,1)S(1)}, u32[]{:S(2)}, u32[]{:S(2)}) collective-permute-start(bf16[80,2048]{1,0:T(8,128)(2,1)S(1)} %get-tuple-element.16), channel_id=1, source_target_pairs={{0,3},{1,0},{2,1},{3,2},{4,7},{5,4},{6,5},{7,6},{8,11},{9,8},{10,9... | collective-permute-start | bytes 983048 | tf_op jit(solution)/shard_map/ppermute | solution.py:39
  166.6 11.9 %collective-permute-start.10 = (bf16[80,2176]{1,0:T(8,128)(2,1)S(1)}, bf16[80,2176]{1,0:T(8,128)(2,1)S(1)}, u32[]{:S(2)}, u32[]{:S(2)}) collective-permute-start(bf16[80,2176]{1,0:T(8,128)(2,1)S(1)} %get-tuple-element.10), channel_id=1, source_target_pairs={{0,3},{1,0},{2,1},{3,2},{4,7},{5,4},{6,5},{7,6},{8,11},{9,8},{10,9... | collective-permute-start | bytes 1044488 | tf_op jit(solution)/shard_map/ppermute | solution.py:39
  167.3 12.2 %collective-permute-start.8 = (bf16[80,2176]{1,0:T(8,128)(2,1)S(1)}, bf16[80,2176]{1,0:T(8,128)(2,1)S(1)}, u32[]{:S(2)}, u32[]{:S(2)}) collective-permute-start(bf16[80,2176]{1,0:T(8,128)(2,1)S(1)} %get-tuple-element.9), channel_id=1, source_target_pairs={{0,1},{1,2},{2,3},{3,0},{4,5},{5,6},{6,7},{7,4},{8,9},{9,10},{10,1... | collective-permute-start | bytes 1044488 | tf_op jit(solution)/shard_map/ppermute | solution.py:38
  172.3 21.2 %collective-permute-start.14 = (bf16[160,2048]{1,0:T(8,128)(2,1)S(1)}, bf16[160,2048]{1,0:T(8,128)(2,1)S(1)}, u32[]{:S(2)}, u32[]{:S(2)}) collective-permute-start(bf16[160,2048]{1,0:T(8,128)(2,1)S(1)} %pad_maximum_fusion.4), channel_id=1, source_target_pairs={{0,1},{1,2},{2,3},{3,0},{4,5},{5,6},{6,7},{7,4},{8,9},{9,10},{10,1... | collective-permute-start | bytes 1966088 | tf_op jit(solution)/shard_map/ppermute | solution.py:44
  172.8 20.7 %collective-permute-start.16 = (bf16[160,2048]{1,0:T(8,128)(2,1)S(1)}, bf16[160,2048]{1,0:T(8,128)(2,1)S(1)}, u32[]{:S(2)}, u32[]{:S(2)}) collective-permute-start(bf16[160,2048]{1,0:T(8,128)(2,1)S(1)} %pad_maximum_fusion.5), channel_id=1, source_target_pairs={{0,3},{1,0},{2,1},{3,2},{4,7},{5,4},{6,5},{7,6},{8,11},{9,8},{10,9... | collective-permute-start | bytes 1966088 | tf_op jit(solution)/shard_map/ppermute | solution.py:45
  180.6 27.9 %collective-permute-start.9 = (bf16[160,2176]{1,0:T(8,128)(2,1)}, bf16[160,2176]{1,0:T(8,128)(2,1)S(1)}, u32[]{:S(2)}, u32[]{:S(2)}) collective-permute-start(bf16[160,2176]{1,0:T(8,128)(2,1)} %pad_maximum_fusion.2), channel_id=1, source_target_pairs={{0,1},{1,2},{2,3},{3,0},{4,5},{5,6},{6,7},{7,4},{8,9},{9,10},{10,1... | collective-permute-start | bytes 2088968 | tf_op jit(solution)/shard_map/ppermute | solution.py:44
  181.9 26.6 %collective-permute-start.11 = (bf16[160,2176]{1,0:T(8,128)(2,1)}, bf16[160,2176]{1,0:T(8,128)(2,1)S(1)}, u32[]{:S(2)}, u32[]{:S(2)}) collective-permute-start(bf16[160,2176]{1,0:T(8,128)(2,1)} %pad_maximum_fusion.3), channel_id=1, source_target_pairs={{0,3},{1,0},{2,1},{3,2},{4,7},{5,4},{6,5},{7,6},{8,11},{9,8},{10,9... | collective-permute-start | bytes 2088968 | tf_op jit(solution)/shard_map/ppermute | solution.py:45
  195.3 26.3 %all-to-all-start.3 = ((bf16[16,8,2560]{2,1,0:T(8,128)(2,1)}), bf16[16,8,2560]{2,1,0:T(8,128)(2,1)S(1)}, u32[]{:S(2)}, u32[]{:S(2)}) async-start(bf16[16,8,2560]{2,1,0:T(8,128)(2,1)} %reshape.84), calls=%async_computation.3 | async-start | bytes 1310720 | tf_op jit(solution)/shard_map/all_to_all | solution.py:164
  221.7 23.7 %all-to-all-start.2 = ((bf16[16,8,2688]{2,1,0:T(8,128)(2,1)}), bf16[16,8,2688]{2,1,0:T(8,128)(2,1)S(1)}, u32[]{:S(2)}, u32[]{:S(2)}) async-start(bf16[16,8,2688]{2,1,0:T(8,128)(2,1)} %fusion.20), calls=%async_computation.2 | async-start | bytes 1376256 | tf_op jit(solution)/shard_map/all_to_all | solution.py:164
  233.4 17.9 %collective-permute-start.17 = (bf16[128,2048]{1,0:T(8,128)(2,1)S(1)}, bf16[128,2048]{1,0:T(8,128)(2,1)}, u32[]{:S(2)}, u32[]{:S(2)}) collective-permute-start(bf16[128,2048]{1,0:T(8,128)(2,1)S(1)} %convolution_convert_fusion.6), channel_id=1, source_target_pairs={{64,0},{128,64},{192,128},{65,1},{129,65},{193,129},{66,2},{130,66... | collective-permute-start | bytes 1572872 | tf_op jit(solution)/shard_map/ppermute | solution.py:10
  245.4 20.5 %copy-start.1 = (bf16[1,1,192,4096]{3,2,1,0:T(8,128)(2,1)S(1)}, bf16[1,1,192,4096]{3,2,1,0:T(8,128)(2,1)}, u32[]{:S(2)}) copy-start(bf16[1,1,192,4096]{3,2,1,0:T(8,128)(2,1)} %param.13) | copy-start | bytes 4718596
  249.1 14.7 %collective-permute-start.12 = (bf16[128,2048]{1,0:T(8,128)(2,1)}, bf16[128,2048]{1,0:T(8,128)(2,1)S(1)}, u32[]{:S(2)}, u32[]{:S(2)}) collective-permute-start(bf16[128,2048]{1,0:T(8,128)(2,1)} %convolution_convert_fusion.7), channel_id=1, source_target_pairs={{64,0},{128,64},{192,128},{65,1},{129,65},{193,129},{66,2},{130,66... | collective-permute-start | bytes 1572872 | tf_op jit(solution)/shard_map/ppermute | solution.py:10
  (6 other events, 47.1 us)

commit v10 on v9

--- a/solution.py
+++ b/solution.py
@@ -145,11 +145,13 @@
     grad_down = jnp.concatenate(grad_down, axis=1)
     grad_gate = jnp.concatenate(grad_gate, axis=1)
     grad_up = jnp.concatenate(grad_up, axis=1)
-    back_pieces = 2
-    back_width = model_width // back_pieces
+    unit = model_width // 8
+    back_widths = [4 * unit, 3 * unit, unit]
     handed = []
-    for q in range(back_pieces):
-        cols = slice(q * back_width, (q + 1) * back_width)
+    offset = 0
+    for q, back_width in enumerate(back_widths):
+        cols = slice(offset, offset + back_width)
+        offset += back_width
         partial_in = jnp.dot(pre_both, both_mat[:, cols], preferred_element_type=jnp.float32)
         if q == 0:
             score_cols = jnp.pad(row_score[:, None], ((0, 0), (0, 127)))

time: 267 us -> 292 us (1.094)
  starting transfers between devices: 47.9 us -> 69.3 us
  waiting for transfers between devices: 155 us -> 144 us
  local copies, waits for them, and re-layouts: 25.7 us -> 33.5 us
  other arithmetic: 11.9 us -> 16.5 us
    ppermute x2 -> x3, waiting for transfers between devices: 12.2 us -> 0.01 us  [ring_reduce_scatter(): from_left = lax.ppermute(to_right.astype(jnp.bfloat16), axis, fwd)]
    ppermute x2 -> x3, starting transfers between devices: 2.95 us -> 14.8 us  [ring_reduce_scatter(): got_bottom = lax.ppermute(far[half:], axis, bwd)]
    all_to_all x2 -> x3, waiting for transfers between devices: 20.6 us -> 26 us  [per_device(): back = lax.all_to_all(body, 'expert', 0, 0, tiled=True)]
    all_to_all x2 -> x3, starting transfers between devices: 9.81 us -> 14.6 us  [per_device(): back = lax.all_to_all(body, 'expert', 0, 0, tiled=True)]
    reshape x2 -> x3, local copies, waits for them, and re-layouts: 2.11 us -> 5.77 us  [per_device(): body = summed[:, :back_width].reshape(experts, 8, span)]
    ppermute x2 -> x3, waiting for transfers between devices: 4.87 us -> 1.22 us  [ring_reduce_scatter(): got_top = lax.ppermute(far[:half], axis, fwd)]
    ppermute x2 -> x3, starting transfers between devices: 4.64 us -> 8.02 us  [ring_reduce_scatter(): from_right = lax.ppermute(to_left.astype(jnp.bfloat16), axis, bwd)]
    convert_element_type x2 -> x3, other arithmetic: 1.68 us -> 4.66 us  [ring_reduce_scatter(): return total.astype(jnp.bfloat16)]
  transfers between devices with their start and end apart: 22 -> 28, of which waited for: 13 -> 12; matrix products, arithmetic and copies ran while one was open for 17% -> 16% of each run, Pallas kernels for 0% -> 0%
where the time goes in v10:
time: 292 us; the launch traced here: 288 us
  waiting for transfers between devices  144 us (49%)
  starting transfers between devices  69.3 us (24%)
  local copies, waits for them, and re-layouts  33.5 us (11%)
  matrix products  22.9 us (8%)
  other arithmetic  16.5 us (6%)
    all_to_all x1, waiting for transfers between devices, per_device(): lax.all_to_all(dense_chunks(local_x[:, cols], experts), 'expert', 0, 0, t...  28.5 us
    all_to_all x1, waiting for transfers between devices, per_device(): lax.all_to_all(dense_chunks(local_dy[:, cols], experts), 'expert', 0, 0,...  27 us
    all_to_all x3, waiting for transfers between devices, per_device(): back = lax.all_to_all(body, 'expert', 0, 0, tiled=True)  26 us
    ppermute x2, waiting for transfers between devices, ring_gather(): far_top = lax.ppermute(from_left[:half], axis, fwd)  22.6 us
    ppermute x2, waiting for transfers between devices, ring_gather(): from_left = lax.ppermute(piece, axis, fwd)  22.5 us
    ppermute x3, starting transfers between devices, ring_reduce_scatter(): got_bottom = lax.ppermute(far[half:], axis, bwd)  14.8 us
    all_to_all x3, starting transfers between devices, per_device(): back = lax.all_to_all(body, 'expert', 0, 0, tiled=True)  14.6 us
    ppermute x3, waiting for transfers between devices, from_behind(): return lax.ppermute(shard, axis, pairs)  12.3 us
  transfers between devices with their start and end apart: 28, of which 12 were waited for; matrix products, arithmetic and copies ran while one was open for 16% of the time, Pallas kernels for 0%

profile of v10, /device:TPU:1, one launch (start us, length us, event | category | flops | bytes accessed | tf_op | source)
XLA Modules:
  0.0 288.1 jit_solution(14804147148643443938)
XLA Ops:
  8.6 10.0 %all-to-all-start = ((bf16[16,40,1024]{2,1,0:T(8,128)(2,1)}), bf16[16,40,1024]{2,1,0:T(8,128)(2,1)S(1)}, u32[]{:S(2)}, u32[]{:S(2)}) async-start(bf16[16,40,1024]{2,1,0:T(8,128)(2,1)} %reshape.84), calls=%async_computation | async-start | bytes 2621440 | tf_op jit(solution)/shard_map/all_to_all | solution.py:104
  18.5 2.8 convolution_convert_fusion.2
  21.3 3.4 %reshape.86 = bf16[16,40,1024]{2,1,0:T(8,128)(2,1)} reshape(bf16[160,4096]{1,0:T(8,128)(2,1)} %convolution_convert_fusion.2) | data formatting | bytes 2621440 | tf_op jit(solution)/shard_map/reshape | solution.py:65
  24.7 27.0 %all-to-all-done = bf16[16,40,1024]{2,1,0:T(8,128)(2,1)S(1)} async-done(((bf16[16,40,1024]{2,1,0:T(8,128)(2,1)}), bf16[16,40,1024]{2,1,0:T(8,128)(2,1)S(1)}, u32[]{:S(2)}, u32[]{:S(2)}) %all-to-all-start) | async-done | bytes 1310752 | tf_op jit(solution)/shard_map/all_to_all | solution.py:104
  51.7 4.3 %all-to-all-start.1 = ((bf16[16,40,1024]{2,1,0:T(8,128)(2,1)}), bf16[16,40,1024]{2,1,0:T(8,128)(2,1)}, u32[]{:S(2)}, u32[]{:S(2)}) async-start(bf16[16,40,1024]{2,1,0:T(8,128)(2,1)} %reshape.86), calls=%async_computation.1 | async-start | bytes 2621440 | tf_op jit(solution)/shard_map/all_to_all | solution.py:99
  60.4 28.5 %all-to-all-done.1 = bf16[16,40,1024]{2,1,0:T(8,128)(2,1)} async-done(((bf16[16,40,1024]{2,1,0:T(8,128)(2,1)}), bf16[16,40,1024]{2,1,0:T(8,128)(2,1)}, u32[]{:S(2)}, u32[]{:S(2)}) %all-to-all-start.1) | async-done | bytes 1310752 | tf_op jit(solution)/shard_map/all_to_all | solution.py:99
  98.3 2.7 collective-permute-start.3
  101.0 22.5 %collective-permute-done.5 = bf16[160,4096]{1,0:T(8,128)(2,1)S(1)} collective-permute-done((bf16[160,4096]{1,0:T(8,128)(2,1)S(1)}, bf16[160,4096]{1,0:T(8,128)(2,1)S(1)}, u32[]{:S(2)}, u32[]{:S(2)}) %collective-permute-start.5) | collective-permute-done | bytes 1310752 | tf_op jit(solution)/shard_map/ppermute | solution.py:19
  123.7 3.0 %collective-permute-start.7 = (bf16[80,4096]{1,0:T(8,128)(2,1)S(1)}, bf16[80,4096]{1,0:T(8,128)(2,1)S(1)}, u32[]{:S(2)}, u32[]{:S(2)}) collective-permute-start(bf16[80,4096]{1,0:T(8,128)(2,1)S(1)} %slice.209), channel_id=1, source_target_pairs={{0,3},{1,0},{2,1},{3,2},{4,7},{5,4},{6,5},{7,6},{8,11},{9,8},{10,9... | collective-permute-start | bytes 1966088 | tf_op jit(solution)/shard_map/ppermute | solution.py:22
  128.3 22.6 %collective-permute-done.6 = bf16[80,4096]{1,0:T(8,128)(2,1)S(1)} collective-permute-done((bf16[80,4096]{1,0:T(8,128)(2,1)S(1)}, bf16[80,4096]{1,0:T(8,128)(2,1)S(1)}, u32[]{:S(2)}, u32[]{:S(2)}) %collective-permute-start.6) | collective-permute-done | bytes 655392 | tf_op jit(solution)/shard_map/ppermute | solution.py:21
  152.8 2.6 fusion.2
  158.9 4.0 %convolution_convert_fusion = bf16[384,4096]{1,0:T(8,128)(2,1)} fusion(bf16[640,4096]{1,0:T(8,128)(2,1)S(1)} %constant_dynamic-update-slice_fusion.5, bf16[640,192]{0,1:T(8,128)(2,1)S(1)} %get-tuple-element.20, bf16[640,192]{0,1:T(8,128)(2,1)S(1)} %get-tuple-element.19), kind=kOutput, calls=%fused_computation.1 | convolution fusion | flops 2015821824 | bytes 8880128 | tf_op jit(solution)/shard_map/dot_general | solution.py:140
  171.0 12.1 %collective-permute-start.15 = (bf16[80,1536]{1,0:T(8,128)(2,1)S(1)}, bf16[80,1536]{1,0:T(8,128)(2,1)S(1)}, u32[]{:S(2)}, u32[]{:S(2)}) collective-permute-start(bf16[80,1536]{1,0:T(8,128)(2,1)S(1)} %get-tuple-element.16), channel_id=1, source_target_pairs={{0,3},{1,0},{2,1},{3,2},{4,7},{5,4},{6,5},{7,6},{8,11},{9,8},{10,9... | collective-permute-start | bytes 737288 | tf_op jit(solution)/shard_map/ppermute | solution.py:39
  183.2 2.7 collective-permute-start.20
  197.2 3.3 %collective-permute-start.16 = (bf16[160,1536]{1,0:T(8,128)(2,1)}, bf16[160,1536]{1,0:T(8,128)(2,1)}, u32[]{:S(2)}, u32[]{:S(2)}) collective-permute-start(bf16[160,1536]{1,0:T(8,128)(2,1)} %pad_maximum_fusion.6), channel_id=1, source_target_pairs={{0,3},{1,0},{2,1},{3,2},{4,7},{5,4},{6,5},{7,6},{8,11},{9,8},{10,9... | collective-permute-start | bytes 1474568 | tf_op jit(solution)/shard_map/ppermute | solution.py:45
  202.5 2.7 collective-permute-start.11
  207.7 7.6 %all-to-all-start.4 = ((bf16[16,8,640]{2,1,0:T(8,128)(2,1)}), bf16[16,8,640]{2,1,0:T(8,128)(2,1)}, u32[]{:S(2)}, u32[]{:S(2)}) async-start(bf16[16,8,640]{2,1,0:T(8,128)(2,1)} %reshape.92), calls=%async_computation.4 | async-start | bytes 327680 | tf_op jit(solution)/shard_map/all_to_all | solution.py:166
  219.8 5.3 %all-to-all-done.4 = bf16[16,8,640]{2,1,0:T(8,128)(2,1)} async-done(((bf16[16,8,640]{2,1,0:T(8,128)(2,1)}), bf16[16,8,640]{2,1,0:T(8,128)(2,1)}, u32[]{:S(2)}, u32[]{:S(2)}) %all-to-all-start.4) | async-done | bytes 163872 | tf_op jit(solution)/shard_map/all_to_all | solution.py:166
  225.1 3.5 %all-to-all-start.3 = ((bf16[16,8,1920]{2,1,0:T(8,128)(2,1)}), bf16[16,8,1920]{2,1,0:T(8,128)(2,1)S(1)}, u32[]{:S(2)}, u32[]{:S(2)}) async-start(bf16[16,8,1920]{2,1,0:T(8,128)(2,1)} %reshape.90), calls=%async_computation.3 | async-start | bytes 983040 | tf_op jit(solution)/shard_map/all_to_all | solution.py:166
  234.1 10.7 %all-to-all-done.3 = bf16[16,8,1920]{2,1,0:T(8,128)(2,1)S(1)} async-done(((bf16[16,8,1920]{2,1,0:T(8,128)(2,1)}), bf16[16,8,1920]{2,1,0:T(8,128)(2,1)S(1)}, u32[]{:S(2)}, u32[]{:S(2)}) %all-to-all-start.3) | async-done | bytes 491552 | tf_op jit(solution)/shard_map/all_to_all | solution.py:166
  244.8 3.5 %all-to-all-start.2 = ((bf16[16,8,2688]{2,1,0:T(8,128)(2,1)}), bf16[16,8,2688]{2,1,0:T(8,128)(2,1)S(1)}, u32[]{:S(2)}, u32[]{:S(2)}) async-start(bf16[16,8,2688]{2,1,0:T(8,128)(2,1)} %fusion.20), calls=%async_computation.2 | async-start | bytes 1376256 | tf_op jit(solution)/shard_map/all_to_all | solution.py:166
  248.3 3.9 %slice_bitcast_fusion = (bf16[1,1,192,4096]{3,2,1,0:T(8,128)(2,1)}, bf16[1,1,192,4096]{3,2,1,0:T(8,128)(2,1)}) fusion(bf16[384,4096]{1,0:T(8,128)(2,1)} %convolution_convert_fusion), kind=kLoop, calls=%fused_computation.24 | loop fusion | bytes 6291456 | tf_op jit(solution)/shard_map/broadcast_in_dim | solution.py:184
  258.3 10.0 %all-to-all-done.2 = bf16[16,8,2688]{2,1,0:T(8,128)(2,1)S(1)} async-done(((bf16[16,8,2688]{2,1,0:T(8,128)(2,1)}), bf16[16,8,2688]{2,1,0:T(8,128)(2,1)S(1)}, u32[]{:S(2)}, u32[]{:S(2)}) %all-to-all-start.2) | async-done | bytes 688160 | tf_op jit(solution)/shard_map/all_to_all | solution.py:166
  273.6 12.2 %collective-permute-done.12 = bf16[128,2048]{1,0:T(8,128)(2,1)S(1)} collective-permute-done((bf16[128,2048]{1,0:T(8,128)(2,1)S(1)}, bf16[128,2048]{1,0:T(8,128)(2,1)S(1)}, u32[]{:S(2)}, u32[]{:S(2)}) %collective-permute-start.12) | collective-permute-done | bytes 524320 | tf_op jit(solution)/shard_map/ppermute | solution.py:10
  (121 shorter events, 75.9 us)
Async XLA Ops:
  8.6 43.2 %all-to-all-start = ((bf16[16,40,1024]{2,1,0:T(8,128)(2,1)}), bf16[16,40,1024]{2,1,0:T(8,128)(2,1)S(1)}, u32[]{:S(2)}, u32[]{:S(2)}) async-start(bf16[16,40,1024]{2,1,0:T(8,128)(2,1)} %reshape.84), calls=%async_computation | async-start | bytes 2621440 | tf_op jit(solution)/shard_map/all_to_all | solution.py:104
  51.7 37.2 %all-to-all-start.1 = ((bf16[16,40,1024]{2,1,0:T(8,128)(2,1)}), bf16[16,40,1024]{2,1,0:T(8,128)(2,1)}, u32[]{:S(2)}, u32[]{:S(2)}) async-start(bf16[16,40,1024]{2,1,0:T(8,128)(2,1)} %reshape.86), calls=%async_computation.1 | async-start | bytes 2621440 | tf_op jit(solution)/shard_map/all_to_all | solution.py:99
  57.7 38.2 %collective-permute-start.1 = (bf16[160,4096]{1,0:T(8,128)(2,1)}, bf16[160,4096]{1,0:T(8,128)(2,1)}, u32[]{:S(2)}, u32[]{:S(2)}) collective-permute-start(bf16[160,4096]{1,0:T(8,128)(2,1)} %reshape.85), channel_id=1, source_target_pairs={{0,1},{1,2},{2,3},{3,0},{4,5},{5,6},{6,7},{7,4},{8,9},{9,10},{10,1... | collective-permute-start | bytes 3932168 | tf_op jit(solution)/shard_map/ppermute | solution.py:19
  59.0 38.2 %collective-permute-start = (bf16[160,4096]{1,0:T(8,128)(2,1)}, bf16[160,4096]{1,0:T(8,128)(2,1)}, u32[]{:S(2)}, u32[]{:S(2)}) collective-permute-start(bf16[160,4096]{1,0:T(8,128)(2,1)} %reshape.85), channel_id=1, source_target_pairs={{0,3},{1,0},{2,1},{3,2},{4,7},{5,4},{6,5},{7,6},{8,11},{9,8},{10,9... | collective-permute-start | bytes 3932168 | tf_op jit(solution)/shard_map/ppermute | solution.py:20
  91.4 32.1 %collective-permute-start.5 = (bf16[160,4096]{1,0:T(8,128)(2,1)S(1)}, bf16[160,4096]{1,0:T(8,128)(2,1)S(1)}, u32[]{:S(2)}, u32[]{:S(2)}) collective-permute-start(bf16[160,4096]{1,0:T(8,128)(2,1)S(1)} %reshape.87), channel_id=1, source_target_pairs={{0,1},{1,2},{2,3},{3,0},{4,5},{5,6},{6,7},{7,4},{8,9},{9,10},{10,1... | collective-permute-start | bytes 3932168 | tf_op jit(solution)/shard_map/ppermute | solution.py:19
  92.8 30.9 %collective-permute-start.4 = (bf16[160,4096]{1,0:T(8,128)(2,1)S(1)}, bf16[160,4096]{1,0:T(8,128)(2,1)S(1)}, u32[]{:S(2)}, u32[]{:S(2)}) collective-permute-start(bf16[160,4096]{1,0:T(8,128)(2,1)S(1)} %reshape.87), channel_id=1, source_target_pairs={{0,3},{1,0},{2,1},{3,2},{4,7},{5,4},{6,5},{7,6},{8,11},{9,8},{10,9... | collective-permute-start | bytes 3932168 | tf_op jit(solution)/shard_map/ppermute | solution.py:20
  97.0 54.4 %collective-permute-start.2 = (bf16[80,4096]{1,0:T(8,128)(2,1)S(1)}, bf16[80,4096]{1,0:T(8,128)(2,1)S(1)}, u32[]{:S(2)}, u32[]{:S(2)}) collective-permute-start(bf16[80,4096]{1,0:T(8,128)(2,1)S(1)} %slice.206), channel_id=1, source_target_pairs={{0,1},{1,2},{2,3},{3,0},{4,5},{5,6},{6,7},{7,4},{8,9},{9,10},{10,1... | collective-permute-start | bytes 1966088 | tf_op jit(solution)/shard_map/ppermute | solution.py:21
  98.3 57.1 %collective-permute-start.3 = (bf16[80,4096]{1,0:T(8,128)(2,1)S(1)}, bf16[80,4096]{1,0:T(8,128)(2,1)S(1)}, u32[]{:S(2)}, u32[]{:S(2)}) collective-permute-start(bf16[80,4096]{1,0:T(8,128)(2,1)S(1)} %slice.207), channel_id=1, source_target_pairs={{0,3},{1,0},{2,1},{3,2},{4,7},{5,4},{6,5},{7,6},{8,11},{9,8},{10,9... | collective-permute-start | bytes 1966088 | tf_op jit(solution)/shard_map/ppermute | solution.py:22
  123.6 27.3 %collective-permute-start.6 = (bf16[80,4096]{1,0:T(8,128)(2,1)S(1)}, bf16[80,4096]{1,0:T(8,128)(2,1)S(1)}, u32[]{:S(2)}, u32[]{:S(2)}) collective-permute-start(bf16[80,4096]{1,0:T(8,128)(2,1)S(1)} %slice.208), channel_id=1, source_target_pairs={{0,1},{1,2},{2,3},{3,0},{4,5},{5,6},{6,7},{7,4},{8,9},{9,10},{10,1... | collective-permute-start | bytes 1966088 | tf_op jit(solution)/shard_map/ppermute | solution.py:21
  123.7 27.6 %collective-permute-start.7 = (bf16[80,4096]{1,0:T(8,128)(2,1)S(1)}, bf16[80,4096]{1,0:T(8,128)(2,1)S(1)}, u32[]{:S(2)}, u32[]{:S(2)}) collective-permute-start(bf16[80,4096]{1,0:T(8,128)(2,1)S(1)} %slice.209), channel_id=1, source_target_pairs={{0,3},{1,0},{2,1},{3,2},{4,7},{5,4},{6,5},{7,6},{8,11},{9,8},{10,9... | collective-permute-start | bytes 1966088 | tf_op jit(solution)/shard_map/ppermute | solution.py:22
  170.5 20.8 %collective-permute-start.13 = (bf16[80,1536]{1,0:T(8,128)(2,1)S(1)}, bf16[80,1536]{1,0:T(8,128)(2,1)S(1)}, u32[]{:S(2)}, u32[]{:S(2)}) collective-permute-start(bf16[80,1536]{1,0:T(8,128)(2,1)S(1)} %get-tuple-element.15), channel_id=1, source_target_pairs={{0,1},{1,2},{2,3},{3,0},{4,5},{5,6},{6,7},{7,4},{8,9},{9,10},{10,1... | collective-permute-start | bytes 737288 | tf_op jit(solution)/shard_map/ppermute | solution.py:38
  171.0 22.3 %collective-permute-start.15 = (bf16[80,1536]{1,0:T(8,128)(2,1)S(1)}, bf16[80,1536]{1,0:T(8,128)(2,1)S(1)}, u32[]{:S(2)}, u32[]{:S(2)}) collective-permute-start(bf16[80,1536]{1,0:T(8,128)(2,1)S(1)} %get-tuple-element.16), channel_id=1, source_target_pairs={{0,3},{1,0},{2,1},{3,2},{4,7},{5,4},{6,5},{7,6},{8,11},{9,8},{10,9... | collective-permute-start | bytes 737288 | tf_op jit(solution)/shard_map/ppermute | solution.py:39
  187.7 12.8 %collective-permute-start.8 = (bf16[80,2176]{1,0:T(8,128)(2,1)S(1)}, bf16[80,2176]{1,0:T(8,128)(2,1)S(1)}, u32[]{:S(2)}, u32[]{:S(2)}) collective-permute-start(bf16[80,2176]{1,0:T(8,128)(2,1)S(1)} %get-tuple-element.9), channel_id=1, source_target_pairs={{0,1},{1,2},{2,3},{3,0},{4,5},{5,6},{6,7},{7,4},{8,9},{9,10},{10,1... | collective-permute-start | bytes 1044488 | tf_op jit(solution)/shard_map/ppermute | solution.py:38
  191.3 13.9 %collective-permute-start.21 = (bf16[160,512]{1,0:T(8,128)(2,1)S(1)}, bf16[160,512]{1,0:T(8,128)(2,1)S(1)}, u32[]{:S(2)}, u32[]{:S(2)}) collective-permute-start(bf16[160,512]{1,0:T(8,128)(2,1)S(1)} %pad_maximum_fusion.8), channel_id=1, source_target_pairs={{0,3},{1,0},{2,1},{3,2},{4,7},{5,4},{6,5},{7,6},{8,11},{9,8},{10,9... | collective-permute-start | bytes 491528 | tf_op jit(solution)/shard_map/ppermute | solution.py:45
  194.3 21.0 %collective-permute-start.14 = (bf16[160,1536]{1,0:T(8,128)(2,1)}, bf16[160,1536]{1,0:T(8,128)(2,1)}, u32[]{:S(2)}, u32[]{:S(2)}) collective-permute-start(bf16[160,1536]{1,0:T(8,128)(2,1)} %pad_maximum_fusion.5), channel_id=1, source_target_pairs={{0,1},{1,2},{2,3},{3,0},{4,5},{5,6},{6,7},{7,4},{8,9},{9,10},{10,1... | collective-permute-start | bytes 1474568 | tf_op jit(solution)/shard_map/ppermute | solution.py:44
  197.2 18.1 %collective-permute-start.16 = (bf16[160,1536]{1,0:T(8,128)(2,1)}, bf16[160,1536]{1,0:T(8,128)(2,1)}, u32[]{:S(2)}, u32[]{:S(2)}) collective-permute-start(bf16[160,1536]{1,0:T(8,128)(2,1)} %pad_maximum_fusion.6), channel_id=1, source_target_pairs={{0,3},{1,0},{2,1},{3,2},{4,7},{5,4},{6,5},{7,6},{8,11},{9,8},{10,9... | collective-permute-start | bytes 1474568 | tf_op jit(solution)/shard_map/ppermute | solution.py:45
  201.6 26.9 %collective-permute-start.9 = (bf16[160,2176]{1,0:T(8,128)(2,1)}, bf16[160,2176]{1,0:T(8,128)(2,1)}, u32[]{:S(2)}, u32[]{:S(2)}) collective-permute-start(bf16[160,2176]{1,0:T(8,128)(2,1)} %pad_maximum_fusion.2), channel_id=1, source_target_pairs={{0,1},{1,2},{2,3},{3,0},{4,5},{5,6},{6,7},{7,4},{8,9},{9,10},{10,1... | collective-permute-start | bytes 2088968 | tf_op jit(solution)/shard_map/ppermute | solution.py:44
  202.5 26.1 %collective-permute-start.11 = (bf16[160,2176]{1,0:T(8,128)(2,1)}, bf16[160,2176]{1,0:T(8,128)(2,1)}, u32[]{:S(2)}, u32[]{:S(2)}) collective-permute-start(bf16[160,2176]{1,0:T(8,128)(2,1)} %pad_maximum_fusion.3), channel_id=1, source_target_pairs={{0,3},{1,0},{2,1},{3,2},{4,7},{5,4},{6,5},{7,6},{8,11},{9,8},{10,9... | collective-permute-start | bytes 2088968 | tf_op jit(solution)/shard_map/ppermute | solution.py:45
  207.7 17.4 %all-to-all-start.4 = ((bf16[16,8,640]{2,1,0:T(8,128)(2,1)}), bf16[16,8,640]{2,1,0:T(8,128)(2,1)}, u32[]{:S(2)}, u32[]{:S(2)}) async-start(bf16[16,8,640]{2,1,0:T(8,128)(2,1)} %reshape.92), calls=%async_computation.4 | async-start | bytes 327680 | tf_op jit(solution)/shard_map/all_to_all | solution.py:166
  225.1 19.7 %all-to-all-start.3 = ((bf16[16,8,1920]{2,1,0:T(8,128)(2,1)}), bf16[16,8,1920]{2,1,0:T(8,128)(2,1)S(1)}, u32[]{:S(2)}, u32[]{:S(2)}) async-start(bf16[16,8,1920]{2,1,0:T(8,128)(2,1)} %reshape.90), calls=%async_computation.3 | async-start | bytes 983040 | tf_op jit(solution)/shard_map/all_to_all | solution.py:166
  244.8 23.6 %all-to-all-start.2 = ((bf16[16,8,2688]{2,1,0:T(8,128)(2,1)}), bf16[16,8,2688]{2,1,0:T(8,128)(2,1)S(1)}, u32[]{:S(2)}, u32[]{:S(2)}) async-start(bf16[16,8,2688]{2,1,0:T(8,128)(2,1)} %fusion.20), calls=%async_computation.2 | async-start | bytes 1376256 | tf_op jit(solution)/shard_map/all_to_all | solution.py:166
  254.2 19.4 %collective-permute-start.22 = (bf16[128,512]{1,0:T(8,128)(2,1)}, bf16[128,512]{1,0:T(8,128)(2,1)}, u32[]{:S(2)}, u32[]{:S(2)}) collective-permute-start(bf16[128,512]{1,0:T(8,128)(2,1)} %convolution_convert_fusion.9), channel_id=1, source_target_pairs={{64,0},{128,64},{192,128},{65,1},{129,65},{193,129},{66,2},{130,66... | collective-permute-start | bytes 393224 | tf_op jit(solution)/shard_map/ppermute | solution.py:10
  257.0 16.5 %collective-permute-start.17 = (bf16[128,1536]{1,0:T(8,128)(2,1)}, bf16[128,1536]{1,0:T(8,128)(2,1)}, u32[]{:S(2)}, u32[]{:S(2)}) collective-permute-start(bf16[128,1536]{1,0:T(8,128)(2,1)} %convolution_convert_fusion.6), channel_id=1, source_target_pairs={{64,0},{128,64},{192,128},{65,1},{129,65},{193,129},{66,2},{130,66... | collective-permute-start | bytes 1179656 | tf_op jit(solution)/shard_map/ppermute | solution.py:10
  271.3 14.5 %collective-permute-start.12 = (bf16[128,2048]{1,0:T(8,128)(2,1)S(1)}, bf16[128,2048]{1,0:T(8,128)(2,1)S(1)}, u32[]{:S(2)}, u32[]{:S(2)}) collective-permute-start(bf16[128,2048]{1,0:T(8,128)(2,1)S(1)} %convolution_convert_fusion.7), channel_id=1, source_target_pairs={{64,0},{128,64},{192,128},{65,1},{129,65},{193,129},{66,2},{130,66... | collective-permute-start | bytes 1572872 | tf_op jit(solution)/shard_map/ppermute | solution.py:10
  (11 other events, 242.8 us)

commit v11 on v9

--- a/solution.py
+++ b/solution.py
@@ -46,6 +46,15 @@
     total = block(0).astype(jnp.float32) + from_left.astype(jnp.float32)
     total = total + from_right.astype(jnp.float32)
     return total.astype(jnp.bfloat16)
+
+
+def slot_table(route_col, experts, capacity):
+    expert_ids = jnp.arange(experts, dtype=jnp.int32)
+    onehot = (route_col[:, None] == expert_ids).astype(jnp.int32)
+    earlier = jnp.cumsum(onehot, axis=0) - onehot
+    slot = jnp.sum(onehot * earlier, axis=1)
+    position = route_col * capacity + slot
+    return position[:, None] == jnp.arange(experts * capacity, dtype=jnp.int32)
 
 
 def route_tables(route_col, score_rows, experts, capacity):
@@ -81,6 +90,8 @@
     capacity = max(2, token_count * 5 // (4 * experts))
     weights, gate, table = route_tables(route_col, score_rows, experts, capacity)
     table_half = table.astype(jnp.bfloat16)
+    next_route = from_behind(route_col, "pipe", -1)
+    next_table = slot_table(next_route, experts, capacity).astype(jnp.bfloat16)
     token_contract = (((0,), (0,)), ((), ()))
     feature_contract = (((1,), (1,)), ((), ()))
     scaled = (gate[:, None] * upstream.astype(jnp.float32)).astype(jnp.bfloat16)
@@ -161,14 +172,17 @@
             tail = summed[:, back_width].reshape(experts, 1, capacity)
             tail = jnp.pad(tail, ((0, 0), (0, 7), (0, 128 - capacity)))
             body = jnp.concatenate([body, tail], axis=2)
+        last = q == back_pieces - 1
+        if last:
+            body = from_behind(body, "pipe", -1)
         back = lax.all_to_all(body, "expert", 0, 0, tiled=True)
         if q == 0:
             slot_score = back[:, 0, span : span + capacity]
         flat_in = back[:, :, :span].reshape(experts * capacity, back_width)
-        piece_grad = jnp.dot(table_half, flat_in, preferred_element_type=jnp.float32).astype(
-            jnp.bfloat16
-        )
-        handed.append(from_behind(piece_grad, "pipe", -1))
+        piece_grad = jnp.dot(
+            next_table if last else table_half, flat_in, preferred_element_type=jnp.float32
+        ).astype(jnp.bfloat16)
+        handed.append(piece_grad if last else from_behind(piece_grad, "pipe", -1))
     handed = jnp.concatenate(handed, axis=1)
     slot_score = slot_score.astype(jnp.float32).reshape(-1)
     picked = jnp.sum(jnp.where(table, slot_score[None, :], jnp.float32(0.0)), axis=1)

time: 267 us -> 268 us (level)
  waiting for transfers between devices: 155 us -> 143 us
  local copies, waits for them, and re-layouts: 25.7 us -> 32 us
  starting transfers between devices: 47.9 us -> 53 us
    all_to_all x2, waiting for transfers between devices: 20.6 us -> 7.78 us  [per_device(): back = lax.all_to_all(body, 'expert', 0, 0, tiled=True)]
    all_to_all x2, starting transfers between devices: 9.81 us -> 13.7 us  [per_device(): back = lax.all_to_all(body, 'expert', 0, 0, tiled=True)]
    ppermute x2, waiting for transfers between devices: 4.87 us -> 1.06 us  [ring_reduce_scatter(): got_top = lax.ppermute(far[:half], axis, fwd)]
    ppermute x2, waiting for transfers between devices: 22.6 us -> 19.6 us  [ring_gather(): far_top = lax.ppermute(from_left[:half], axis, fwd)]
    ppermute x2 -> x3, waiting for transfers between devices: 12.5 us -> 15.2 us  [from_behind(): return lax.ppermute(shard, axis, pairs)]
  transfers between devices with their start and end apart: 22 -> 23, of which waited for: 13 -> 11; matrix products, arithmetic and copies ran while one was open for 17% -> 20% of each run, Pallas kernels for 0% -> 0%
where the time goes in v11:
time: 268 us; the launch traced here: 267 us
  waiting for transfers between devices  143 us (53%)
  starting transfers between devices  53 us (20%)
  local copies, waits for them, and re-layouts  32 us (12%)
  matrix products  24.9 us (9%)
  other arithmetic  12.5 us (5%)
    all_to_all x1, waiting for transfers between devices, per_device(): lax.all_to_all(dense_chunks(local_x[:, cols], experts), 'expert', 0, 0, t...  27.2 us
    all_to_all x1, waiting for transfers between devices, per_device(): lax.all_to_all(dense_chunks(local_dy[:, cols], experts), 'expert', 0, 0,...  27 us
    ppermute x2, waiting for transfers between devices, ring_gather(): from_left = lax.ppermute(piece, axis, fwd)  24.9 us
    ppermute x2, waiting for transfers between devices, ring_gather(): far_top = lax.ppermute(from_left[:half], axis, fwd)  19.6 us
    ppermute x3, waiting for transfers between devices, from_behind(): return lax.ppermute(shard, axis, pairs)  15.2 us
    ppermute x2, waiting for transfers between devices, ring_reduce_scatter(): from_left = lax.ppermute(to_right.astype(jnp.bfloat16), axis, fwd)  14.2 us
    all_to_all x2, starting transfers between devices, per_device(): back = lax.all_to_all(body, 'expert', 0, 0, tiled=True)  13.7 us
    all_to_all x1, starting transfers between devices, per_device(): lax.all_to_all(dense_chunks(local_dy[:, cols], experts), 'expert', 0, 0,...  9.98 us
  transfers between devices with their start and end apart: 23, of which 11 were waited for; matrix products, arithmetic and copies ran while one was open for 20% of the time, Pallas kernels for 0%

profile of v11, /device:TPU:1, one launch (start us, length us, event | category | flops | bytes accessed | tf_op | source)
XLA Modules:
  0.0 266.5 jit_solution(9596443477995754420)
XLA Ops:
  8.1 10.0 %all-to-all-start = ((bf16[16,40,1024]{2,1,0:T(8,128)(2,1)}), bf16[16,40,1024]{2,1,0:T(8,128)(2,1)S(1)}, u32[]{:S(2)}, u32[]{:S(2)}) async-start(bf16[16,40,1024]{2,1,0:T(8,128)(2,1)} %reshape.80), calls=%async_computation | async-start | bytes 2621440 | tf_op jit(solution)/shard_map/all_to_all | solution.py:115
  18.0 2.8 %convolution_convert_fusion.2 = bf16[160,4096]{1,0:T(8,128)(2,1)} fusion(bf16[1,128,4096]{2,1,0:T(8,128)(2,1)} %param.7, s32[128]{0:T(128)S(1)} %multiply_add_fusion.1), kind=kOutput, calls=%fused_computation.5 | convolution fusion | flops 168448000 | bytes 2359808 | tf_op jit(solution)/shard_map/dot_general | solution.py:98
  20.8 3.4 %reshape.82 = bf16[16,40,1024]{2,1,0:T(8,128)(2,1)} reshape(bf16[160,4096]{1,0:T(8,128)(2,1)} %convolution_convert_fusion.2) | data formatting | bytes 2621440 | tf_op jit(solution)/shard_map/reshape | solution.py:74
  24.2 27.0 %all-to-all-done = bf16[16,40,1024]{2,1,0:T(8,128)(2,1)S(1)} async-done(((bf16[16,40,1024]{2,1,0:T(8,128)(2,1)}), bf16[16,40,1024]{2,1,0:T(8,128)(2,1)S(1)}, u32[]{:S(2)}, u32[]{:S(2)}) %all-to-all-start) | async-done | bytes 1310752 | tf_op jit(solution)/shard_map/all_to_all | solution.py:115
  51.2 4.3 %all-to-all-start.1 = ((bf16[16,40,1024]{2,1,0:T(8,128)(2,1)}), bf16[16,40,1024]{2,1,0:T(8,128)(2,1)}, u32[]{:S(2)}, u32[]{:S(2)}) async-start(bf16[16,40,1024]{2,1,0:T(8,128)(2,1)} %reshape.82), calls=%async_computation.1 | async-start | bytes 2621440 | tf_op jit(solution)/shard_map/all_to_all | solution.py:110
  58.5 2.7 %collective-permute-start = (bf16[160,4096]{1,0:T(8,128)(2,1)}, bf16[160,4096]{1,0:T(8,128)(2,1)}, u32[]{:S(2)}, u32[]{:S(2)}) collective-permute-start(bf16[160,4096]{1,0:T(8,128)(2,1)} %reshape.81), channel_id=1, source_target_pairs={{0,3},{1,0},{2,1},{3,2},{4,7},{5,4},{6,5},{7,6},{8,11},{9,8},{10,9... | collective-permute-start | bytes 3932168 | tf_op jit(solution)/shard_map/ppermute | solution.py:20
  61.2 27.2 %all-to-all-done.1 = bf16[16,40,1024]{2,1,0:T(8,128)(2,1)} async-done(((bf16[16,40,1024]{2,1,0:T(8,128)(2,1)}), bf16[16,40,1024]{2,1,0:T(8,128)(2,1)}, u32[]{:S(2)}, u32[]{:S(2)}) %all-to-all-start.1) | async-done | bytes 1310752 | tf_op jit(solution)/shard_map/all_to_all | solution.py:110
  90.9 2.8 %collective-permute-start.4 = (bf16[160,4096]{1,0:T(8,128)(2,1)S(1)}, bf16[160,4096]{1,0:T(8,128)(2,1)}, u32[]{:S(2)}, u32[]{:S(2)}) collective-permute-start(bf16[160,4096]{1,0:T(8,128)(2,1)S(1)} %reshape.83), channel_id=1, source_target_pairs={{0,3},{1,0},{2,1},{3,2},{4,7},{5,4},{6,5},{7,6},{8,11},{9,8},{10,9... | collective-permute-start | bytes 3932168 | tf_op jit(solution)/shard_map/ppermute | solution.py:20
  98.1 2.7 %collective-permute-start.3 = (bf16[80,4096]{1,0:T(8,128)(2,1)S(1)}, bf16[80,4096]{1,0:T(8,128)(2,1)S(1)}, u32[]{:S(2)}, u32[]{:S(2)}) collective-permute-start(bf16[80,4096]{1,0:T(8,128)(2,1)S(1)} %slice.156), channel_id=1, source_target_pairs={{0,3},{1,0},{2,1},{3,2},{4,7},{5,4},{6,5},{7,6},{8,11},{9,8},{10,9... | collective-permute-start | bytes 1966088 | tf_op jit(solution)/shard_map/ppermute | solution.py:22
  100.9 24.9 %collective-permute-done.5 = bf16[160,4096]{1,0:T(8,128)(2,1)} collective-permute-done((bf16[160,4096]{1,0:T(8,128)(2,1)S(1)}, bf16[160,4096]{1,0:T(8,128)(2,1)}, u32[]{:S(2)}, u32[]{:S(2)}) %collective-permute-start.5) | collective-permute-done | bytes 1310752 | tf_op jit(solution)/shard_map/ppermute | solution.py:19
  128.1 2.9 %collective-permute-start.7 = (bf16[80,4096]{1,0:T(8,128)(2,1)S(1)}, bf16[80,4096]{1,0:T(8,128)(2,1)S(1)}, u32[]{:S(2)}, u32[]{:S(2)}) collective-permute-start(bf16[80,4096]{1,0:T(8,128)(2,1)S(1)} %slice.158), channel_id=1, source_target_pairs={{0,3},{1,0},{2,1},{3,2},{4,7},{5,4},{6,5},{7,6},{8,11},{9,8},{10,9... | collective-permute-start | bytes 1966088 | tf_op jit(solution)/shard_map/ppermute | solution.py:22
  133.9 19.6 %collective-permute-done.6 = bf16[80,4096]{1,0:T(8,128)(2,1)S(1)} collective-permute-done((bf16[80,4096]{1,0:T(8,128)(2,1)S(1)}, bf16[80,4096]{1,0:T(8,128)(2,1)S(1)}, u32[]{:S(2)}, u32[]{:S(2)}) %collective-permute-start.6) | collective-permute-done | bytes 655392 | tf_op jit(solution)/shard_map/ppermute | solution.py:21
  171.7 4.2 %convolution_convert_fusion = bf16[384,4096]{1,0:T(8,128)(2,1)} fusion(bf16[640,4096]{1,0:T(8,128)(2,1)S(1)} %constant_dynamic-update-slice_fusion.5, bf16[640,192]{0,1:T(8,128)(2,1)S(1)} %get-tuple-element.20, bf16[640,192]{0,1:T(8,128)(2,1)S(1)} %get-tuple-element.19), kind=kOutput, calls=%fused_computation.1 | convolution fusion | flops 2015821824 | bytes 8880128 | tf_op jit(solution)/shard_map/dot_general | solution.py:151
  175.9 5.9 %collective-permute-done.10 = bf16[80,2176]{1,0:T(8,128)(2,1)S(1)} collective-permute-done((bf16[80,2176]{1,0:T(8,128)(2,1)S(1)}, bf16[80,2176]{1,0:T(8,128)(2,1)S(1)}, u32[]{:S(2)}, u32[]{:S(2)}) %collective-permute-start.10) | collective-permute-done | bytes 348192 | tf_op jit(solution)/shard_map/ppermute | solution.py:39
  183.2 2.7 %collective-permute-start.11 = (bf16[160,2176]{1,0:T(8,128)(2,1)S(1)}, bf16[160,2176]{1,0:T(8,128)(2,1)S(1)}, u32[]{:S(2)}, u32[]{:S(2)}) collective-permute-start(bf16[160,2176]{1,0:T(8,128)(2,1)S(1)} %pad_maximum_fusion.3), channel_id=1, source_target_pairs={{0,3},{1,0},{2,1},{3,2},{4,7},{5,4},{6,5},{7,6},{8,11},{9,8},{10,9... | collective-permute-start | bytes 2088968 | tf_op jit(solution)/shard_map/ppermute | solution.py:45
  190.7 9.6 %collective-permute-done.9 = bf16[160,2176]{1,0:T(8,128)(2,1)S(1)} collective-permute-done((bf16[160,2176]{1,0:T(8,128)(2,1)S(1)}, bf16[160,2176]{1,0:T(8,128)(2,1)S(1)}, u32[]{:S(2)}, u32[]{:S(2)}) %collective-permute-start.9) | collective-permute-done | bytes 696352 | tf_op jit(solution)/shard_map/ppermute | solution.py:44
  202.4 7.3 %all-to-all-start.2 = ((bf16[16,8,2688]{2,1,0:T(8,128)(2,1)}), bf16[16,8,2688]{2,1,0:T(8,128)(2,1)S(1)}, u32[]{:S(2)}, u32[]{:S(2)}) async-start(bf16[16,8,2688]{2,1,0:T(8,128)(2,1)} %fusion.20), calls=%async_computation.2 | async-start | bytes 1376256 | tf_op jit(solution)/shard_map/all_to_all | solution.py:178
  209.6 4.7 %collective-permute-done.15 = bf16[160,2048]{1,0:T(8,128)(2,1)S(1)} collective-permute-done((bf16[160,2048]{1,0:T(8,128)(2,1)}, bf16[160,2048]{1,0:T(8,128)(2,1)S(1)}, u32[]{:S(2)}, u32[]{:S(2)}) %collective-permute-start.15) | collective-permute-done | bytes 655392 | tf_op jit(solution)/shard_map/ppermute | solution.py:44
  217.8 3.9 %slice_bitcast_fusion = (bf16[1,1,192,4096]{3,2,1,0:T(8,128)(2,1)}, bf16[1,1,192,4096]{3,2,1,0:T(8,128)(2,1)}) fusion(bf16[384,4096]{1,0:T(8,128)(2,1)} %convolution_convert_fusion), kind=kLoop, calls=%fused_computation.23 | loop fusion | bytes 6291456 | tf_op jit(solution)/shard_map/broadcast_in_dim | solution.py:196
  221.7 10.9 %collective-permute-done.18 = bf16[16,8,2560]{2,1,0:T(8,128)(2,1)} collective-permute-done((bf16[16,8,2560]{2,1,0:T(8,128)(2,1)S(1)}, bf16[16,8,2560]{2,1,0:T(8,128)(2,1)}, u32[]{:S(2)}, u32[]{:S(2)}) %collective-permute-start.18) | collective-permute-done | bytes 655392 | tf_op jit(solution)/shard_map/ppermute | solution.py:10
  232.6 6.5 %all-to-all-start.3 = ((bf16[16,8,2560]{2,1,0:T(8,128)(2,1)}), bf16[16,8,2560]{2,1,0:T(8,128)(2,1)S(1)}, u32[]{:S(2)}, u32[]{:S(2)}) async-start(bf16[16,8,2560]{2,1,0:T(8,128)(2,1)} %collective-permute-done.18), calls=%async_computation.3 | async-start | bytes 1310720 | tf_op jit(solution)/shard_map/all_to_all | solution.py:178
  239.1 5.0 %fusion.1 = bf16[1,1,192,4096]{3,2,1,0:T(8,128)(2,1)} fusion(bf16[640,192]{0,1:T(8,128)(2,1)S(1)} %get-tuple-element.21, bf16[640,4096]{1,0:T(8,128)(2,1)} %copy-done.2), kind=kOutput, calls=%fused_computation.7 | convolution fusion | flops 1007419392 | bytes 7061504 | tf_op jit(solution)/shard_map/dot_general | solution.py:148
  251.3 7.8 %all-to-all-done.3 = bf16[16,8,2560]{2,1,0:T(8,128)(2,1)S(1)} async-done(((bf16[16,8,2560]{2,1,0:T(8,128)(2,1)}), bf16[16,8,2560]{2,1,0:T(8,128)(2,1)S(1)}, u32[]{:S(2)}, u32[]{:S(2)}) %all-to-all-start.3) | async-done | bytes 655392 | tf_op jit(solution)/shard_map/all_to_all | solution.py:178
  260.1 4.3 %collective-permute-done.12 = bf16[128,2048]{1,0:T(8,128)(2,1)} collective-permute-done((bf16[128,2048]{1,0:T(8,128)(2,1)S(1)}, bf16[128,2048]{1,0:T(8,128)(2,1)}, u32[]{:S(2)}, u32[]{:S(2)}) %collective-permute-start.12) | collective-permute-done | bytes 524320 | tf_op jit(solution)/shard_map/ppermute | solution.py:10
  (108 shorter events, 62.4 us)
Async XLA Ops:
  0.6 159.3 %copy-start = (bf16[1,1,192,4096]{3,2,1,0:T(8,128)(2,1)S(1)}, bf16[1,1,192,4096]{3,2,1,0:T(8,128)(2,1)}, u32[]{:S(2)}) copy-start(bf16[1,1,192,4096]{3,2,1,0:T(8,128)(2,1)} %param.13) | copy-start | bytes 4718596
  8.1 43.2 %all-to-all-start = ((bf16[16,40,1024]{2,1,0:T(8,128)(2,1)}), bf16[16,40,1024]{2,1,0:T(8,128)(2,1)S(1)}, u32[]{:S(2)}, u32[]{:S(2)}) async-start(bf16[16,40,1024]{2,1,0:T(8,128)(2,1)} %reshape.80), calls=%async_computation | async-start | bytes 2621440 | tf_op jit(solution)/shard_map/all_to_all | solution.py:115
  51.2 37.2 %all-to-all-start.1 = ((bf16[16,40,1024]{2,1,0:T(8,128)(2,1)}), bf16[16,40,1024]{2,1,0:T(8,128)(2,1)}, u32[]{:S(2)}, u32[]{:S(2)}) async-start(bf16[16,40,1024]{2,1,0:T(8,128)(2,1)} %reshape.82), calls=%async_computation.1 | async-start | bytes 2621440 | tf_op jit(solution)/shard_map/all_to_all | solution.py:110
  55.5 38.2 %collective-permute-start.13 = (s32[128]{0:T(128)S(1)}, s32[128]{0:T(128)S(1)}, u32[]{:S(2)}, u32[]{:S(2)}) collective-permute-start(s32[128]{0:T(128)S(1)} %bitcast.50), channel_id=1, source_target_pairs={{64,0},{128,64},{192,128},{65,1},{129,65},{193,129},{66,2},{130,66... | collective-permute-start | bytes 1544 | tf_op jit(solution)/shard_map/ppermute | solution.py:10
  58.5 38.5 %collective-permute-start = (bf16[160,4096]{1,0:T(8,128)(2,1)}, bf16[160,4096]{1,0:T(8,128)(2,1)}, u32[]{:S(2)}, u32[]{:S(2)}) collective-permute-start(bf16[160,4096]{1,0:T(8,128)(2,1)} %reshape.81), channel_id=1, source_target_pairs={{0,3},{1,0},{2,1},{3,2},{4,7},{5,4},{6,5},{7,6},{8,11},{9,8},{10,9... | collective-permute-start | bytes 3932168 | tf_op jit(solution)/shard_map/ppermute | solution.py:20
  61.2 34.5 %collective-permute-start.1 = (bf16[160,4096]{1,0:T(8,128)(2,1)}, bf16[160,4096]{1,0:T(8,128)(2,1)}, u32[]{:S(2)}, u32[]{:S(2)}) collective-permute-start(bf16[160,4096]{1,0:T(8,128)(2,1)} %reshape.81), channel_id=1, source_target_pairs={{0,1},{1,2},{2,3},{3,0},{4,5},{5,6},{6,7},{7,4},{8,9},{9,10},{10,1... | collective-permute-start | bytes 3932168 | tf_op jit(solution)/shard_map/ppermute | solution.py:19
  90.9 36.0 %collective-permute-start.4 = (bf16[160,4096]{1,0:T(8,128)(2,1)S(1)}, bf16[160,4096]{1,0:T(8,128)(2,1)}, u32[]{:S(2)}, u32[]{:S(2)}) collective-permute-start(bf16[160,4096]{1,0:T(8,128)(2,1)S(1)} %reshape.83), channel_id=1, source_target_pairs={{0,3},{1,0},{2,1},{3,2},{4,7},{5,4},{6,5},{7,6},{8,11},{9,8},{10,9... | collective-permute-start | bytes 3932168 | tf_op jit(solution)/shard_map/ppermute | solution.py:20
  93.7 32.0 %collective-permute-start.5 = (bf16[160,4096]{1,0:T(8,128)(2,1)S(1)}, bf16[160,4096]{1,0:T(8,128)(2,1)}, u32[]{:S(2)}, u32[]{:S(2)}) collective-permute-start(bf16[160,4096]{1,0:T(8,128)(2,1)S(1)} %reshape.83), channel_id=1, source_target_pairs={{0,1},{1,2},{2,3},{3,0},{4,5},{5,6},{6,7},{7,4},{8,9},{9,10},{10,1... | collective-permute-start | bytes 3932168 | tf_op jit(solution)/shard_map/ppermute | solution.py:19
  96.9 58.3 %collective-permute-start.2 = (bf16[80,4096]{1,0:T(8,128)(2,1)S(1)}, bf16[80,4096]{1,0:T(8,128)(2,1)S(1)}, u32[]{:S(2)}, u32[]{:S(2)}) collective-permute-start(bf16[80,4096]{1,0:T(8,128)(2,1)S(1)} %slice.155), channel_id=1, source_target_pairs={{0,1},{1,2},{2,3},{3,0},{4,5},{5,6},{6,7},{7,4},{8,9},{9,10},{10,1... | collective-permute-start | bytes 1966088 | tf_op jit(solution)/shard_map/ppermute | solution.py:21
  98.1 60.3 %collective-permute-start.3 = (bf16[80,4096]{1,0:T(8,128)(2,1)S(1)}, bf16[80,4096]{1,0:T(8,128)(2,1)S(1)}, u32[]{:S(2)}, u32[]{:S(2)}) collective-permute-start(bf16[80,4096]{1,0:T(8,128)(2,1)S(1)} %slice.156), channel_id=1, source_target_pairs={{0,3},{1,0},{2,1},{3,2},{4,7},{5,4},{6,5},{7,6},{8,11},{9,8},{10,9... | collective-permute-start | bytes 1966088 | tf_op jit(solution)/shard_map/ppermute | solution.py:22
  126.9 26.6 %collective-permute-start.6 = (bf16[80,4096]{1,0:T(8,128)(2,1)S(1)}, bf16[80,4096]{1,0:T(8,128)(2,1)S(1)}, u32[]{:S(2)}, u32[]{:S(2)}) collective-permute-start(bf16[80,4096]{1,0:T(8,128)(2,1)S(1)} %slice.157), channel_id=1, source_target_pairs={{0,1},{1,2},{2,3},{3,0},{4,5},{5,6},{6,7},{7,4},{8,9},{9,10},{10,1... | collective-permute-start | bytes 1966088 | tf_op jit(solution)/shard_map/ppermute | solution.py:21
  128.1 25.4 %collective-permute-start.7 = (bf16[80,4096]{1,0:T(8,128)(2,1)S(1)}, bf16[80,4096]{1,0:T(8,128)(2,1)S(1)}, u32[]{:S(2)}, u32[]{:S(2)}) collective-permute-start(bf16[80,4096]{1,0:T(8,128)(2,1)S(1)} %slice.158), channel_id=1, source_target_pairs={{0,3},{1,0},{2,1},{3,2},{4,7},{5,4},{6,5},{7,6},{8,11},{9,8},{10,9... | collective-permute-start | bytes 1966088 | tf_op jit(solution)/shard_map/ppermute | solution.py:22
  165.2 20.8 %collective-permute-start.14 = (bf16[80,2048]{1,0:T(8,128)(2,1)S(1)}, bf16[80,2048]{1,0:T(8,128)(2,1)S(1)}, u32[]{:S(2)}, u32[]{:S(2)}) collective-permute-start(bf16[80,2048]{1,0:T(8,128)(2,1)S(1)} %get-tuple-element.15), channel_id=1, source_target_pairs={{0,1},{1,2},{2,3},{3,0},{4,5},{5,6},{6,7},{7,4},{8,9},{9,10},{10,1... | collective-permute-start | bytes 983048 | tf_op jit(solution)/shard_map/ppermute | solution.py:38
  165.3 20.7 %collective-permute-start.16 = (bf16[80,2048]{1,0:T(8,128)(2,1)S(1)}, bf16[80,2048]{1,0:T(8,128)(2,1)S(1)}, u32[]{:S(2)}, u32[]{:S(2)}) collective-permute-start(bf16[80,2048]{1,0:T(8,128)(2,1)S(1)} %get-tuple-element.16), channel_id=1, source_target_pairs={{0,3},{1,0},{2,1},{3,2},{4,7},{5,4},{6,5},{7,6},{8,11},{9,8},{10,9... | collective-permute-start | bytes 983048 | tf_op jit(solution)/shard_map/ppermute | solution.py:39
  170.1 11.7 %collective-permute-start.10 = (bf16[80,2176]{1,0:T(8,128)(2,1)S(1)}, bf16[80,2176]{1,0:T(8,128)(2,1)S(1)}, u32[]{:S(2)}, u32[]{:S(2)}) collective-permute-start(bf16[80,2176]{1,0:T(8,128)(2,1)S(1)} %get-tuple-element.10), channel_id=1, source_target_pairs={{0,3},{1,0},{2,1},{3,2},{4,7},{5,4},{6,5},{7,6},{8,11},{9,8},{10,9... | collective-permute-start | bytes 1044488 | tf_op jit(solution)/shard_map/ppermute | solution.py:39
  170.2 12.6 %collective-permute-start.8 = (bf16[80,2176]{1,0:T(8,128)(2,1)S(1)}, bf16[80,2176]{1,0:T(8,128)(2,1)S(1)}, u32[]{:S(2)}, u32[]{:S(2)}) collective-permute-start(bf16[80,2176]{1,0:T(8,128)(2,1)S(1)} %get-tuple-element.9), channel_id=1, source_target_pairs={{0,1},{1,2},{2,3},{3,0},{4,5},{5,6},{6,7},{7,4},{8,9},{9,10},{10,1... | collective-permute-start | bytes 1044488 | tf_op jit(solution)/shard_map/ppermute | solution.py:38
  183.1 17.2 %collective-permute-start.9 = (bf16[160,2176]{1,0:T(8,128)(2,1)S(1)}, bf16[160,2176]{1,0:T(8,128)(2,1)S(1)}, u32[]{:S(2)}, u32[]{:S(2)}) collective-permute-start(bf16[160,2176]{1,0:T(8,128)(2,1)S(1)} %pad_maximum_fusion.2), channel_id=1, source_target_pairs={{0,1},{1,2},{2,3},{3,0},{4,5},{5,6},{6,7},{7,4},{8,9},{9,10},{10,1... | collective-permute-start | bytes 2088968 | tf_op jit(solution)/shard_map/ppermute | solution.py:44
  183.2 17.0 %collective-permute-start.11 = (bf16[160,2176]{1,0:T(8,128)(2,1)S(1)}, bf16[160,2176]{1,0:T(8,128)(2,1)S(1)}, u32[]{:S(2)}, u32[]{:S(2)}) collective-permute-start(bf16[160,2176]{1,0:T(8,128)(2,1)S(1)} %pad_maximum_fusion.3), channel_id=1, source_target_pairs={{0,3},{1,0},{2,1},{3,2},{4,7},{5,4},{6,5},{7,6},{8,11},{9,8},{10,9... | collective-permute-start | bytes 2088968 | tf_op jit(solution)/shard_map/ppermute | solution.py:45
  187.1 27.2 %collective-permute-start.15 = (bf16[160,2048]{1,0:T(8,128)(2,1)}, bf16[160,2048]{1,0:T(8,128)(2,1)S(1)}, u32[]{:S(2)}, u32[]{:S(2)}) collective-permute-start(bf16[160,2048]{1,0:T(8,128)(2,1)} %pad_maximum_fusion.4), channel_id=1, source_target_pairs={{0,1},{1,2},{2,3},{3,0},{4,5},{5,6},{6,7},{7,4},{8,9},{9,10},{10,1... | collective-permute-start | bytes 1966088 | tf_op jit(solution)/shard_map/ppermute | solution.py:44
  188.0 26.3 %collective-permute-start.17 = (bf16[160,2048]{1,0:T(8,128)(2,1)}, bf16[160,2048]{1,0:T(8,128)(2,1)}, u32[]{:S(2)}, u32[]{:S(2)}) collective-permute-start(bf16[160,2048]{1,0:T(8,128)(2,1)} %pad_maximum_fusion.5), channel_id=1, source_target_pairs={{0,3},{1,0},{2,1},{3,2},{4,7},{5,4},{6,5},{7,6},{8,11},{9,8},{10,9... | collective-permute-start | bytes 1966088 | tf_op jit(solution)/shard_map/ppermute | solution.py:45
  202.4 30.3 %all-to-all-start.2 = ((bf16[16,8,2688]{2,1,0:T(8,128)(2,1)}), bf16[16,8,2688]{2,1,0:T(8,128)(2,1)S(1)}, u32[]{:S(2)}, u32[]{:S(2)}) async-start(bf16[16,8,2688]{2,1,0:T(8,128)(2,1)} %fusion.20), calls=%async_computation.2 | async-start | bytes 1376256 | tf_op jit(solution)/shard_map/all_to_all | solution.py:178
  216.5 16.1 %collective-permute-start.18 = (bf16[16,8,2560]{2,1,0:T(8,128)(2,1)S(1)}, bf16[16,8,2560]{2,1,0:T(8,128)(2,1)}, u32[]{:S(2)}, u32[]{:S(2)}) collective-permute-start(bf16[16,8,2560]{2,1,0:T(8,128)(2,1)S(1)} %reshape.86), channel_id=1, source_target_pairs={{64,0},{128,64},{192,128},{65,1},{129,65},{193,129},{66,2},{130,66... | collective-permute-start | bytes 1966088 | tf_op jit(solution)/shard_map/ppermute | solution.py:10
  232.6 26.5 %all-to-all-start.3 = ((bf16[16,8,2560]{2,1,0:T(8,128)(2,1)}), bf16[16,8,2560]{2,1,0:T(8,128)(2,1)S(1)}, u32[]{:S(2)}, u32[]{:S(2)}) async-start(bf16[16,8,2560]{2,1,0:T(8,128)(2,1)} %collective-permute-done.18), calls=%async_computation.3 | async-start | bytes 1310720 | tf_op jit(solution)/shard_map/all_to_all | solution.py:178
  249.1 15.3 %collective-permute-start.12 = (bf16[128,2048]{1,0:T(8,128)(2,1)S(1)}, bf16[128,2048]{1,0:T(8,128)(2,1)}, u32[]{:S(2)}, u32[]{:S(2)}) collective-permute-start(bf16[128,2048]{1,0:T(8,128)(2,1)S(1)} %convolution_convert_fusion.7), channel_id=1, source_target_pairs={{64,0},{128,64},{192,128},{65,1},{129,65},{193,129},{66,2},{130,66... | collective-permute-start | bytes 1572872 | tf_op jit(solution)/shard_map/ppermute | solution.py:10
  (7 other events, 97.4 us)

commit v12 on v9

--- a/solution.py
+++ b/solution.py
@@ -103,6 +103,7 @@
         cols = slice(q * width, (q + 1) * width)
         dy_e = lax.all_to_all(dense_chunks(local_dy[:, cols], experts), "expert", 0, 0, tiled=True)
         dy_e = dy_e.reshape(experts * capacity, width)
+        dy_e, rows_x[q] = lax.optimization_barrier((dy_e, rows_x[q]))
         rows_grad.append(ring_gather(dy_e, "dp", my_group))
     both_mat = jnp.concatenate([gate_mat, up_mat], axis=0)
     hidden = gate_mat.shape[0]

time: 267 us -> 275 us (1.030)
  starting transfers between devices: 47.9 us -> 55.4 us
  waiting for transfers between devices: 155 us -> 150 us
  local copies, waits for them, and re-layouts: 25.7 us -> 29.1 us
    ppermute x2, waiting for transfers between devices: 22.5 us -> 51.6 us  [ring_gather(): from_left = lax.ppermute(piece, axis, fwd)]
    all_to_all x1, waiting for transfers between devices: 27 us -> 0.01 us  [per_device(): lax.all_to_all(dense_chunks(local_dy[:, cols], experts), 'expert', 0, 0,...]
    ppermute x2, waiting for transfers between devices: 12.2 us -> 4.64 us  [ring_reduce_scatter(): from_left = lax.ppermute(to_right.astype(jnp.bfloat16), axis, fwd)]
    all_to_all x2, starting transfers between devices: 9.81 us -> 16.6 us  [per_device(): back = lax.all_to_all(body, 'expert', 0, 0, tiled=True)]
    all_to_all x2, waiting for transfers between devices: 20.6 us -> 27.4 us  [per_device(): back = lax.all_to_all(body, 'expert', 0, 0, tiled=True)]
    all_to_all x1, starting transfers between devices: 9.98 us -> 4.28 us  [per_device(): lax.all_to_all(dense_chunks(local_dy[:, cols], experts), 'expert', 0, 0,...]
    all_to_all x1, starting transfers between devices: 4.29 us -> 9.98 us  [per_device(): lax.all_to_all(dense_chunks(local_x[:, cols], experts), 'expert', 0, 0, t...]
    ppermute x2, waiting for transfers between devices: 22.6 us -> 17.6 us  [ring_gather(): far_top = lax.ppermute(from_left[:half], axis, fwd)]
  transfers between devices with their start and end apart: 22 -> 22, of which waited for: 13 -> 13; matrix products, arithmetic and copies ran while one was open for 17% -> 18% of each run, Pallas kernels for 0% -> 0%
where the time goes in v12:
time: 275 us; the launch traced here: 274 us
  waiting for transfers between devices  150 us (55%)
  starting transfers between devices  55.4 us (20%)
  local copies, waits for them, and re-layouts  29.1 us (11%)
  matrix products  27.1 us (10%)
  other arithmetic  10.6 us (4%)
    ppermute x2, waiting for transfers between devices, ring_gather(): from_left = lax.ppermute(piece, axis, fwd)  51.6 us
    all_to_all x2, waiting for transfers between devices, per_device(): back = lax.all_to_all(body, 'expert', 0, 0, tiled=True)  27.4 us
    all_to_all x1, waiting for transfers between devices, per_device(): lax.all_to_all(dense_chunks(local_x[:, cols], experts), 'expert', 0, 0, t...  26.9 us
    ppermute x2, waiting for transfers between devices, ring_gather(): far_top = lax.ppermute(from_left[:half], axis, fwd)  17.6 us
    all_to_all x2, starting transfers between devices, per_device(): back = lax.all_to_all(body, 'expert', 0, 0, tiled=True)  16.6 us
    ppermute x2, waiting for transfers between devices, from_behind(): return lax.ppermute(shard, axis, pairs)  12.5 us
    all_to_all x1, starting transfers between devices, per_device(): lax.all_to_all(dense_chunks(local_x[:, cols], experts), 'expert', 0, 0, t...  9.98 us
    unnamed x36, local copies, waits for them, and re-layouts  8.32 us
  transfers between devices with their start and end apart: 22, of which 13 were waited for; matrix products, arithmetic and copies ran while one was open for 18% of the time, Pallas kernels for 0%

profile of v12, /device:TPU:1, one launch (start us, length us, event | category | flops | bytes accessed | tf_op | source)
XLA Modules:
  0.0 273.6 jit_solution(4748117724187580092)
XLA Ops:
  6.6 10.0 %all-to-all-start.1 = ((bf16[16,40,1024]{2,1,0:T(8,128)(2,1)}), bf16[16,40,1024]{2,1,0:T(8,128)(2,1)S(1)}, u32[]{:S(2)}, u32[]{:S(2)}) async-start(bf16[16,40,1024]{2,1,0:T(8,128)(2,1)} %reshape.80), calls=%async_computation.1 | async-start | bytes 2621440 | tf_op jit(solution)/shard_map/all_to_all | solution.py:99
  16.6 2.9 %convolution_convert_fusion.3 = bf16[160,4096]{1,0:T(8,128)(2,1)} fusion(bf16[1,128,4096]{2,1,0:T(8,128)(2,1)} %param.10, f32[128]{0:T(128)S(1)} %convert_element_type.124, s32[128]{0:T(128)S(1)} %multiply_add_fusion), kind=kOutput, calls=%fused_computation.6 | convolution fusion | flops 170020864 | bytes 2360320 | tf_op jit(solution)/shard_map/dot_general | solution.py:90
  19.5 3.4 %reshape.78 = bf16[16,40,1024]{2,1,0:T(8,128)(2,1)} reshape(bf16[160,4096]{1,0:T(8,128)(2,1)} %convolution_convert_fusion.3) | data formatting | bytes 2621440 | tf_op jit(solution)/shard_map/reshape | solution.py:65
  22.9 26.9 %all-to-all-done.1 = bf16[16,40,1024]{2,1,0:T(8,128)(2,1)S(1)} async-done(((bf16[16,40,1024]{2,1,0:T(8,128)(2,1)}), bf16[16,40,1024]{2,1,0:T(8,128)(2,1)S(1)}, u32[]{:S(2)}, u32[]{:S(2)}) %all-to-all-start.1) | async-done | bytes 1310752 | tf_op jit(solution)/shard_map/all_to_all | solution.py:99
  49.8 4.3 %all-to-all-start = ((bf16[16,40,1024]{2,1,0:T(8,128)(2,1)}), bf16[16,40,1024]{2,1,0:T(8,128)(2,1)}, u32[]{:S(2)}, u32[]{:S(2)}) async-start(bf16[16,40,1024]{2,1,0:T(8,128)(2,1)} %reshape.78), calls=%async_computation | async-start | bytes 2621440 | tf_op jit(solution)/shard_map/all_to_all | solution.py:104
  58.4 29.4 %collective-permute-done.1 = bf16[160,4096]{1,0:T(8,128)(2,1)S(1)} collective-permute-done((bf16[160,4096]{1,0:T(8,128)(2,1)}, bf16[160,4096]{1,0:T(8,128)(2,1)S(1)}, u32[]{:S(2)}, u32[]{:S(2)}) %collective-permute-start.1) | collective-permute-done | bytes 1310752 | tf_op jit(solution)/shard_map/ppermute | solution.py:19
  96.0 2.7 collective-permute-start.3
  101.2 5.7 %collective-permute-done.2 = bf16[80,4096]{1,0:T(8,128)(2,1)S(1)} collective-permute-done((bf16[80,4096]{1,0:T(8,128)(2,1)}, bf16[80,4096]{1,0:T(8,128)(2,1)S(1)}, u32[]{:S(2)}, u32[]{:S(2)}) %collective-permute-start.2) | collective-permute-done | bytes 655392 | tf_op jit(solution)/shard_map/ppermute | solution.py:21
  107.9 4.1 %collective-permute-done.3 = bf16[80,4096]{1,0:T(8,128)(2,1)S(1)} collective-permute-done((bf16[80,4096]{1,0:T(8,128)(2,1)S(1)}, bf16[80,4096]{1,0:T(8,128)(2,1)S(1)}, u32[]{:S(2)}, u32[]{:S(2)}) %collective-permute-start.3) | collective-permute-done | bytes 655392 | tf_op jit(solution)/shard_map/ppermute | solution.py:22
  117.5 5.1 %fusion.2 = f32[640,384]{0,1:T(8,128)S(1)} fusion(bf16[640,4096]{1,0:T(8,128)(2,1)} %constant_dynamic-update-slice_fusion, bf16[192,4096]{1,0:T(8,128)(2,1)S(1)} %bitcast.52, bf16[192,4096]{1,0:T(8,128)(2,1)S(1)} %bitcast.55), kind=kOutput, calls=%fused_computation.15 | convolution fusion | flops 2019557376 | bytes 9371648 | tf_op jit(solution)/shard_map/dot_general | solution.py:113
  122.7 22.2 %collective-permute-done.5 = bf16[160,4096]{1,0:T(8,128)(2,1)S(1)} collective-permute-done((bf16[160,4096]{1,0:T(8,128)(2,1)S(1)}, bf16[160,4096]{1,0:T(8,128)(2,1)S(1)}, u32[]{:S(2)}, u32[]{:S(2)}) %collective-permute-start.5) | collective-permute-done | bytes 1310752 | tf_op jit(solution)/shard_map/ppermute | solution.py:19
  145.2 2.9 %collective-permute-start.7 = (bf16[80,4096]{1,0:T(8,128)(2,1)S(1)}, bf16[80,4096]{1,0:T(8,128)(2,1)S(1)}, u32[]{:S(2)}, u32[]{:S(2)}) collective-permute-start(bf16[80,4096]{1,0:T(8,128)(2,1)S(1)} %slice.158), channel_id=1, source_target_pairs={{0,3},{1,0},{2,1},{3,2},{4,7},{5,4},{6,5},{7,6},{8,11},{9,8},{10,9... | collective-permute-start | bytes 1966088 | tf_op jit(solution)/shard_map/ppermute | solution.py:22
  148.2 11.9 %collective-permute-done.6 = bf16[80,4096]{1,0:T(8,128)(2,1)S(1)} collective-permute-done((bf16[80,4096]{1,0:T(8,128)(2,1)S(1)}, bf16[80,4096]{1,0:T(8,128)(2,1)S(1)}, u32[]{:S(2)}, u32[]{:S(2)}) %collective-permute-start.6) | collective-permute-done | bytes 655392 | tf_op jit(solution)/shard_map/ppermute | solution.py:21
  165.7 2.8 %collective-permute-start.15 = (bf16[80,2048]{1,0:T(8,128)(2,1)S(1)}, bf16[80,2048]{1,0:T(8,128)(2,1)S(1)}, u32[]{:S(2)}, u32[]{:S(2)}) collective-permute-start(bf16[80,2048]{1,0:T(8,128)(2,1)S(1)} %get-tuple-element.20), channel_id=1, source_target_pairs={{0,3},{1,0},{2,1},{3,2},{4,7},{5,4},{6,5},{7,6},{8,11},{9,8},{10,9... | collective-permute-start | bytes 983048 | tf_op jit(solution)/shard_map/ppermute | solution.py:39
  176.1 4.9 %collective-permute-done.10 = bf16[80,2176]{1,0:T(8,128)(2,1)S(1)} collective-permute-done((bf16[80,2176]{1,0:T(8,128)(2,1)S(1)}, bf16[80,2176]{1,0:T(8,128)(2,1)S(1)}, u32[]{:S(2)}, u32[]{:S(2)}) %collective-permute-start.10) | collective-permute-done | bytes 348192 | tf_op jit(solution)/shard_map/ppermute | solution.py:39
  183.0 2.7 collective-permute-start.11
  185.7 4.0 %convolution_convert_fusion = bf16[384,4096]{1,0:T(8,128)(2,1)} fusion(bf16[640,4096]{1,0:T(8,128)(2,1)S(1)} %bitcast.49, bf16[640,192]{0,1:T(8,128)(2,1)S(1)} %get-tuple-element.24, bf16[640,192]{0,1:T(8,128)(2,1)S(1)} %get-tuple-element.23), kind=kOutput, calls=%fused_computation.1 | convolution fusion | flops 2015821824 | bytes 8880128 | tf_op jit(solution)/shard_map/dot_general | solution.py:141
  189.7 4.6 %collective-permute-done.14 = bf16[160,2048]{1,0:T(8,128)(2,1)S(1)} collective-permute-done((bf16[160,2048]{1,0:T(8,128)(2,1)S(1)}, bf16[160,2048]{1,0:T(8,128)(2,1)S(1)}, u32[]{:S(2)}, u32[]{:S(2)}) %collective-permute-start.14) | collective-permute-done | bytes 655392 | tf_op jit(solution)/shard_map/ppermute | solution.py:44
  196.2 13.1 %all-to-all-start.3 = ((bf16[16,8,2560]{2,1,0:T(8,128)(2,1)}), bf16[16,8,2560]{2,1,0:T(8,128)(2,1)S(1)}, u32[]{:S(2)}, u32[]{:S(2)}) async-start(bf16[16,8,2560]{2,1,0:T(8,128)(2,1)} %reshape.84), calls=%async_computation.3 | async-start | bytes 1310720 | tf_op jit(solution)/shard_map/all_to_all | solution.py:165
  212.6 16.8 %all-to-all-done.3 = bf16[16,8,2560]{2,1,0:T(8,128)(2,1)S(1)} async-done(((bf16[16,8,2560]{2,1,0:T(8,128)(2,1)}), bf16[16,8,2560]{2,1,0:T(8,128)(2,1)S(1)}, u32[]{:S(2)}, u32[]{:S(2)}) %all-to-all-start.3) | async-done | bytes 655392 | tf_op jit(solution)/shard_map/all_to_all | solution.py:165
  229.4 3.5 %all-to-all-start.2 = ((bf16[16,8,2688]{2,1,0:T(8,128)(2,1)}), bf16[16,8,2688]{2,1,0:T(8,128)(2,1)S(1)}, u32[]{:S(2)}, u32[]{:S(2)}) async-start(bf16[16,8,2688]{2,1,0:T(8,128)(2,1)} %fusion.20), calls=%async_computation.2 | async-start | bytes 1376256 | tf_op jit(solution)/shard_map/all_to_all | solution.py:165
  232.9 5.2 %fusion.1 = bf16[1,1,192,4096]{3,2,1,0:T(8,128)(2,1)} fusion(bf16[640,192]{0,1:T(8,128)(2,1)S(1)} %get-tuple-element.25, bf16[640,4096]{1,0:T(8,128)(2,1)} %copy-done.2), kind=kOutput, calls=%fused_computation.7 | convolution fusion | flops 1007419392 | bytes 7061504 | tf_op jit(solution)/shard_map/dot_general | solution.py:138
  242.4 10.6 %all-to-all-done.2 = bf16[16,8,2688]{2,1,0:T(8,128)(2,1)S(1)} async-done(((bf16[16,8,2688]{2,1,0:T(8,128)(2,1)}), bf16[16,8,2688]{2,1,0:T(8,128)(2,1)S(1)}, u32[]{:S(2)}, u32[]{:S(2)}) %all-to-all-start.2) | async-done | bytes 688160 | tf_op jit(solution)/shard_map/all_to_all | solution.py:165
  259.0 12.5 %collective-permute-done.12 = bf16[128,2048]{1,0:T(8,128)(2,1)S(1)} collective-permute-done((bf16[128,2048]{1,0:T(8,128)(2,1)}, bf16[128,2048]{1,0:T(8,128)(2,1)S(1)}, u32[]{:S(2)}, u32[]{:S(2)}) %collective-permute-start.12) | collective-permute-done | bytes 524320 | tf_op jit(solution)/shard_map/ppermute | solution.py:10
  (115 shorter events, 60.3 us)
Async XLA Ops:
  0.6 159.7 %copy-start = (bf16[1,1,192,4096]{3,2,1,0:T(8,128)(2,1)S(1)}, bf16[1,1,192,4096]{3,2,1,0:T(8,128)(2,1)}, u32[]{:S(2)}) copy-start(bf16[1,1,192,4096]{3,2,1,0:T(8,128)(2,1)} %param.13) | copy-start | bytes 4718596
  6.6 43.2 %all-to-all-start.1 = ((bf16[16,40,1024]{2,1,0:T(8,128)(2,1)}), bf16[16,40,1024]{2,1,0:T(8,128)(2,1)S(1)}, u32[]{:S(2)}, u32[]{:S(2)}) async-start(bf16[16,40,1024]{2,1,0:T(8,128)(2,1)} %reshape.80), calls=%async_computation.1 | async-start | bytes 2621440 | tf_op jit(solution)/shard_map/all_to_all | solution.py:99
  16.6 33.2 %copy-start.8 = (bf16[128]{0:T(256)(128)(2,1)}, bf16[128]{0:T(256)(128)(2,1)S(1)}, u32[]{:S(2)}) copy-start(bf16[128]{0:T(256)(128)(2,1)S(1)} %convert_bitcast_fusion) | copy-start | bytes 772
  49.8 42.6 %all-to-all-start = ((bf16[16,40,1024]{2,1,0:T(8,128)(2,1)}), bf16[16,40,1024]{2,1,0:T(8,128)(2,1)}, u32[]{:S(2)}, u32[]{:S(2)}) async-start(bf16[16,40,1024]{2,1,0:T(8,128)(2,1)} %reshape.78), calls=%async_computation | async-start | bytes 2621440 | tf_op jit(solution)/shard_map/all_to_all | solution.py:104
  55.7 32.1 %collective-permute-start.1 = (bf16[160,4096]{1,0:T(8,128)(2,1)}, bf16[160,4096]{1,0:T(8,128)(2,1)S(1)}, u32[]{:S(2)}, u32[]{:S(2)}) collective-permute-start(bf16[160,4096]{1,0:T(8,128)(2,1)} %reshape.81), channel_id=1, source_target_pairs={{0,1},{1,2},{2,3},{3,0},{4,5},{5,6},{6,7},{7,4},{8,9},{9,10},{10,1... | collective-permute-start | bytes 3932168 | tf_op jit(solution)/shard_map/ppermute | solution.py:19
  57.0 37.9 %collective-permute-start = (bf16[160,4096]{1,0:T(8,128)(2,1)}, bf16[160,4096]{1,0:T(8,128)(2,1)}, u32[]{:S(2)}, u32[]{:S(2)}) collective-permute-start(bf16[160,4096]{1,0:T(8,128)(2,1)} %reshape.81), channel_id=1, source_target_pairs={{0,3},{1,0},{2,1},{3,2},{4,7},{5,4},{6,5},{7,6},{8,11},{9,8},{10,9... | collective-permute-start | bytes 3932168 | tf_op jit(solution)/shard_map/ppermute | solution.py:20
  89.8 17.2 %collective-permute-start.2 = (bf16[80,4096]{1,0:T(8,128)(2,1)}, bf16[80,4096]{1,0:T(8,128)(2,1)S(1)}, u32[]{:S(2)}, u32[]{:S(2)}) collective-permute-start(bf16[80,4096]{1,0:T(8,128)(2,1)} %slice.155), channel_id=1, source_target_pairs={{0,1},{1,2},{2,3},{3,0},{4,5},{5,6},{6,7},{7,4},{8,9},{9,10},{10,1... | collective-permute-start | bytes 1966088 | tf_op jit(solution)/shard_map/ppermute | solution.py:21
  96.0 15.9 %collective-permute-start.3 = (bf16[80,4096]{1,0:T(8,128)(2,1)S(1)}, bf16[80,4096]{1,0:T(8,128)(2,1)S(1)}, u32[]{:S(2)}, u32[]{:S(2)}) collective-permute-start(bf16[80,4096]{1,0:T(8,128)(2,1)S(1)} %slice.156), channel_id=1, source_target_pairs={{0,3},{1,0},{2,1},{3,2},{4,7},{5,4},{6,5},{7,6},{8,11},{9,8},{10,9... | collective-permute-start | bytes 1966088 | tf_op jit(solution)/shard_map/ppermute | solution.py:22
  114.1 30.8 %collective-permute-start.5 = (bf16[160,4096]{1,0:T(8,128)(2,1)S(1)}, bf16[160,4096]{1,0:T(8,128)(2,1)S(1)}, u32[]{:S(2)}, u32[]{:S(2)}) collective-permute-start(bf16[160,4096]{1,0:T(8,128)(2,1)S(1)} %reshape.79), channel_id=1, source_target_pairs={{0,1},{1,2},{2,3},{3,0},{4,5},{5,6},{6,7},{7,4},{8,9},{9,10},{10,1... | collective-permute-start | bytes 3932168 | tf_op jit(solution)/shard_map/ppermute | solution.py:19
  115.1 30.1 %collective-permute-start.4 = (bf16[160,4096]{1,0:T(8,128)(2,1)S(1)}, bf16[160,4096]{1,0:T(8,128)(2,1)S(1)}, u32[]{:S(2)}, u32[]{:S(2)}) collective-permute-start(bf16[160,4096]{1,0:T(8,128)(2,1)S(1)} %reshape.79), channel_id=1, source_target_pairs={{0,3},{1,0},{2,1},{3,2},{4,7},{5,4},{6,5},{7,6},{8,11},{9,8},{10,9... | collective-permute-start | bytes 3932168 | tf_op jit(solution)/shard_map/ppermute | solution.py:20
  145.0 15.2 %collective-permute-start.6 = (bf16[80,4096]{1,0:T(8,128)(2,1)S(1)}, bf16[80,4096]{1,0:T(8,128)(2,1)S(1)}, u32[]{:S(2)}, u32[]{:S(2)}) collective-permute-start(bf16[80,4096]{1,0:T(8,128)(2,1)S(1)} %slice.157), channel_id=1, source_target_pairs={{0,1},{1,2},{2,3},{3,0},{4,5},{5,6},{6,7},{7,4},{8,9},{9,10},{10,1... | collective-permute-start | bytes 1966088 | tf_op jit(solution)/shard_map/ppermute | solution.py:21
  145.2 15.0 %collective-permute-start.7 = (bf16[80,4096]{1,0:T(8,128)(2,1)S(1)}, bf16[80,4096]{1,0:T(8,128)(2,1)S(1)}, u32[]{:S(2)}, u32[]{:S(2)}) collective-permute-start(bf16[80,4096]{1,0:T(8,128)(2,1)S(1)} %slice.158), channel_id=1, source_target_pairs={{0,3},{1,0},{2,1},{3,2},{4,7},{5,4},{6,5},{7,6},{8,11},{9,8},{10,9... | collective-permute-start | bytes 1966088 | tf_op jit(solution)/shard_map/ppermute | solution.py:22
  165.6 7.3 %collective-permute-start.13 = (bf16[80,2048]{1,0:T(8,128)(2,1)S(1)}, bf16[80,2048]{1,0:T(8,128)(2,1)S(1)}, u32[]{:S(2)}, u32[]{:S(2)}) collective-permute-start(bf16[80,2048]{1,0:T(8,128)(2,1)S(1)} %get-tuple-element.19), channel_id=1, source_target_pairs={{0,1},{1,2},{2,3},{3,0},{4,5},{5,6},{6,7},{7,4},{8,9},{9,10},{10,1... | collective-permute-start | bytes 983048 | tf_op jit(solution)/shard_map/ppermute | solution.py:38
  165.7 7.2 %collective-permute-start.15 = (bf16[80,2048]{1,0:T(8,128)(2,1)S(1)}, bf16[80,2048]{1,0:T(8,128)(2,1)S(1)}, u32[]{:S(2)}, u32[]{:S(2)}) collective-permute-start(bf16[80,2048]{1,0:T(8,128)(2,1)S(1)} %get-tuple-element.20), channel_id=1, source_target_pairs={{0,3},{1,0},{2,1},{3,2},{4,7},{5,4},{6,5},{7,6},{8,11},{9,8},{10,9... | collective-permute-start | bytes 983048 | tf_op jit(solution)/shard_map/ppermute | solution.py:39
  170.7 10.3 %collective-permute-start.10 = (bf16[80,2176]{1,0:T(8,128)(2,1)S(1)}, bf16[80,2176]{1,0:T(8,128)(2,1)S(1)}, u32[]{:S(2)}, u32[]{:S(2)}) collective-permute-start(bf16[80,2176]{1,0:T(8,128)(2,1)S(1)} %get-tuple-element.14), channel_id=1, source_target_pairs={{0,3},{1,0},{2,1},{3,2},{4,7},{5,4},{6,5},{7,6},{8,11},{9,8},{10,9... | collective-permute-start | bytes 1044488 | tf_op jit(solution)/shard_map/ppermute | solution.py:39
  172.2 8.8 %collective-permute-start.8 = (bf16[80,2176]{1,0:T(8,128)(2,1)S(1)}, bf16[80,2176]{1,0:T(8,128)(2,1)S(1)}, u32[]{:S(2)}, u32[]{:S(2)}) collective-permute-start(bf16[80,2176]{1,0:T(8,128)(2,1)S(1)} %get-tuple-element.13), channel_id=1, source_target_pairs={{0,1},{1,2},{2,3},{3,0},{4,5},{5,6},{6,7},{7,4},{8,9},{9,10},{10,1... | collective-permute-start | bytes 1044488 | tf_op jit(solution)/shard_map/ppermute | solution.py:38
  173.2 21.1 %collective-permute-start.14 = (bf16[160,2048]{1,0:T(8,128)(2,1)S(1)}, bf16[160,2048]{1,0:T(8,128)(2,1)S(1)}, u32[]{:S(2)}, u32[]{:S(2)}) collective-permute-start(bf16[160,2048]{1,0:T(8,128)(2,1)S(1)} %pad_maximum_fusion.4), channel_id=1, source_target_pairs={{0,1},{1,2},{2,3},{3,0},{4,5},{5,6},{6,7},{7,4},{8,9},{9,10},{10,1... | collective-permute-start | bytes 1966088 | tf_op jit(solution)/shard_map/ppermute | solution.py:44
  174.4 20.0 %collective-permute-start.16 = (bf16[160,2048]{1,0:T(8,128)(2,1)S(1)}, bf16[160,2048]{1,0:T(8,128)(2,1)S(1)}, u32[]{:S(2)}, u32[]{:S(2)}) collective-permute-start(bf16[160,2048]{1,0:T(8,128)(2,1)S(1)} %pad_maximum_fusion.5), channel_id=1, source_target_pairs={{0,3},{1,0},{2,1},{3,2},{4,7},{5,4},{6,5},{7,6},{8,11},{9,8},{10,9... | collective-permute-start | bytes 1966088 | tf_op jit(solution)/shard_map/ppermute | solution.py:45
  182.1 27.2 %collective-permute-start.9 = (bf16[160,2176]{1,0:T(8,128)(2,1)}, bf16[160,2176]{1,0:T(8,128)(2,1)S(1)}, u32[]{:S(2)}, u32[]{:S(2)}) collective-permute-start(bf16[160,2176]{1,0:T(8,128)(2,1)} %pad_maximum_fusion.2), channel_id=1, source_target_pairs={{0,1},{1,2},{2,3},{3,0},{4,5},{5,6},{6,7},{7,4},{8,9},{9,10},{10,1... | collective-permute-start | bytes 2088968 | tf_op jit(solution)/shard_map/ppermute | solution.py:44
  183.0 26.3 %collective-permute-start.11 = (bf16[160,2176]{1,0:T(8,128)(2,1)}, bf16[160,2176]{1,0:T(8,128)(2,1)S(1)}, u32[]{:S(2)}, u32[]{:S(2)}) collective-permute-start(bf16[160,2176]{1,0:T(8,128)(2,1)} %pad_maximum_fusion.3), channel_id=1, source_target_pairs={{0,3},{1,0},{2,1},{3,2},{4,7},{5,4},{6,5},{7,6},{8,11},{9,8},{10,9... | collective-permute-start | bytes 2088968 | tf_op jit(solution)/shard_map/ppermute | solution.py:45
  196.2 33.2 %all-to-all-start.3 = ((bf16[16,8,2560]{2,1,0:T(8,128)(2,1)}), bf16[16,8,2560]{2,1,0:T(8,128)(2,1)S(1)}, u32[]{:S(2)}, u32[]{:S(2)}) async-start(bf16[16,8,2560]{2,1,0:T(8,128)(2,1)} %reshape.84), calls=%async_computation.3 | async-start | bytes 1310720 | tf_op jit(solution)/shard_map/all_to_all | solution.py:165
  229.4 23.7 %all-to-all-start.2 = ((bf16[16,8,2688]{2,1,0:T(8,128)(2,1)}), bf16[16,8,2688]{2,1,0:T(8,128)(2,1)S(1)}, u32[]{:S(2)}, u32[]{:S(2)}) async-start(bf16[16,8,2688]{2,1,0:T(8,128)(2,1)} %fusion.20), calls=%async_computation.2 | async-start | bytes 1376256 | tf_op jit(solution)/shard_map/all_to_all | solution.py:165
  241.1 17.9 %collective-permute-start.17 = (bf16[128,2048]{1,0:T(8,128)(2,1)S(1)}, bf16[128,2048]{1,0:T(8,128)(2,1)}, u32[]{:S(2)}, u32[]{:S(2)}) collective-permute-start(bf16[128,2048]{1,0:T(8,128)(2,1)S(1)} %convolution_convert_fusion.6), channel_id=1, source_target_pairs={{64,0},{128,64},{192,128},{65,1},{129,65},{193,129},{66,2},{130,66... | collective-permute-start | bytes 1572872 | tf_op jit(solution)/shard_map/ppermute | solution.py:10
  256.8 14.7 %collective-permute-start.12 = (bf16[128,2048]{1,0:T(8,128)(2,1)}, bf16[128,2048]{1,0:T(8,128)(2,1)S(1)}, u32[]{:S(2)}, u32[]{:S(2)}) collective-permute-start(bf16[128,2048]{1,0:T(8,128)(2,1)} %convolution_convert_fusion.7), channel_id=1, source_target_pairs={{64,0},{128,64},{192,128},{65,1},{129,65},{193,129},{66,2},{130,66... | collective-permute-start | bytes 1572872 | tf_op jit(solution)/shard_map/ppermute | solution.py:10
  (12 other events, 153.0 us)

commit v13 on v10

--- a/solution.py
+++ b/solution.py
@@ -146,7 +146,7 @@
     grad_gate = jnp.concatenate(grad_gate, axis=1)
     grad_up = jnp.concatenate(grad_up, axis=1)
     unit = model_width // 8
-    back_widths = [4 * unit, 3 * unit, unit]
+    back_widths = [5 * unit, 3 * unit]
     handed = []
     offset = 0
     for q, back_width in enumerate(back_widths):

time: 292 us -> 267 us (0.914)
  starting transfers between devices: 69.3 us -> 49.5 us
  waiting for transfers between devices: 144 us -> 153 us
  local copies, waits for them, and re-layouts: 33.5 us -> 25.1 us
  other arithmetic: 16.5 us -> 10.7 us
  matrix products: 22.9 us -> 26.6 us
    ppermute x3 -> x2, waiting for transfers between devices: 0.01 us -> 12.8 us  [ring_reduce_scatter(): from_left = lax.ppermute(to_right.astype(jnp.bfloat16), axis, fwd)]
    ppermute x3 -> x2, starting transfers between devices: 14.8 us -> 2.96 us  [ring_reduce_scatter(): got_bottom = lax.ppermute(far[half:], axis, bwd)]
    all_to_all x3 -> x2, waiting for transfers between devices: 26 us -> 16.1 us  [per_device(): back = lax.all_to_all(body, 'expert', 0, 0, tiled=True)]
    reshape x3 -> x2, local copies, waits for them, and re-layouts: 5.77 us -> 2.06 us  [per_device(): body = summed[:, :back_width].reshape(experts, 8, span)]
    all_to_all x3 -> x2, starting transfers between devices: 14.6 us -> 11 us  [per_device(): back = lax.all_to_all(body, 'expert', 0, 0, tiled=True)]
    ppermute x3 -> x2, starting transfers between devices: 8.02 us -> 4.47 us  [ring_reduce_scatter(): from_right = lax.ppermute(to_left.astype(jnp.bfloat16), axis, bwd)]
    ppermute x3 -> x2, waiting for transfers between devices: 12.3 us -> 15 us  [from_behind(): return lax.ppermute(shard, axis, pairs)]
  transfers between devices with their start and end apart: 28 -> 22, of which waited for: 12 -> 13; matrix products, arithmetic and copies ran while one was open for 16% -> 17% of each run, Pallas kernels for 0% -> 0%
where the time goes in v13:
time: 267 us; the launch traced here: 266 us
  waiting for transfers between devices  153 us (57%)
  starting transfers between devices  49.5 us (19%)
  matrix products  26.6 us (10%)
  local copies, waits for them, and re-layouts  25.1 us (9%)
  other arithmetic  10.7 us (4%)
    all_to_all x1, waiting for transfers between devices, per_device(): lax.all_to_all(dense_chunks(local_x[:, cols], experts), 'expert', 0, 0, t...  28.5 us
    all_to_all x1, waiting for transfers between devices, per_device(): lax.all_to_all(dense_chunks(local_dy[:, cols], experts), 'expert', 0, 0,...  27 us
    ppermute x2, waiting for transfers between devices, ring_gather(): far_top = lax.ppermute(from_left[:half], axis, fwd)  22.6 us
    ppermute x2, waiting for transfers between devices, ring_gather(): from_left = lax.ppermute(piece, axis, fwd)  22.5 us
    all_to_all x2, waiting for transfers between devices, per_device(): back = lax.all_to_all(body, 'expert', 0, 0, tiled=True)  16.1 us
    ppermute x2, waiting for transfers between devices, from_behind(): return lax.ppermute(shard, axis, pairs)  15 us
    ppermute x2, waiting for transfers between devices, ring_reduce_scatter(): from_left = lax.ppermute(to_right.astype(jnp.bfloat16), axis, fwd)  12.8 us
    all_to_all x2, starting transfers between devices, per_device(): back = lax.all_to_all(body, 'expert', 0, 0, tiled=True)  11 us
  transfers between devices with their start and end apart: 22, of which 13 were waited for; matrix products, arithmetic and copies ran while one was open for 17% of the time, Pallas kernels for 0%

profile of v13, /device:TPU:1, one launch (start us, length us, event | category | flops | bytes accessed | tf_op | source)
XLA Modules:
  0.0 266.0 jit_solution(8119147116988061924)
XLA Ops:
  8.6 10.0 %all-to-all-start = ((bf16[16,40,1024]{2,1,0:T(8,128)(2,1)}), bf16[16,40,1024]{2,1,0:T(8,128)(2,1)S(1)}, u32[]{:S(2)}, u32[]{:S(2)}) async-start(bf16[16,40,1024]{2,1,0:T(8,128)(2,1)} %reshape.78), calls=%async_computation | async-start | bytes 2621440 | tf_op jit(solution)/shard_map/all_to_all | solution.py:104
  18.5 2.8 %convolution_convert_fusion.2 = bf16[160,4096]{1,0:T(8,128)(2,1)} fusion(bf16[1,128,4096]{2,1,0:T(8,128)(2,1)} %param.7, s32[128]{0:T(128)S(1)} %multiply_add_fusion), kind=kOutput, calls=%fused_computation.5 | convolution fusion | flops 168448000 | bytes 2359808 | tf_op jit(solution)/shard_map/dot_general | solution.py:87
  21.3 3.4 %reshape.80 = bf16[16,40,1024]{2,1,0:T(8,128)(2,1)} reshape(bf16[160,4096]{1,0:T(8,128)(2,1)} %convolution_convert_fusion.2) | data formatting | bytes 2621440 | tf_op jit(solution)/shard_map/reshape | solution.py:65
  24.7 27.0 %all-to-all-done = bf16[16,40,1024]{2,1,0:T(8,128)(2,1)S(1)} async-done(((bf16[16,40,1024]{2,1,0:T(8,128)(2,1)}), bf16[16,40,1024]{2,1,0:T(8,128)(2,1)S(1)}, u32[]{:S(2)}, u32[]{:S(2)}) %all-to-all-start) | async-done | bytes 1310752 | tf_op jit(solution)/shard_map/all_to_all | solution.py:104
  51.7 4.3 %all-to-all-start.1 = ((bf16[16,40,1024]{2,1,0:T(8,128)(2,1)}), bf16[16,40,1024]{2,1,0:T(8,128)(2,1)}, u32[]{:S(2)}, u32[]{:S(2)}) async-start(bf16[16,40,1024]{2,1,0:T(8,128)(2,1)} %reshape.80), calls=%async_computation.1 | async-start | bytes 2621440 | tf_op jit(solution)/shard_map/all_to_all | solution.py:99
  60.4 28.5 %all-to-all-done.1 = bf16[16,40,1024]{2,1,0:T(8,128)(2,1)} async-done(((bf16[16,40,1024]{2,1,0:T(8,128)(2,1)}), bf16[16,40,1024]{2,1,0:T(8,128)(2,1)}, u32[]{:S(2)}, u32[]{:S(2)}) %all-to-all-start.1) | async-done | bytes 1310752 | tf_op jit(solution)/shard_map/all_to_all | solution.py:99
  88.9 2.5 reshape.81
  98.3 2.7 %collective-permute-start.3 = (bf16[80,4096]{1,0:T(8,128)(2,1)S(1)}, bf16[80,4096]{1,0:T(8,128)(2,1)S(1)}, u32[]{:S(2)}, u32[]{:S(2)}) collective-permute-start(bf16[80,4096]{1,0:T(8,128)(2,1)S(1)} %slice.156), channel_id=1, source_target_pairs={{0,3},{1,0},{2,1},{3,2},{4,7},{5,4},{6,5},{7,6},{8,11},{9,8},{10,9... | collective-permute-start | bytes 1966088 | tf_op jit(solution)/shard_map/ppermute | solution.py:22
  101.0 22.5 %collective-permute-done.5 = bf16[160,4096]{1,0:T(8,128)(2,1)S(1)} collective-permute-done((bf16[160,4096]{1,0:T(8,128)(2,1)S(1)}, bf16[160,4096]{1,0:T(8,128)(2,1)S(1)}, u32[]{:S(2)}, u32[]{:S(2)}) %collective-permute-start.5) | collective-permute-done | bytes 1310752 | tf_op jit(solution)/shard_map/ppermute | solution.py:19
  123.7 2.9 %collective-permute-start.7 = (bf16[80,4096]{1,0:T(8,128)(2,1)S(1)}, bf16[80,4096]{1,0:T(8,128)(2,1)S(1)}, u32[]{:S(2)}, u32[]{:S(2)}) collective-permute-start(bf16[80,4096]{1,0:T(8,128)(2,1)S(1)} %slice.158), channel_id=1, source_target_pairs={{0,3},{1,0},{2,1},{3,2},{4,7},{5,4},{6,5},{7,6},{8,11},{9,8},{10,9... | collective-permute-start | bytes 1966088 | tf_op jit(solution)/shard_map/ppermute | solution.py:22
  128.2 22.6 %collective-permute-done.6 = bf16[80,4096]{1,0:T(8,128)(2,1)S(1)} collective-permute-done((bf16[80,4096]{1,0:T(8,128)(2,1)S(1)}, bf16[80,4096]{1,0:T(8,128)(2,1)S(1)}, u32[]{:S(2)}, u32[]{:S(2)}) %collective-permute-start.6) | collective-permute-done | bytes 655392 | tf_op jit(solution)/shard_map/ppermute | solution.py:21
  152.8 2.6 fusion.3
  171.4 2.4 collective-permute-start.16
  173.8 5.3 %collective-permute-done.10 = bf16[80,2688]{1,0:T(8,128)(2,1)S(1)} collective-permute-done((bf16[80,2688]{1,0:T(8,128)(2,1)S(1)}, bf16[80,2688]{1,0:T(8,128)(2,1)S(1)}, u32[]{:S(2)}, u32[]{:S(2)}) %collective-permute-start.10) | collective-permute-done | bytes 430112 | tf_op jit(solution)/shard_map/ppermute | solution.py:39
  182.9 4.0 %convolution_convert_fusion = bf16[384,4096]{1,0:T(8,128)(2,1)} fusion(bf16[640,4096]{1,0:T(8,128)(2,1)S(1)} %constant_dynamic-update-slice_fusion.5, bf16[640,192]{0,1:T(8,128)(2,1)S(1)} %get-tuple-element.20, bf16[640,192]{0,1:T(8,128)(2,1)S(1)} %get-tuple-element.19), kind=kOutput, calls=%fused_computation.3 | convolution fusion | flops 2015821824 | bytes 8880128 | tf_op jit(solution)/shard_map/dot_general | solution.py:140
  186.9 3.2 %collective-permute-done.14 = bf16[160,1536]{1,0:T(8,128)(2,1)S(1)} collective-permute-done((bf16[160,1536]{1,0:T(8,128)(2,1)S(1)}, bf16[160,1536]{1,0:T(8,128)(2,1)S(1)}, u32[]{:S(2)}, u32[]{:S(2)}) %collective-permute-start.14) | collective-permute-done | bytes 491552 | tf_op jit(solution)/shard_map/ppermute | solution.py:44
  191.5 7.5 %all-to-all-start.3 = ((bf16[16,8,1920]{2,1,0:T(8,128)(2,1)}), bf16[16,8,1920]{2,1,0:T(8,128)(2,1)S(1)}, u32[]{:S(2)}, u32[]{:S(2)}) async-start(bf16[16,8,1920]{2,1,0:T(8,128)(2,1)} %reshape.84), calls=%async_computation.3 | async-start | bytes 983040 | tf_op jit(solution)/shard_map/all_to_all | solution.py:166
  199.0 9.6 %collective-permute-done.9 = bf16[160,2688]{1,0:T(8,128)(2,1)} collective-permute-done((bf16[160,2688]{1,0:T(8,128)(2,1)S(1)}, bf16[160,2688]{1,0:T(8,128)(2,1)}, u32[]{:S(2)}, u32[]{:S(2)}) %collective-permute-start.9) | collective-permute-done | bytes 860192 | tf_op jit(solution)/shard_map/ppermute | solution.py:44
  212.7 3.0 %all-to-all-done.3 = bf16[16,8,1920]{2,1,0:T(8,128)(2,1)S(1)} async-done(((bf16[16,8,1920]{2,1,0:T(8,128)(2,1)}), bf16[16,8,1920]{2,1,0:T(8,128)(2,1)S(1)}, u32[]{:S(2)}, u32[]{:S(2)}) %all-to-all-start.3) | async-done | bytes 491552 | tf_op jit(solution)/shard_map/all_to_all | solution.py:166
  215.7 3.5 %all-to-all-start.2 = ((bf16[16,8,3328]{2,1,0:T(8,128)(2,1)}), bf16[16,8,3328]{2,1,0:T(8,128)(2,1)S(1)}, u32[]{:S(2)}, u32[]{:S(2)}) async-start(bf16[16,8,3328]{2,1,0:T(8,128)(2,1)} %fusion.20), calls=%async_computation.2 | async-start | bytes 1703936 | tf_op jit(solution)/shard_map/all_to_all | solution.py:166
  219.2 5.2 %fusion.1 = bf16[1,1,192,4096]{3,2,1,0:T(8,128)(2,1)} fusion(bf16[640,192]{0,1:T(8,128)(2,1)S(1)} %get-tuple-element.21, bf16[640,4096]{1,0:T(8,128)(2,1)} %copy-done.2), kind=kOutput, calls=%fused_computation.7 | convolution fusion | flops 1007419392 | bytes 7061504 | tf_op jit(solution)/shard_map/dot_general | solution.py:137
  229.4 13.1 %all-to-all-done.2 = bf16[16,8,3328]{2,1,0:T(8,128)(2,1)S(1)} async-done(((bf16[16,8,3328]{2,1,0:T(8,128)(2,1)}), bf16[16,8,3328]{2,1,0:T(8,128)(2,1)S(1)}, u32[]{:S(2)}, u32[]{:S(2)}) %all-to-all-start.2) | async-done | bytes 852000 | tf_op jit(solution)/shard_map/all_to_all | solution.py:166
  244.3 2.4 convolution_convert_fusion.5
  248.9 15.0 %collective-permute-done.12 = bf16[128,2560]{1,0:T(8,128)(2,1)S(1)} collective-permute-done((bf16[128,2560]{1,0:T(8,128)(2,1)}, bf16[128,2560]{1,0:T(8,128)(2,1)S(1)}, u32[]{:S(2)}, u32[]{:S(2)}) %collective-permute-start.12) | collective-permute-done | bytes 655392 | tf_op jit(solution)/shard_map/ppermute | solution.py:10
  (106 shorter events, 58.8 us)
Async XLA Ops:
  0.6 156.3 %copy-start = (bf16[1,1,192,4096]{3,2,1,0:T(8,128)(2,1)S(1)}, bf16[1,1,192,4096]{3,2,1,0:T(8,128)(2,1)}, u32[]{:S(2)}) copy-start(bf16[1,1,192,4096]{3,2,1,0:T(8,128)(2,1)} %param.13) | copy-start | bytes 4718596
  8.6 43.2 %all-to-all-start = ((bf16[16,40,1024]{2,1,0:T(8,128)(2,1)}), bf16[16,40,1024]{2,1,0:T(8,128)(2,1)S(1)}, u32[]{:S(2)}, u32[]{:S(2)}) async-start(bf16[16,40,1024]{2,1,0:T(8,128)(2,1)} %reshape.78), calls=%async_computation | async-start | bytes 2621440 | tf_op jit(solution)/shard_map/all_to_all | solution.py:104
  51.7 37.2 %all-to-all-start.1 = ((bf16[16,40,1024]{2,1,0:T(8,128)(2,1)}), bf16[16,40,1024]{2,1,0:T(8,128)(2,1)}, u32[]{:S(2)}, u32[]{:S(2)}) async-start(bf16[16,40,1024]{2,1,0:T(8,128)(2,1)} %reshape.80), calls=%async_computation.1 | async-start | bytes 2621440 | tf_op jit(solution)/shard_map/all_to_all | solution.py:99
  57.7 38.2 %collective-permute-start.1 = (bf16[160,4096]{1,0:T(8,128)(2,1)}, bf16[160,4096]{1,0:T(8,128)(2,1)}, u32[]{:S(2)}, u32[]{:S(2)}) collective-permute-start(bf16[160,4096]{1,0:T(8,128)(2,1)} %reshape.79), channel_id=1, source_target_pairs={{0,1},{1,2},{2,3},{3,0},{4,5},{5,6},{6,7},{7,4},{8,9},{9,10},{10,1... | collective-permute-start | bytes 3932168 | tf_op jit(solution)/shard_map/ppermute | solution.py:19
  59.0 38.1 %collective-permute-start = (bf16[160,4096]{1,0:T(8,128)(2,1)}, bf16[160,4096]{1,0:T(8,128)(2,1)}, u32[]{:S(2)}, u32[]{:S(2)}) collective-permute-start(bf16[160,4096]{1,0:T(8,128)(2,1)} %reshape.79), channel_id=1, source_target_pairs={{0,3},{1,0},{2,1},{3,2},{4,7},{5,4},{6,5},{7,6},{8,11},{9,8},{10,9... | collective-permute-start | bytes 3932168 | tf_op jit(solution)/shard_map/ppermute | solution.py:20
  91.4 32.1 %collective-permute-start.5 = (bf16[160,4096]{1,0:T(8,128)(2,1)S(1)}, bf16[160,4096]{1,0:T(8,128)(2,1)S(1)}, u32[]{:S(2)}, u32[]{:S(2)}) collective-permute-start(bf16[160,4096]{1,0:T(8,128)(2,1)S(1)} %reshape.81), channel_id=1, source_target_pairs={{0,1},{1,2},{2,3},{3,0},{4,5},{5,6},{6,7},{7,4},{8,9},{9,10},{10,1... | collective-permute-start | bytes 3932168 | tf_op jit(solution)/shard_map/ppermute | solution.py:19
  92.8 30.9 %collective-permute-start.4 = (bf16[160,4096]{1,0:T(8,128)(2,1)S(1)}, bf16[160,4096]{1,0:T(8,128)(2,1)S(1)}, u32[]{:S(2)}, u32[]{:S(2)}) collective-permute-start(bf16[160,4096]{1,0:T(8,128)(2,1)S(1)} %reshape.81), channel_id=1, source_target_pairs={{0,3},{1,0},{2,1},{3,2},{4,7},{5,4},{6,5},{7,6},{8,11},{9,8},{10,9... | collective-permute-start | bytes 3932168 | tf_op jit(solution)/shard_map/ppermute | solution.py:20
  97.0 54.5 %collective-permute-start.2 = (bf16[80,4096]{1,0:T(8,128)(2,1)S(1)}, bf16[80,4096]{1,0:T(8,128)(2,1)S(1)}, u32[]{:S(2)}, u32[]{:S(2)}) collective-permute-start(bf16[80,4096]{1,0:T(8,128)(2,1)S(1)} %slice.155), channel_id=1, source_target_pairs={{0,1},{1,2},{2,3},{3,0},{4,5},{5,6},{6,7},{7,4},{8,9},{9,10},{10,1... | collective-permute-start | bytes 1966088 | tf_op jit(solution)/shard_map/ppermute | solution.py:21
  98.3 57.2 %collective-permute-start.3 = (bf16[80,4096]{1,0:T(8,128)(2,1)S(1)}, bf16[80,4096]{1,0:T(8,128)(2,1)S(1)}, u32[]{:S(2)}, u32[]{:S(2)}) collective-permute-start(bf16[80,4096]{1,0:T(8,128)(2,1)S(1)} %slice.156), channel_id=1, source_target_pairs={{0,3},{1,0},{2,1},{3,2},{4,7},{5,4},{6,5},{7,6},{8,11},{9,8},{10,9... | collective-permute-start | bytes 1966088 | tf_op jit(solution)/shard_map/ppermute | solution.py:22
  123.6 27.3 %collective-permute-start.6 = (bf16[80,4096]{1,0:T(8,128)(2,1)S(1)}, bf16[80,4096]{1,0:T(8,128)(2,1)S(1)}, u32[]{:S(2)}, u32[]{:S(2)}) collective-permute-start(bf16[80,4096]{1,0:T(8,128)(2,1)S(1)} %slice.157), channel_id=1, source_target_pairs={{0,1},{1,2},{2,3},{3,0},{4,5},{5,6},{6,7},{7,4},{8,9},{9,10},{10,1... | collective-permute-start | bytes 1966088 | tf_op jit(solution)/shard_map/ppermute | solution.py:21
  123.7 27.6 %collective-permute-start.7 = (bf16[80,4096]{1,0:T(8,128)(2,1)S(1)}, bf16[80,4096]{1,0:T(8,128)(2,1)S(1)}, u32[]{:S(2)}, u32[]{:S(2)}) collective-permute-start(bf16[80,4096]{1,0:T(8,128)(2,1)S(1)} %slice.158), channel_id=1, source_target_pairs={{0,3},{1,0},{2,1},{3,2},{4,7},{5,4},{6,5},{7,6},{8,11},{9,8},{10,9... | collective-permute-start | bytes 1966088 | tf_op jit(solution)/shard_map/ppermute | solution.py:22
  162.1 8.6 %collective-permute-start.13 = (bf16[80,1536]{1,0:T(8,128)(2,1)S(1)}, bf16[80,1536]{1,0:T(8,128)(2,1)S(1)}, u32[]{:S(2)}, u32[]{:S(2)}) collective-permute-start(bf16[80,1536]{1,0:T(8,128)(2,1)S(1)} %get-tuple-element.15), channel_id=1, source_target_pairs={{0,1},{1,2},{2,3},{3,0},{4,5},{5,6},{6,7},{7,4},{8,9},{9,10},{10,1... | collective-permute-start | bytes 737288 | tf_op jit(solution)/shard_map/ppermute | solution.py:38
  162.6 8.2 %collective-permute-start.15 = (bf16[80,1536]{1,0:T(8,128)(2,1)S(1)}, bf16[80,1536]{1,0:T(8,128)(2,1)S(1)}, u32[]{:S(2)}, u32[]{:S(2)}) collective-permute-start(bf16[80,1536]{1,0:T(8,128)(2,1)S(1)} %get-tuple-element.16), channel_id=1, source_target_pairs={{0,3},{1,0},{2,1},{3,2},{4,7},{5,4},{6,5},{7,6},{8,11},{9,8},{10,9... | collective-permute-start | bytes 737288 | tf_op jit(solution)/shard_map/ppermute | solution.py:39
  167.1 12.1 %collective-permute-start.10 = (bf16[80,2688]{1,0:T(8,128)(2,1)S(1)}, bf16[80,2688]{1,0:T(8,128)(2,1)S(1)}, u32[]{:S(2)}, u32[]{:S(2)}) collective-permute-start(bf16[80,2688]{1,0:T(8,128)(2,1)S(1)} %get-tuple-element.8), channel_id=1, source_target_pairs={{0,3},{1,0},{2,1},{3,2},{4,7},{5,4},{6,5},{7,6},{8,11},{9,8},{10,9... | collective-permute-start | bytes 1290248 | tf_op jit(solution)/shard_map/ppermute | solution.py:39
  167.8 11.8 %collective-permute-start.8 = (bf16[80,2688]{1,0:T(8,128)(2,1)S(1)}, bf16[80,2688]{1,0:T(8,128)(2,1)S(1)}, u32[]{:S(2)}, u32[]{:S(2)}) collective-permute-start(bf16[80,2688]{1,0:T(8,128)(2,1)S(1)} %get-tuple-element.7), channel_id=1, source_target_pairs={{0,1},{1,2},{2,3},{3,0},{4,5},{5,6},{6,7},{7,4},{8,9},{9,10},{10,1... | collective-permute-start | bytes 1290248 | tf_op jit(solution)/shard_map/ppermute | solution.py:38
  170.9 19.2 %collective-permute-start.14 = (bf16[160,1536]{1,0:T(8,128)(2,1)S(1)}, bf16[160,1536]{1,0:T(8,128)(2,1)S(1)}, u32[]{:S(2)}, u32[]{:S(2)}) collective-permute-start(bf16[160,1536]{1,0:T(8,128)(2,1)S(1)} %pad_maximum_fusion.5), channel_id=1, source_target_pairs={{0,1},{1,2},{2,3},{3,0},{4,5},{5,6},{6,7},{7,4},{8,9},{9,10},{10,1... | collective-permute-start | bytes 1474568 | tf_op jit(solution)/shard_map/ppermute | solution.py:44
  171.4 18.7 %collective-permute-start.16 = (bf16[160,1536]{1,0:T(8,128)(2,1)S(1)}, bf16[160,1536]{1,0:T(8,128)(2,1)S(1)}, u32[]{:S(2)}, u32[]{:S(2)}) collective-permute-start(bf16[160,1536]{1,0:T(8,128)(2,1)S(1)} %pad_maximum_fusion.6), channel_id=1, source_target_pairs={{0,3},{1,0},{2,1},{3,2},{4,7},{5,4},{6,5},{7,6},{8,11},{9,8},{10,9... | collective-permute-start | bytes 1474568 | tf_op jit(solution)/shard_map/ppermute | solution.py:45
  179.9 28.7 %collective-permute-start.9 = (bf16[160,2688]{1,0:T(8,128)(2,1)S(1)}, bf16[160,2688]{1,0:T(8,128)(2,1)}, u32[]{:S(2)}, u32[]{:S(2)}) collective-permute-start(bf16[160,2688]{1,0:T(8,128)(2,1)S(1)} %pad_maximum_fusion.2), channel_id=1, source_target_pairs={{0,1},{1,2},{2,3},{3,0},{4,5},{5,6},{6,7},{7,4},{8,9},{9,10},{10,1... | collective-permute-start | bytes 2580488 | tf_op jit(solution)/shard_map/ppermute | solution.py:44
  180.8 27.8 %collective-permute-start.11 = (bf16[160,2688]{1,0:T(8,128)(2,1)S(1)}, bf16[160,2688]{1,0:T(8,128)(2,1)}, u32[]{:S(2)}, u32[]{:S(2)}) collective-permute-start(bf16[160,2688]{1,0:T(8,128)(2,1)S(1)} %pad_maximum_fusion.3), channel_id=1, source_target_pairs={{0,3},{1,0},{2,1},{3,2},{4,7},{5,4},{6,5},{7,6},{8,11},{9,8},{10,9... | collective-permute-start | bytes 2580488 | tf_op jit(solution)/shard_map/ppermute | solution.py:45
  191.5 24.1 %all-to-all-start.3 = ((bf16[16,8,1920]{2,1,0:T(8,128)(2,1)}), bf16[16,8,1920]{2,1,0:T(8,128)(2,1)S(1)}, u32[]{:S(2)}, u32[]{:S(2)}) async-start(bf16[16,8,1920]{2,1,0:T(8,128)(2,1)} %reshape.84), calls=%async_computation.3 | async-start | bytes 983040 | tf_op jit(solution)/shard_map/all_to_all | solution.py:166
  215.7 26.9 %all-to-all-start.2 = ((bf16[16,8,3328]{2,1,0:T(8,128)(2,1)}), bf16[16,8,3328]{2,1,0:T(8,128)(2,1)S(1)}, u32[]{:S(2)}, u32[]{:S(2)}) async-start(bf16[16,8,3328]{2,1,0:T(8,128)(2,1)} %fusion.20), calls=%async_computation.2 | async-start | bytes 1703936 | tf_op jit(solution)/shard_map/all_to_all | solution.py:166
  228.0 20.9 %collective-permute-start.17 = (bf16[128,1536]{1,0:T(8,128)(2,1)}, bf16[128,1536]{1,0:T(8,128)(2,1)}, u32[]{:S(2)}, u32[]{:S(2)}) collective-permute-start(bf16[128,1536]{1,0:T(8,128)(2,1)} %convolution_convert_fusion.7), channel_id=1, source_target_pairs={{64,0},{128,64},{192,128},{65,1},{129,65},{193,129},{66,2},{130,66... | collective-permute-start | bytes 1179656 | tf_op jit(solution)/shard_map/ppermute | solution.py:10
  242.6 23.5 %copy-start.1 = (bf16[1,1,192,4096]{3,2,1,0:T(8,128)(2,1)S(1)}, bf16[1,1,192,4096]{3,2,1,0:T(8,128)(2,1)}, u32[]{:S(2)}) copy-start(bf16[1,1,192,4096]{3,2,1,0:T(8,128)(2,1)} %param.13) | copy-start | bytes 4718596
  246.7 17.3 %collective-permute-start.12 = (bf16[128,2560]{1,0:T(8,128)(2,1)}, bf16[128,2560]{1,0:T(8,128)(2,1)S(1)}, u32[]{:S(2)}, u32[]{:S(2)}) collective-permute-start(bf16[128,2560]{1,0:T(8,128)(2,1)} %convolution_convert_fusion.5), channel_id=1, source_target_pairs={{64,0},{128,64},{192,128},{65,1},{129,65},{193,129},{66,2},{130,66... | collective-permute-start | bytes 1966088 | tf_op jit(solution)/shard_map/ppermute | solution.py:10
  (8 other events, 70.0 us)

commit v14 on v13

--- a/solution.py
+++ b/solution.py
@@ -146,7 +146,7 @@
     grad_gate = jnp.concatenate(grad_gate, axis=1)
     grad_up = jnp.concatenate(grad_up, axis=1)
     unit = model_width // 8
-    back_widths = [5 * unit, 3 * unit]
+    back_widths = [6 * unit, 2 * unit]
     handed = []
     offset = 0
     for q, back_width in enumerate(back_widths):

time: 267 us -> 298 us (1.12)
  waiting for transfers between devices: 153 us -> 180 us
  local copies, waits for them, and re-layouts: 25.1 us -> 28.3 us
    ppermute x2, waiting for transfers between devices: 12.8 us -> 23.9 us  [ring_reduce_scatter(): from_left = lax.ppermute(to_right.astype(jnp.bfloat16), axis, fwd)]
    ppermute x2, waiting for transfers between devices: 15 us -> 22.4 us  [from_behind(): return lax.ppermute(shard, axis, pairs)]
    all_to_all x2, waiting for transfers between devices: 16.1 us -> 22.2 us  [per_device(): back = lax.all_to_all(body, 'expert', 0, 0, tiled=True)]
    unnamed x28 -> x40, local copies, waits for them, and re-layouts: 5.02 us -> 6.2 us
  transfers between devices with their start and end apart: 22 -> 22, of which waited for: 13 -> 12; matrix products, arithmetic and copies ran while one was open for 17% -> 14% of each run, Pallas kernels for 0% -> 0%
where the time goes in v14:
time: 298 us; the launch traced here: 297 us
  waiting for transfers between devices  180 us (60%)
  starting transfers between devices  48 us (16%)
  local copies, waits for them, and re-layouts  28.3 us (9%)
  matrix products  27.3 us (9%)
  other arithmetic  12.1 us (4%)
    all_to_all x1, waiting for transfers between devices, per_device(): lax.all_to_all(dense_chunks(local_x[:, cols], experts), 'expert', 0, 0, t...  28.5 us
    all_to_all x1, waiting for transfers between devices, per_device(): lax.all_to_all(dense_chunks(local_dy[:, cols], experts), 'expert', 0, 0,...  27 us
    ppermute x2, waiting for transfers between devices, ring_reduce_scatter(): from_left = lax.ppermute(to_right.astype(jnp.bfloat16), axis, fwd)  23.9 us
    ppermute x2, waiting for transfers between devices, ring_gather(): far_top = lax.ppermute(from_left[:half], axis, fwd)  22.6 us
    ppermute x2, waiting for transfers between devices, ring_gather(): from_left = lax.ppermute(piece, axis, fwd)  22.5 us
    ppermute x2, waiting for transfers between devices, from_behind(): return lax.ppermute(shard, axis, pairs)  22.4 us
    all_to_all x2, waiting for transfers between devices, per_device(): back = lax.all_to_all(body, 'expert', 0, 0, tiled=True)  22.2 us
    all_to_all x1, starting transfers between devices, per_device(): lax.all_to_all(dense_chunks(local_dy[:, cols], experts), 'expert', 0, 0,...  9.97 us
  transfers between devices with their start and end apart: 22, of which 12 were waited for; matrix products, arithmetic and copies ran while one was open for 14% of the time, Pallas kernels for 0%

profile of v14, /device:TPU:1, one launch (start us, length us, event | category | flops | bytes accessed | tf_op | source)
XLA Modules:
  0.0 296.9 jit_solution(233196992722722133)
XLA Ops:
  8.6 10.0 %all-to-all-start = ((bf16[16,40,1024]{2,1,0:T(8,128)(2,1)}), bf16[16,40,1024]{2,1,0:T(8,128)(2,1)S(1)}, u32[]{:S(2)}, u32[]{:S(2)}) async-start(bf16[16,40,1024]{2,1,0:T(8,128)(2,1)} %reshape.78), calls=%async_computation | async-start | bytes 2621440 | tf_op jit(solution)/shard_map/all_to_all | solution.py:104
  18.5 2.8 convolution_convert_fusion.2
  21.3 3.4 %reshape.80 = bf16[16,40,1024]{2,1,0:T(8,128)(2,1)} reshape(bf16[160,4096]{1,0:T(8,128)(2,1)} %convolution_convert_fusion.2) | data formatting | bytes 2621440 | tf_op jit(solution)/shard_map/reshape | solution.py:65
  24.7 27.0 %all-to-all-done = bf16[16,40,1024]{2,1,0:T(8,128)(2,1)S(1)} async-done(((bf16[16,40,1024]{2,1,0:T(8,128)(2,1)}), bf16[16,40,1024]{2,1,0:T(8,128)(2,1)S(1)}, u32[]{:S(2)}, u32[]{:S(2)}) %all-to-all-start) | async-done | bytes 1310752 | tf_op jit(solution)/shard_map/all_to_all | solution.py:104
  51.7 4.3 %all-to-all-start.1 = ((bf16[16,40,1024]{2,1,0:T(8,128)(2,1)}), bf16[16,40,1024]{2,1,0:T(8,128)(2,1)}, u32[]{:S(2)}, u32[]{:S(2)}) async-start(bf16[16,40,1024]{2,1,0:T(8,128)(2,1)} %reshape.80), calls=%async_computation.1 | async-start | bytes 2621440 | tf_op jit(solution)/shard_map/all_to_all | solution.py:99
  60.4 28.5 %all-to-all-done.1 = bf16[16,40,1024]{2,1,0:T(8,128)(2,1)} async-done(((bf16[16,40,1024]{2,1,0:T(8,128)(2,1)}), bf16[16,40,1024]{2,1,0:T(8,128)(2,1)}, u32[]{:S(2)}, u32[]{:S(2)}) %all-to-all-start.1) | async-done | bytes 1310752 | tf_op jit(solution)/shard_map/all_to_all | solution.py:99
  98.3 2.7 collective-permute-start.3
  101.0 22.5 %collective-permute-done.5 = bf16[160,4096]{1,0:T(8,128)(2,1)S(1)} collective-permute-done((bf16[160,4096]{1,0:T(8,128)(2,1)S(1)}, bf16[160,4096]{1,0:T(8,128)(2,1)S(1)}, u32[]{:S(2)}, u32[]{:S(2)}) %collective-permute-start.5) | collective-permute-done | bytes 1310752 | tf_op jit(solution)/shard_map/ppermute | solution.py:19
  123.7 2.9 collective-permute-start.7
  128.2 22.6 %collective-permute-done.6 = bf16[80,4096]{1,0:T(8,128)(2,1)S(1)} collective-permute-done((bf16[80,4096]{1,0:T(8,128)(2,1)S(1)}, bf16[80,4096]{1,0:T(8,128)(2,1)S(1)}, u32[]{:S(2)}, u32[]{:S(2)}) %collective-permute-start.6) | collective-permute-done | bytes 655392 | tf_op jit(solution)/shard_map/ppermute | solution.py:21
  153.6 2.6 fusion.3
  167.2 2.7 collective-permute-start.15
  169.9 8.3 %collective-permute-done.10 = bf16[80,3200]{1,0:T(8,128)(2,1)S(1)} collective-permute-done((bf16[80,3200]{1,0:T(8,128)(2,1)S(1)}, bf16[80,3200]{1,0:T(8,128)(2,1)S(1)}, u32[]{:S(2)}, u32[]{:S(2)}) %collective-permute-start.10) | collective-permute-done | bytes 512032 | tf_op jit(solution)/shard_map/ppermute | solution.py:39
  181.4 2.7 collective-permute-start.11
  184.4 2.7 collective-permute-start.16
  187.1 23.9 %collective-permute-done.14 = bf16[160,1024]{1,0:T(8,128)(2,1)S(1)} collective-permute-done((bf16[160,1024]{1,0:T(8,128)(2,1)S(1)}, bf16[160,1024]{1,0:T(8,128)(2,1)S(1)}, u32[]{:S(2)}, u32[]{:S(2)}) %collective-permute-start.14) | collective-permute-done | bytes 327712 | tf_op jit(solution)/shard_map/ppermute | solution.py:44
  212.4 6.3 %all-to-all-start.3 = ((bf16[16,8,1280]{2,1,0:T(8,128)(2,1)}), bf16[16,8,1280]{2,1,0:T(8,128)(2,1)S(1)}, u32[]{:S(2)}, u32[]{:S(2)}) async-start(bf16[16,8,1280]{2,1,0:T(8,128)(2,1)} %reshape.84), calls=%async_computation.3 | async-start | bytes 655360 | tf_op jit(solution)/shard_map/all_to_all | solution.py:166
  223.3 8.4 %all-to-all-done.3 = bf16[16,8,1280]{2,1,0:T(8,128)(2,1)S(1)} async-done(((bf16[16,8,1280]{2,1,0:T(8,128)(2,1)}), bf16[16,8,1280]{2,1,0:T(8,128)(2,1)S(1)}, u32[]{:S(2)}, u32[]{:S(2)}) %all-to-all-start.3) | async-done | bytes 327712 | tf_op jit(solution)/shard_map/all_to_all | solution.py:166
  231.8 3.5 %all-to-all-start.2 = ((bf16[16,8,3968]{2,1,0:T(8,128)(2,1)}), bf16[16,8,3968]{2,1,0:T(8,128)(2,1)S(1)}, u32[]{:S(2)}, u32[]{:S(2)}) async-start(bf16[16,8,3968]{2,1,0:T(8,128)(2,1)} %fusion.18), calls=%async_computation.2 | async-start | bytes 2031616 | tf_op jit(solution)/shard_map/all_to_all | solution.py:166
  235.3 5.1 %fusion.1 = bf16[1,1,192,4096]{3,2,1,0:T(8,128)(2,1)} fusion(bf16[640,192]{0,1:T(8,128)(2,1)S(1)} %copy-done.7, bf16[640,4096]{1,0:T(8,128)(2,1)} %copy-done.2), kind=kOutput, calls=%fused_computation.7 | convolution fusion | flops 1007419392 | bytes 7061504 | tf_op jit(solution)/shard_map/dot_general | solution.py:137
  240.4 5.6 %convolution_convert_fusion = bf16[384,4096]{1,0:T(8,128)(2,1)S(1)} fusion(bf16[640,4096]{1,0:T(8,128)(2,1)} %copy-done.8, bf16[640,192]{0,1:T(8,128)(2,1)S(1)} %copy-done.12, bf16[640,192]{0,1:T(8,128)(2,1)S(1)} %copy-done.10), kind=kOutput, calls=%fused_computation.3 | convolution fusion | flops 2015821824 | bytes 8880128 | tf_op jit(solution)/shard_map/dot_general | solution.py:140
  248.2 13.8 %all-to-all-done.2 = bf16[16,8,3968]{2,1,0:T(8,128)(2,1)S(1)} async-done(((bf16[16,8,3968]{2,1,0:T(8,128)(2,1)}), bf16[16,8,3968]{2,1,0:T(8,128)(2,1)S(1)}, u32[]{:S(2)}, u32[]{:S(2)}) %all-to-all-start.2) | async-done | bytes 1015840 | tf_op jit(solution)/shard_map/all_to_all | solution.py:166
  263.0 3.0 %reshape.83 = bf16[160,3072]{1,0:T(8,128)(2,1)} reshape(bf16[16,8,3840]{2,1,0:T(8,128)(2,1)} %slice.173) | data formatting | bytes 1966080 | tf_op jit(solution)/shard_map/reshape | solution.py:169
  272.3 22.4 %collective-permute-done.17 = bf16[128,1024]{1,0:T(8,128)(2,1)S(1)} collective-permute-done((bf16[128,1024]{1,0:T(8,128)(2,1)S(1)}, bf16[128,1024]{1,0:T(8,128)(2,1)S(1)}, u32[]{:S(2)}, u32[]{:S(2)}) %collective-permute-start.17) | collective-permute-done | bytes 262176 | tf_op jit(solution)/shard_map/ppermute | solution.py:10
  (118 shorter events, 57.9 us)
Async XLA Ops:
  0.6 157.1 %copy-start = (bf16[1,1,192,4096]{3,2,1,0:T(8,128)(2,1)S(1)}, bf16[1,1,192,4096]{3,2,1,0:T(8,128)(2,1)}, u32[]{:S(2)}) copy-start(bf16[1,1,192,4096]{3,2,1,0:T(8,128)(2,1)} %param.13) | copy-start | bytes 4718596
  8.6 43.2 %all-to-all-start = ((bf16[16,40,1024]{2,1,0:T(8,128)(2,1)}), bf16[16,40,1024]{2,1,0:T(8,128)(2,1)S(1)}, u32[]{:S(2)}, u32[]{:S(2)}) async-start(bf16[16,40,1024]{2,1,0:T(8,128)(2,1)} %reshape.78), calls=%async_computation | async-start | bytes 2621440 | tf_op jit(solution)/shard_map/all_to_all | solution.py:104
  51.7 37.2 %all-to-all-start.1 = ((bf16[16,40,1024]{2,1,0:T(8,128)(2,1)}), bf16[16,40,1024]{2,1,0:T(8,128)(2,1)}, u32[]{:S(2)}, u32[]{:S(2)}) async-start(bf16[16,40,1024]{2,1,0:T(8,128)(2,1)} %reshape.80), calls=%async_computation.1 | async-start | bytes 2621440 | tf_op jit(solution)/shard_map/all_to_all | solution.py:99
  57.7 38.2 %collective-permute-start.1 = (bf16[160,4096]{1,0:T(8,128)(2,1)}, bf16[160,4096]{1,0:T(8,128)(2,1)}, u32[]{:S(2)}, u32[]{:S(2)}) collective-permute-start(bf16[160,4096]{1,0:T(8,128)(2,1)} %reshape.79), channel_id=1, source_target_pairs={{0,1},{1,2},{2,3},{3,0},{4,5},{5,6},{6,7},{7,4},{8,9},{9,10},{10,1... | collective-permute-start | bytes 3932168 | tf_op jit(solution)/shard_map/ppermute | solution.py:19
  59.0 38.1 %collective-permute-start = (bf16[160,4096]{1,0:T(8,128)(2,1)}, bf16[160,4096]{1,0:T(8,128)(2,1)}, u32[]{:S(2)}, u32[]{:S(2)}) collective-permute-start(bf16[160,4096]{1,0:T(8,128)(2,1)} %reshape.79), channel_id=1, source_target_pairs={{0,3},{1,0},{2,1},{3,2},{4,7},{5,4},{6,5},{7,6},{8,11},{9,8},{10,9... | collective-permute-start | bytes 3932168 | tf_op jit(solution)/shard_map/ppermute | solution.py:20
  91.4 32.1 %collective-permute-start.5 = (bf16[160,4096]{1,0:T(8,128)(2,1)S(1)}, bf16[160,4096]{1,0:T(8,128)(2,1)S(1)}, u32[]{:S(2)}, u32[]{:S(2)}) collective-permute-start(bf16[160,4096]{1,0:T(8,128)(2,1)S(1)} %reshape.81), channel_id=1, source_target_pairs={{0,1},{1,2},{2,3},{3,0},{4,5},{5,6},{6,7},{7,4},{8,9},{9,10},{10,1... | collective-permute-start | bytes 3932168 | tf_op jit(solution)/shard_map/ppermute | solution.py:19
  92.8 30.9 %collective-permute-start.4 = (bf16[160,4096]{1,0:T(8,128)(2,1)S(1)}, bf16[160,4096]{1,0:T(8,128)(2,1)S(1)}, u32[]{:S(2)}, u32[]{:S(2)}) collective-permute-start(bf16[160,4096]{1,0:T(8,128)(2,1)S(1)} %reshape.81), channel_id=1, source_target_pairs={{0,3},{1,0},{2,1},{3,2},{4,7},{5,4},{6,5},{7,6},{8,11},{9,8},{10,9... | collective-permute-start | bytes 3932168 | tf_op jit(solution)/shard_map/ppermute | solution.py:20
  97.0 54.5 %collective-permute-start.2 = (bf16[80,4096]{1,0:T(8,128)(2,1)S(1)}, bf16[80,4096]{1,0:T(8,128)(2,1)S(1)}, u32[]{:S(2)}, u32[]{:S(2)}) collective-permute-start(bf16[80,4096]{1,0:T(8,128)(2,1)S(1)} %slice.155), channel_id=1, source_target_pairs={{0,1},{1,2},{2,3},{3,0},{4,5},{5,6},{6,7},{7,4},{8,9},{9,10},{10,1... | collective-permute-start | bytes 1966088 | tf_op jit(solution)/shard_map/ppermute | solution.py:21
  98.3 58.0 %collective-permute-start.3 = (bf16[80,4096]{1,0:T(8,128)(2,1)S(1)}, bf16[80,4096]{1,0:T(8,128)(2,1)S(1)}, u32[]{:S(2)}, u32[]{:S(2)}) collective-permute-start(bf16[80,4096]{1,0:T(8,128)(2,1)S(1)} %slice.156), channel_id=1, source_target_pairs={{0,3},{1,0},{2,1},{3,2},{4,7},{5,4},{6,5},{7,6},{8,11},{9,8},{10,9... | collective-permute-start | bytes 1966088 | tf_op jit(solution)/shard_map/ppermute | solution.py:22
  123.6 27.3 %collective-permute-start.6 = (bf16[80,4096]{1,0:T(8,128)(2,1)S(1)}, bf16[80,4096]{1,0:T(8,128)(2,1)S(1)}, u32[]{:S(2)}, u32[]{:S(2)}) collective-permute-start(bf16[80,4096]{1,0:T(8,128)(2,1)S(1)} %slice.157), channel_id=1, source_target_pairs={{0,1},{1,2},{2,3},{3,0},{4,5},{5,6},{6,7},{7,4},{8,9},{9,10},{10,1... | collective-permute-start | bytes 1966088 | tf_op jit(solution)/shard_map/ppermute | solution.py:21
  123.7 27.6 %collective-permute-start.7 = (bf16[80,4096]{1,0:T(8,128)(2,1)S(1)}, bf16[80,4096]{1,0:T(8,128)(2,1)S(1)}, u32[]{:S(2)}, u32[]{:S(2)}) collective-permute-start(bf16[80,4096]{1,0:T(8,128)(2,1)S(1)} %slice.158), channel_id=1, source_target_pairs={{0,3},{1,0},{2,1},{3,2},{4,7},{5,4},{6,5},{7,6},{8,11},{9,8},{10,9... | collective-permute-start | bytes 1966088 | tf_op jit(solution)/shard_map/ppermute | solution.py:22
  164.7 13.5 %collective-permute-start.10 = (bf16[80,3200]{1,0:T(8,128)(2,1)S(1)}, bf16[80,3200]{1,0:T(8,128)(2,1)S(1)}, u32[]{:S(2)}, u32[]{:S(2)}) collective-permute-start(bf16[80,3200]{1,0:T(8,128)(2,1)S(1)} %get-tuple-element.8), channel_id=1, source_target_pairs={{0,3},{1,0},{2,1},{3,2},{4,7},{5,4},{6,5},{7,6},{8,11},{9,8},{10,9... | collective-permute-start | bytes 1536008 | tf_op jit(solution)/shard_map/ppermute | solution.py:39
  165.8 14.2 %collective-permute-start.8 = (bf16[80,3200]{1,0:T(8,128)(2,1)S(1)}, bf16[80,3200]{1,0:T(8,128)(2,1)S(1)}, u32[]{:S(2)}, u32[]{:S(2)}) collective-permute-start(bf16[80,3200]{1,0:T(8,128)(2,1)S(1)} %get-tuple-element.7), channel_id=1, source_target_pairs={{0,1},{1,2},{2,3},{3,0},{4,5},{5,6},{6,7},{7,4},{8,9},{9,10},{10,1... | collective-permute-start | bytes 1536008 | tf_op jit(solution)/shard_map/ppermute | solution.py:38
  167.1 17.0 %collective-permute-start.13 = (bf16[80,1024]{1,0:T(8,128)(2,1)S(1)}, bf16[80,1024]{1,0:T(8,128)(2,1)S(1)}, u32[]{:S(2)}, u32[]{:S(2)}) collective-permute-start(bf16[80,1024]{1,0:T(8,128)(2,1)S(1)} %get-tuple-element.17), channel_id=1, source_target_pairs={{0,1},{1,2},{2,3},{3,0},{4,5},{5,6},{6,7},{7,4},{8,9},{9,10},{10,1... | collective-permute-start | bytes 491528 | tf_op jit(solution)/shard_map/ppermute | solution.py:38
  167.2 16.9 %collective-permute-start.15 = (bf16[80,1024]{1,0:T(8,128)(2,1)S(1)}, bf16[80,1024]{1,0:T(8,128)(2,1)S(1)}, u32[]{:S(2)}, u32[]{:S(2)}) collective-permute-start(bf16[80,1024]{1,0:T(8,128)(2,1)S(1)} %get-tuple-element.18), channel_id=1, source_target_pairs={{0,3},{1,0},{2,1},{3,2},{4,7},{5,4},{6,5},{7,6},{8,11},{9,8},{10,9... | collective-permute-start | bytes 491528 | tf_op jit(solution)/shard_map/ppermute | solution.py:39
  180.3 38.4 %collective-permute-start.9 = (bf16[160,3200]{1,0:T(8,128)(2,1)S(1)}, bf16[160,3200]{1,0:T(8,128)(2,1)}, u32[]{:S(2)}, u32[]{:S(2)}) collective-permute-start(bf16[160,3200]{1,0:T(8,128)(2,1)S(1)} %pad_maximum_fusion.2), channel_id=1, source_target_pairs={{0,1},{1,2},{2,3},{3,0},{4,5},{5,6},{6,7},{7,4},{8,9},{9,10},{10,1... | collective-permute-start | bytes 3072008 | tf_op jit(solution)/shard_map/ppermute | solution.py:44
  181.4 37.3 %collective-permute-start.11 = (bf16[160,3200]{1,0:T(8,128)(2,1)}, bf16[160,3200]{1,0:T(8,128)(2,1)}, u32[]{:S(2)}, u32[]{:S(2)}) collective-permute-start(bf16[160,3200]{1,0:T(8,128)(2,1)} %pad_maximum_fusion.3), channel_id=1, source_target_pairs={{0,3},{1,0},{2,1},{3,2},{4,7},{5,4},{6,5},{7,6},{8,11},{9,8},{10,9... | collective-permute-start | bytes 3072008 | tf_op jit(solution)/shard_map/ppermute | solution.py:45
  184.2 26.7 %collective-permute-start.14 = (bf16[160,1024]{1,0:T(8,128)(2,1)S(1)}, bf16[160,1024]{1,0:T(8,128)(2,1)S(1)}, u32[]{:S(2)}, u32[]{:S(2)}) collective-permute-start(bf16[160,1024]{1,0:T(8,128)(2,1)S(1)} %pad_maximum_fusion.5), channel_id=1, source_target_pairs={{0,1},{1,2},{2,3},{3,0},{4,5},{5,6},{6,7},{7,4},{8,9},{9,10},{10,1... | collective-permute-start | bytes 983048 | tf_op jit(solution)/shard_map/ppermute | solution.py:44
  184.4 26.8 %collective-permute-start.16 = (bf16[160,1024]{1,0:T(8,128)(2,1)S(1)}, bf16[160,1024]{1,0:T(8,128)(2,1)S(1)}, u32[]{:S(2)}, u32[]{:S(2)}) collective-permute-start(bf16[160,1024]{1,0:T(8,128)(2,1)S(1)} %pad_maximum_fusion.6), channel_id=1, source_target_pairs={{0,3},{1,0},{2,1},{3,2},{4,7},{5,4},{6,5},{7,6},{8,11},{9,8},{10,9... | collective-permute-start | bytes 983048 | tf_op jit(solution)/shard_map/ppermute | solution.py:45
  212.4 19.4 %all-to-all-start.3 = ((bf16[16,8,1280]{2,1,0:T(8,128)(2,1)}), bf16[16,8,1280]{2,1,0:T(8,128)(2,1)S(1)}, u32[]{:S(2)}, u32[]{:S(2)}) async-start(bf16[16,8,1280]{2,1,0:T(8,128)(2,1)} %reshape.84), calls=%async_computation.3 | async-start | bytes 655360 | tf_op jit(solution)/shard_map/all_to_all | solution.py:166
  231.8 30.3 %all-to-all-start.2 = ((bf16[16,8,3968]{2,1,0:T(8,128)(2,1)}), bf16[16,8,3968]{2,1,0:T(8,128)(2,1)S(1)}, u32[]{:S(2)}, u32[]{:S(2)}) async-start(bf16[16,8,3968]{2,1,0:T(8,128)(2,1)} %fusion.18), calls=%async_computation.2 | async-start | bytes 2031616 | tf_op jit(solution)/shard_map/all_to_all | solution.py:166
  263.0 33.9 %copy-start.1 = (bf16[1,1,192,4096]{3,2,1,0:T(8,128)(2,1)S(1)}, bf16[1,1,192,4096]{3,2,1,0:T(8,128)(2,1)}, u32[]{:S(2)}) copy-start(bf16[1,1,192,4096]{3,2,1,0:T(8,128)(2,1)} %param.13) | copy-start | bytes 4718596
  268.6 26.2 %collective-permute-start.12 = (bf16[128,3072]{1,0:T(8,128)(2,1)}, bf16[128,3072]{1,0:T(8,128)(2,1)}, u32[]{:S(2)}, u32[]{:S(2)}) collective-permute-start(bf16[128,3072]{1,0:T(8,128)(2,1)} %convolution_convert_fusion.5), channel_id=1, source_target_pairs={{64,0},{128,64},{192,128},{65,1},{129,65},{193,129},{66,2},{130,66... | collective-permute-start | bytes 2359304 | tf_op jit(solution)/shard_map/ppermute | solution.py:10
  270.1 24.6 %collective-permute-start.17 = (bf16[128,1024]{1,0:T(8,128)(2,1)S(1)}, bf16[128,1024]{1,0:T(8,128)(2,1)S(1)}, u32[]{:S(2)}, u32[]{:S(2)}) collective-permute-start(bf16[128,1024]{1,0:T(8,128)(2,1)S(1)} %convolution_convert_fusion.7), channel_id=1, source_target_pairs={{64,0},{128,64},{192,128},{65,1},{129,65},{193,129},{66,2},{130,66... | collective-permute-start | bytes 786440 | tf_op jit(solution)/shard_map/ppermute | solution.py:10
  (14 other events, 82.8 us)
